TPU v7x, 128 devices: a whole 4x4x4 slice. The times are simulated.
128 devices in a mesh: rep: 64 (over z, y, x_hi, core), shard: 2 (over x_lo).
Axes of the slice: x: 4 (x_hi: 2, x_lo: 2; x = x_hi * 2 + x_lo), y: 4, z: 4, core: 2. Of those that a mesh axis runs over, the one named last changes fastest.
Arguments:
- grad_xproj: bfloat16 [256, 2, 3072, 128], P(('rep', 'shard')), may hold values from -32 to 32
- grad_chan: bfloat16 [256, 2, 118, 3072], P(('rep', 'shard')), may hold values from -32 to 32
- grad_embed: bfloat16 [256, 1024, 1536], P(('rep', 'shard')), may hold values from -32 to 32
- weight_xproj: float32 [2, 3072, 128], P(None, 'shard'), may hold values from -0.3125 to 0.3125
- weight_chan: float32 [2, 118, 3072], P(None, None, 'shard'), may hold values from -0.3125 to 0.3125
- weight_embed: float32 [1024, 1536], P('shard'), may hold values from -0.3125 to 0.3125
- moment_xproj: float32 [2, 3072, 128], P(None, 'shard'), may hold values from -0.015625 to 0.015625
- moment_chan: float32 [2, 118, 3072], P(None, None, 'shard'), may hold values from -0.015625 to 0.015625
- moment_embed: float32 [1024, 1536], P('shard'), may hold values from -0.015625 to 0.015625
- second_xproj: float32 [2, 3072, 128], P(None, 'shard'), may hold values from 1e-08 to 1e-05
- second_chan: float32 [2, 118, 3072], P(None, None, 'shard'), may hold values from 1e-08 to 1e-05
- second_embed: float32 [1024, 1536], P('shard'), may hold values from 1e-08 to 1e-05
Outputs:
- new_weight_xproj: float32 [2, 3072, 128], P(None, 'shard')
- new_weight_chan: float32 [2, 118, 3072], P(None, None, 'shard')
- new_weight_embed: float32 [1024, 1536], P('shard')
- new_moment_xproj: float32 [2, 3072, 128], P(None, 'shard')
- new_moment_chan: float32 [2, 118, 3072], P(None, None, 'shard')
- new_moment_embed: float32 [1024, 1536], P('shard')
- new_second_xproj: float32 [2, 3072, 128], P(None, 'shard')
- new_second_chan: float32 [2, 118, 3072], P(None, None, 'shard')
- new_second_embed: float32 [1024, 1536], P('shard')
- full_xproj: bfloat16 [2, 3072, 128], replicated
- full_chan: bfloat16 [2, 118, 3072], replicated
- full_embed: bfloat16 [1024, 1536], replicated
- pre_norm: float32 [1], replicated
All inputs are finite; a program needn't handle non-finite values.
Results may differ from a plain program's by a relative error of at most 0.00085.
Values may be sent and summed in bfloat16 or wider, within the bound.
No kernel may reach another device: no remote copies, remote signals or barrier semaphores. Data moves between devices by JAX's collectives and lax.ppermute only.
A program may use at most 448 MiB of HBM per device.

v0:
```python
import jax
import jax.numpy as jnp
from jax import lax
from jax.sharding import PartitionSpec as P

beta_one = 0.9
beta_two = 0.999
learn_rate = 0.003
decay_rate = 0.1
epsilon = 1e-08
correct_one = 0.9999734386011124
correct_two = 0.09520785288629094


def adamw_update(weight, moment, second, gradient, clip_factor):
    clipped = clip_factor * gradient
    new_moment = beta_one * moment + (1.0 - beta_one) * clipped
    new_second = beta_two * second + (1.0 - beta_two) * clipped * clipped
    step_size = new_moment / correct_one / (jnp.sqrt(new_second / correct_two) + epsilon)
    new_weight = weight - learn_rate * (step_size + decay_rate * weight)
    return (new_weight, new_moment, new_second)


def on_device(
    grad_xproj,
    grad_chan,
    grad_embed,
    weight_xproj,
    weight_chan,
    weight_embed,
    moment_xproj,
    moment_chan,
    moment_embed,
    second_xproj,
    second_chan,
    second_embed,
):
    count_rep = lax.axis_size("rep")
    count_shard = lax.axis_size("shard")
    summed_x = jnp.sum(grad_xproj, axis=0, dtype=jnp.float32)
    summed_c = jnp.sum(grad_chan, axis=0, dtype=jnp.float32)
    summed_e = jnp.sum(grad_embed, axis=0, dtype=jnp.float32)
    group = (
        lax.psum_scatter(
            summed_x.astype(jnp.bfloat16), "shard", scatter_dimension=1, tiled=True
        ).astype(jnp.float32),
        lax.psum_scatter(
            summed_c.astype(jnp.bfloat16), "shard", scatter_dimension=2, tiled=True
        ).astype(jnp.float32),
        lax.psum_scatter(
            summed_e.astype(jnp.bfloat16), "shard", scatter_dimension=0, tiled=True
        ).astype(jnp.float32),
    )
    blocks = lax.psum((group[0], group[1], group[2]), "rep")
    inverse = 1.0 / (grad_xproj.shape[0] * count_rep * count_shard)
    mean_x = blocks[0] * inverse
    mean_c = blocks[1] * inverse
    mean_e = blocks[2] * inverse
    partial_squares = jnp.sum(mean_x * mean_x) + jnp.sum(mean_c * mean_c) + jnp.sum(mean_e * mean_e)
    squares = lax.psum(partial_squares, "shard")
    norm_value = jnp.sqrt(squares)
    clip_factor = jnp.minimum(1.0, 1.0 / (norm_value + 1e-06))
    wx, mx, vx = adamw_update(weight_xproj, moment_xproj, second_xproj, mean_x, clip_factor)
    wc, mc, vc = adamw_update(weight_chan, moment_chan, second_chan, mean_c, clip_factor)
    we, me, ve = adamw_update(weight_embed, moment_embed, second_embed, mean_e, clip_factor)
    gathered = (
        lax.all_gather(wx.astype(jnp.bfloat16), "shard", axis=1, tiled=True),
        lax.all_gather(wc.astype(jnp.bfloat16), "shard", axis=2, tiled=True),
        lax.all_gather(we.astype(jnp.bfloat16), "shard", axis=0, tiled=True),
    )
    return (
        wx,
        wc,
        we,
        mx,
        mc,
        me,
        vx,
        vc,
        ve,
        gathered[0],
        gathered[1],
        gathered[2],
        jnp.reshape(norm_value, (1,)),
    )


def solution(mesh):
    placed = (
        P(("rep", "shard"), None, None, None),
        P(("rep", "shard"), None, None, None),
        P(("rep", "shard"), None, None),
        P(None, "shard", None),
        P(None, None, "shard"),
        P("shard", None),
        P(None, "shard", None),
        P(None, None, "shard"),
        P("shard", None),
        P(None, "shard", None),
        P(None, None, "shard"),
        P("shard", None),
    )
    return jax.shard_map(
        on_device,
        mesh=mesh,
        in_specs=placed,
        out_specs=(
            P(None, "shard", None),
            P(None, None, "shard"),
            P("shard", None),
            P(None, "shard", None),
            P(None, None, "shard"),
            P("shard", None),
            P(None, "shard", None),
            P(None, None, "shard"),
            P("shard", None),
            P(),
            P(),
            P(),
            P(),
        ),
        check_vma=False,
    )
```

profile of v0, /device:TPU:0, one launch (start us, length us, event | category | flops | bytes accessed | tf_op | source)
XLA Modules:
  0.0 805.7 jit_solution(3559955693259106270)
XLA Ops:
  7.2 0.0 reduce-scatter.10.cloned.1.call-start
  7.2 6.5 reduce_sum.65
  13.7 66.3 %copy.25 = bf16[2,118,3072]{0,1,2:T(8,128)(2,1)} copy(bf16[2,118,3072]{2,0,1:T(2,128)(2,1)S(1)} %reduce_sum.65) | data formatting | bytes 2899968
  80.0 0.0 copy-start.1
  80.0 86.8 %reshape.30 = bf16[3072,236]{1,0:T(8,128)(2,1)} reshape(bf16[3072,118,2]{2,1,0:T(8,128)(2,1)} %bitcast.1) | data formatting | bytes 2899968
  166.8 0.0 reduce-scatter.10.cloned.1.call-update
  166.8 0.0 reduce-scatter.6.cloned.1.call-start
  166.9 0.0 copy-done.1
  166.9 2.2 reduce_sum.63
  169.0 0.0 reduce-scatter.6.cloned.1.call-update
  169.1 0.0 reduce-scatter.8.cloned.1.call-start
  169.1 6.5 reduce_sum.67
  175.6 0.0 reduce-scatter.8.cloned.1.call-update
  175.6 0.2 all-gather.6.cloned.1.call-start
  175.9 22.1 %reduce-scatter.10.cloned.1.call-done = bf16[1536,236]{1,0:T(8,128)(2,1)} async-done(((bf16[3072,236]{1,0:T(8,128)(2,1)}), bf16[1536,236]{1,0:T(8,128)(2,1)}) %reduce-scatter.10.cloned.1.call-update) | async-done | bytes 725008
  198.0 37.8 %reshape.31 = bf16[1536,118,2]{2,1,0:T(8,128)(2,1)} reshape(bf16[1536,236]{1,0:T(8,128)(2,1)} %reduce-scatter.10.cloned.1.call-done) | data formatting | bytes 1449984
  235.8 42.0 %copy.26 = bf16[2,118,1536]{2,0,1:T(2,128)(2,1)} copy(bf16[2,118,1536]{0,1,2:T(8,128)(2,1)} %bitcast.4) | data formatting | bytes 1449984
  277.8 0.0 reduce-scatter.6.cloned.1.call-done
  277.8 2.7 reduce-scatter.8.cloned.1.call-done
  280.4 381.2 %all-reduce.2 = (f32[2,1536,128]{2,1,0:T(8,128)}, f32[2,118,1536]{2,0,1:T(2,128)}, f32[512,1536]{1,0:T(8,128)S(1)}) all-reduce(bf16[2,1536,128]{2,1,0:T(8,128)(2,1)} %reduce-scatter.6.cloned.1.call-done, bf16[2,118,1536]{2,0,1:T(2,128)(2,1)} %copy.26, ...), channel_id=1, replica_groups=mesh['rep'=64,'shard'=2] {'rep'}, use_global_device_ids=true, to_apply=%region_2.0 | all-reduce | flops 1542144 | bytes 9252864 | tf_op jit(solution)/shard_map/psum | solution.py:54
  661.7 0.0 copy-start
  661.7 2.5 multiply_reduce_fusion.1
  664.2 0.0 copy-done
  664.2 2.1 multiply_reduce_fusion.2
  666.3 1.4 multiply_reduce_fusion
  669.7 5.4 psum.31
  675.9 8.4 %fusion.5 = (bf16[2,118,1536]{2,0,1:T(2,128)(2,1)}, f32[2,118,1536]{2,0,1:T(2,128)}, f32[2,118,1536]{2,0,1:T(2,128)}, f32[2,118,1536]{2,0,1:T(2,128)}) fusion(f32[2,118,1536]{2,0,1:T(2,128)} %param.16, f32[2,118,1536]{2,0,1:T(2,128)} %get-tuple-element.14, f32[]{:T(128)S(6)} %mul.157, f32[2,118,1536]{2,0,1:T(2,128)} %param.19, f32[2,118,1536]{2,0,1:T(2,128)} %param.22), kind=kLoop, calls=%fused_computation.16 | loop fusion | flops 6162432 | bytes 10874884 | tf_op jit(solution)/shard_map/convert_element_type | solution.py:68
  684.3 0.0 all-gather.6.cloned.1.call-update
  684.3 0.0 all-gather.4.cloned.1.call-start
  684.4 6.3 fusion.7
  690.6 0.0 all-gather.4.cloned.1.call-update
  690.6 0.3 all-gather.8.cloned.1.call-start
  690.9 7.3 fusion.3
  698.2 0.0 all-gather.8.cloned.1.call-update
  698.2 8.1 %all-gather.6.cloned.1.call-done = bf16[2,118,3072]{2,0,1:T(2,128)(2,1)} async-done(((bf16[2,118,1536]{2,0,1:T(2,128)(2,1)}), bf16[2,118,3072]{2,0,1:T(2,128)(2,1)}) %all-gather.6.cloned.1.call-update) | async-done | bytes 1450000 | tf_op jit(solution)/shard_map/all_gather | solution.py:68
  706.3 32.9 %all-gather.4.cloned.1.call-done = bf16[2,3072,128]{2,1,0:T(8,128)(2,1)} async-done(((bf16[2,1536,128]{2,1,0:T(8,128)(2,1)}), bf16[2,3072,128]{2,1,0:T(8,128)(2,1)}) %all-gather.4.cloned.1.call-update) | async-done | bytes 1572880 | tf_op jit(solution)/shard_map/all_gather | solution.py:67
  739.2 50.6 %all-gather.8.cloned.1.call-done = bf16[1024,1536]{1,0:T(8,128)(2,1)} async-done(((bf16[512,1536]{1,0:T(8,128)(2,1)}), bf16[1024,1536]{1,0:T(8,128)(2,1)}) %all-gather.8.cloned.1.call-update) | async-done | bytes 3145744 | tf_op jit(solution)/shard_map/all_gather | solution.py:69
  789.8 0.0 copy-start.2
  789.8 2.8 copy.36
  792.6 3.5 copy.37
  796.1 0.0 copy-done.2
  796.1 1.7 copy.38
Async XLA Ops:
  7.2 190.8 %reduce-scatter.10.cloned.1.call-start = ((), (), s32[]{:S(2)}) async-start(), calls=%async_computation.8 | async-start | bytes 2359296
  80.0 86.8 %copy-start.1 = (bf16[2,2,3072,128]{3,2,1,0:T(8,128)(2,1)S(1)}, bf16[2,2,3072,128]{3,2,1,0:T(8,128)(2,1)}, u32[]{:S(2)}) copy-start(bf16[2,2,3072,128]{3,2,1,0:T(8,128)(2,1)} %param.12) | copy-start | bytes 9437188
  166.8 111.0 %reduce-scatter.6.cloned.1.call-start = ((), (), s32[]{:S(2)}) async-start(), calls=%async_computation.3 | async-start | bytes 2359296 | tf_op jit(solution)/shard_map/reduce_scatter | solution.py:44
  169.1 111.4 %reduce-scatter.8.cloned.1.call-start = ((), (), s32[]{:S(2)}) async-start(), calls=%async_computation.4 | async-start | bytes 4718592 | tf_op jit(solution)/shard_map/reduce_scatter | solution.py:50
  175.6 530.7 %all-gather.6.cloned.1.call-start = ((), (), s32[]{:S(2)}) async-start(), calls=%async_computation.6 | async-start | bytes 2174976 | tf_op jit(solution)/shard_map/all_gather | solution.py:68
  661.7 2.5 copy-start
  684.3 54.9 %all-gather.4.cloned.1.call-start = ((), (), s32[]{:S(2)}) async-start(), calls=%async_computation.5 | async-start | bytes 2359296 | tf_op jit(solution)/shard_map/all_gather | solution.py:67
  690.6 99.2 %all-gather.8.cloned.1.call-start = ((), (), s32[]{:S(2)}) async-start(), calls=%async_computation.7 | async-start | bytes 4718592 | tf_op jit(solution)/shard_map/all_gather | solution.py:69
  789.8 6.3 copy-start.2
Sparse Core Ops, SparseCore 0:
  166.9 31.0 reduce-scatter.9
  201.0 29.5 reduce-scatter.5
  233.6 46.8 reduce-scatter.7
  684.4 21.8 all-gather.5
  708.5 30.6 all-gather.3
  741.4 48.4 all-gather.7
where the time goes:
time: 810 us; the launch traced here: 806 us
  blocking collectives  387 us (48%)
  local copies, waits for them, and re-layouts  241 us (30%)
  waiting for transfers between devices  116 us (14%)
  other arithmetic  43.2 us (5%)
  between operations  18 us (2%)
    psum x1, blocking collectives, on_device(): blocks = lax.psum((group[0], group[1], group[2]), 'rep')  381 us
    unnamed x13, local copies, waits for them, and re-layouts  241 us
    all_gather x1, waiting for transfers between devices, on_device(): lax.all_gather(we.astype(jnp.bfloat16), 'shard', axis=0, tiled=True)  50.6 us
    all_gather x1, waiting for transfers between devices, on_device(): lax.all_gather(wx.astype(jnp.bfloat16), 'shard', axis=1, tiled=True)  32.9 us
    unnamed x7, waiting for transfers between devices  22.2 us
  transfers between devices with their start and end apart: 6, of which 5 were waited for; matrix products, arithmetic and copies ran while one was open for 13% of the time, Pallas kernels for 0%

commit v1 on v0

--- a/solution.py
+++ b/solution.py
@@ -37,25 +37,23 @@
 ):
     count_rep = lax.axis_size("rep")
     count_shard = lax.axis_size("shard")
-    summed_x = jnp.sum(grad_xproj, axis=0, dtype=jnp.float32)
-    summed_c = jnp.sum(grad_chan, axis=0, dtype=jnp.float32)
+    micro, layers, inner, xw = grad_xproj.shape
+    _, _, ch, _ = grad_chan.shape
+    gx = grad_xproj.reshape(micro, layers, count_shard, inner // count_shard, xw)
+    summed_x = jnp.transpose(jnp.sum(gx, axis=0, dtype=jnp.float32), (1, 0, 2, 3))
+    gc = grad_chan.reshape(micro, layers, ch, count_shard, inner // count_shard)
+    summed_c = jnp.transpose(jnp.sum(gc, axis=0, dtype=jnp.float32), (2, 0, 1, 3))
     summed_e = jnp.sum(grad_embed, axis=0, dtype=jnp.float32)
-    group = (
-        lax.psum_scatter(
-            summed_x.astype(jnp.bfloat16), "shard", scatter_dimension=1, tiled=True
-        ).astype(jnp.float32),
-        lax.psum_scatter(
-            summed_c.astype(jnp.bfloat16), "shard", scatter_dimension=2, tiled=True
-        ).astype(jnp.float32),
-        lax.psum_scatter(
-            summed_e.astype(jnp.bfloat16), "shard", scatter_dimension=0, tiled=True
-        ).astype(jnp.float32),
-    )
-    blocks = lax.psum((group[0], group[1], group[2]), "rep")
-    inverse = 1.0 / (grad_xproj.shape[0] * count_rep * count_shard)
-    mean_x = blocks[0] * inverse
-    mean_c = blocks[1] * inverse
-    mean_e = blocks[2] * inverse
+    part_x = lax.psum_scatter(summed_x.astype(jnp.bfloat16), "shard", scatter_dimension=0, tiled=True)
+    part_c = lax.psum_scatter(summed_c.astype(jnp.bfloat16), "shard", scatter_dimension=0, tiled=True)
+    part_e = lax.psum_scatter(summed_e.astype(jnp.bfloat16), "shard", scatter_dimension=0, tiled=True)
+    block_x = lax.psum(part_x, "rep")[0]
+    block_c = lax.psum(part_c, "rep")[0]
+    block_e = lax.psum(part_e, "rep")
+    inverse = 1.0 / (micro * count_rep * count_shard)
+    mean_x = block_x.astype(jnp.float32) * inverse
+    mean_c = block_c.astype(jnp.float32) * inverse
+    mean_e = block_e.astype(jnp.float32) * inverse
     partial_squares = jnp.sum(mean_x * mean_x) + jnp.sum(mean_c * mean_c) + jnp.sum(mean_e * mean_e)
     squares = lax.psum(partial_squares, "shard")
     norm_value = jnp.sqrt(squares)

time: 810 us -> 957 us (1.18)
  waiting for transfers between devices: 116 us -> 862 us
  blocking collectives: 387 us -> 5.45 us
  local copies, waits for them, and re-layouts: 241 us -> 25.7 us
    psum x0 -> x1, waiting for transfers between devices: none -> 649 us  [on_device(): block_x = lax.psum(part_x, 'rep')[0]]
    psum x1 -> x0, blocking collectives: 381 us -> none  [on_device(): blocks = lax.psum((group[0], group[1], group[2]), 'rep')]
    unnamed x13 -> x23, local copies, waits for them, and re-layouts: 241 us -> 21.6 us
    unnamed x7, waiting for transfers between devices: 22.2 us -> 84.8 us
    reduce_scatter x1, waiting for transfers between devices: 2.66 us -> 45 us  [on_device(): lax.psum_scatter(summed_e.astype(jnp.bfloat16), 'shard', scatter_dimensio...]
  transfers between devices with their start and end apart: 6 -> 6, of which waited for: 5 -> 6; matrix products, arithmetic and copies ran while one was open for 13% -> 4% of each run, Pallas kernels for 0% -> 0%
where the time goes in v1:
time: 957 us; the launch traced here: 956 us
  waiting for transfers between devices  862 us (90%)
  other arithmetic  43.8 us (5%)
  local copies, waits for them, and re-layouts  25.7 us (3%)
  between operations  18 us (2%)
    psum x1, waiting for transfers between devices, on_device(): block_x = lax.psum(part_x, 'rep')[0]  649 us
    unnamed x7, waiting for transfers between devices  84.8 us
    all_gather x1, waiting for transfers between devices, on_device(): lax.all_gather(we.astype(jnp.bfloat16), 'shard', axis=0, tiled=True)  50.6 us
    reduce_scatter x1, waiting for transfers between devices, on_device(): lax.psum_scatter(summed_e.astype(jnp.bfloat16), 'shard', scatter_dimensio...  45 us
    all_gather x1, waiting for transfers between devices, on_device(): lax.all_gather(wx.astype(jnp.bfloat16), 'shard', axis=1, tiled=True)  28.4 us
    unnamed x23, local copies, waits for them, and re-layouts  21.6 us
  transfers between devices with their start and end apart: 6, of which 6 were waited for; matrix products, arithmetic and copies ran while one was open for 4% of the time, Pallas kernels for 0%

profile of v1, /device:TPU:0, one launch (start us, length us, event | category | flops | bytes accessed | tf_op | source)
XLA Modules:
  0.0 955.8 jit_solution(9110890464267347480)
XLA Ops:
  7.2 0.0 all-reduce.9.cloned.1.call-start
  7.2 6.5 reduce_sum.65
  13.7 1.0 reshape.52
  14.7 2.2 copy.42
  16.9 4.0 reduce_sum.63
  20.9 0.0 all-reduce.9.cloned.1.call-update
  20.9 0.0 reduce-scatter.5.cloned.1.call-start
  21.0 6.5 reduce_sum.67
  27.5 0.0 copy-start.6
  27.5 0.0 reduce-scatter.5.cloned.1.call-update
  27.5 0.0 all-reduce.7.cloned.1.call-start
  27.6 0.6 copy-done.6
  28.1 0.6 dynamic-slice
  28.7 84.7 %all-reduce.9.cloned.1.call-done = (bf16[2,2,1536,128]{3,2,0,1:T(8,128)(2,1)}, bf16[2,2,118,1536]{3,1,2,0:T(2,128)(2,1)}) async-done(((bf16[2,2,1536,128]{3,2,0,1:T(8,128)(2,1)}, bf16[2,2,118,1536]{3,1,2,0:T(2,128)(2,1)}), (bf16[2,2,1536,128]{3,2,0,1:T(8,128)(2,1)}, bf16[2,2,118,1536]{3,1,2,0:T(2,128)(2,1)})) %all-reduce.9.cloned.1.call-update) | async-done | bytes 3022864
  113.4 0.0 copy-start.5
  113.4 2.4 constant_dynamic-slice_fusion
  115.8 0.9 copy.43
  116.7 0.0 copy-done.5
  116.7 1.6 constant_dynamic-slice_fusion.1
  118.3 45.0 %reduce-scatter.5.cloned.1.call-done = bf16[512,1536]{1,0:T(8,128)(2,1)} async-done(((bf16[1024,1536]{1,0:T(8,128)(2,1)}), bf16[512,1536]{1,0:T(8,128)(2,1)}) %reduce-scatter.5.cloned.1.call-update) | async-done | bytes 1572880 | tf_op jit(solution)/shard_map/reduce_scatter | solution.py:49
  163.3 0.0 all-reduce.7.cloned.1.call-update
  163.3 0.2 all-gather.6.cloned.1.call-start
  163.6 648.8 %all-reduce.7.cloned.1.call-done = (bf16[1,2,1536,128]{3,2,0,1:T(8,128)(2,1)}, bf16[1,2,118,1536]{3,2,1,0:T(8,128)(2,1)}, bf16[512,1536]{1,0:T(8,128)(2,1)}) async-done(((bf16[1,2,1536,128]{3,2,0,1:T(8,128)(2,1)}, bf16[1,2,118,1536]{3,2,1,0:T(8,128)(2,1)}, bf16[512,1536]{1,0:T(8,128)(2,1)}), (bf16[1,2,1536,128]{3,2,0,1:T(8,128)(2,1)}, bf16[1,2,118,1536]{3,2,1,0:T(8,128)(2,1)}, ...) | async-done | bytes 3084304 | tf_op jit(solution)/shard_map/psum | solution.py:50
  812.4 0.0 copy-start.4
  812.4 2.2 fusion.12
  814.5 2.1 fusion.6
  816.7 2.8 fusion.3
  821.5 5.4 psum.31
  827.6 0.0 copy-done.4
  827.6 5.5 fusion.20
  833.2 0.0 all-gather.6.cloned.1.call-update
  833.2 0.0 all-gather.4.cloned.1.call-start
  833.3 0.0 copy-start
  833.3 6.0 fusion.23
  839.3 0.0 all-gather.4.cloned.1.call-update
  839.3 0.0 all-gather.8.cloned.1.call-start
  839.4 0.0 copy-done
  839.4 8.1 fusion.17
  847.5 0.0 copy-start.2
  847.5 0.0 all-gather.8.cloned.1.call-update
  847.5 0.0 copy-start.1
  847.5 1.3 copy-done.2
  848.9 2.2 copy.48
  851.1 0.0 copy-done.1
  851.1 2.2 copy.49
  853.3 2.2 copy.50
  855.5 4.8 all-gather.6.cloned.1.call-done
  860.4 4.0 copy.51
  864.3 28.4 %all-gather.4.cloned.1.call-done = bf16[2,3072,128]{2,1,0:T(8,128)(2,1)} async-done(((bf16[2,1536,128]{2,1,0:T(8,128)(2,1)}), bf16[2,3072,128]{2,1,0:T(8,128)(2,1)}) %all-gather.4.cloned.1.call-update) | async-done | bytes 1572880 | tf_op jit(solution)/shard_map/all_gather | solution.py:65
  892.7 50.6 %all-gather.8.cloned.1.call-done = bf16[1024,1536]{1,0:T(8,128)(2,1)} async-done(((bf16[512,1536]{1,0:T(8,128)(2,1)}), bf16[1024,1536]{1,0:T(8,128)(2,1)}) %all-gather.8.cloned.1.call-update) | async-done | bytes 3145744 | tf_op jit(solution)/shard_map/all_gather | solution.py:67
  943.3 0.0 copy-start.3
  943.3 2.8 copy.73
  946.1 0.0 copy-done.3
  946.1 1.7 copy.74
Async XLA Ops:
  7.2 106.2 %all-reduce.9.cloned.1.call-start = ((), (), s32[]{:S(2)}) async-start(), calls=%async_computation.6 | async-start | bytes 6045696
  20.9 142.4 %reduce-scatter.5.cloned.1.call-start = ((), (), s32[]{:S(2)}) async-start(), calls=%async_computation.1 | async-start | bytes 4718592 | tf_op jit(solution)/shard_map/reduce_scatter | solution.py:49
  27.5 0.7 copy-start.6
  27.5 784.8 %all-reduce.7.cloned.1.call-start = ((), (), s32[]{:S(2)}) async-start(), calls=%async_computation.5 | async-start | bytes 6193152 | tf_op jit(solution)/shard_map/psum | solution.py:50
  113.4 3.3 copy-start.5
  163.3 697.0 %all-gather.6.cloned.1.call-start = ((), (), s32[]{:S(2)}) async-start(), calls=%async_computation.3 | async-start | bytes 2211840 | tf_op jit(solution)/shard_map/all_gather | solution.py:66
  812.4 15.3 %copy-start.4 = (bf16[1,2,118,1536]{3,2,1,0:T(8,128)(2,1)S(1)}, bf16[1,2,118,1536]{3,2,1,0:T(8,128)(2,1)}, u32[]{:S(2)}) copy-start(bf16[1,2,118,1536]{3,2,1,0:T(8,128)(2,1)} %get-tuple-element.53) | copy-start | bytes 2174980
  833.2 59.5 %all-gather.4.cloned.1.call-start = ((), (), s32[]{:S(2)}) async-start(), calls=%async_computation.2 | async-start | bytes 2359296 | tf_op jit(solution)/shard_map/all_gather | solution.py:65
  833.3 6.1 copy-start
  839.3 104.0 %all-gather.8.cloned.1.call-start = ((), (), s32[]{:S(2)}) async-start(), calls=%async_computation.4 | async-start | bytes 4718592 | tf_op jit(solution)/shard_map/all_gather | solution.py:67
  847.5 1.4 copy-start.2
  847.5 3.6 copy-start.1
  943.3 2.8 copy-start.3
Sparse Core Ops, SparseCore 0:
  21.1 92.3 all-reduce.8
  116.4 46.8 reduce-scatter.4
  167.2 645.1 all-reduce.6
  833.3 27.0 all-gather.5
  862.0 30.6 all-gather.3
  894.9 48.4 all-gather.7

commit v2 on v1

v2 whole, which is shorter than its diff:
```python
import jax
import jax.numpy as jnp
from jax import lax
from jax.sharding import Mesh, PartitionSpec as P

beta_one = 0.9
beta_two = 0.999
learn_rate = 0.003
decay_rate = 0.1
epsilon = 1e-08
correct_one = 0.9999734386011124
correct_two = 0.09520785288629094

AXES = ("z", "y", "xh", "core", "shard")
XRING = ("xh", "shard")


def adamw_update(weight, moment, second, gradient, clip_factor):
    clipped = clip_factor * gradient
    new_moment = beta_one * moment + (1.0 - beta_one) * clipped
    new_second = beta_two * second + (1.0 - beta_two) * clipped * clipped
    step_size = new_moment / correct_one / (jnp.sqrt(new_second / correct_two) + epsilon)
    new_weight = weight - learn_rate * (step_size + decay_rate * weight)
    return (new_weight, new_moment, new_second)


def reduce_block(buf):
    part = lax.psum_scatter(buf.astype(jnp.bfloat16), "core", scatter_dimension=0, tiled=True)
    part = lax.psum_scatter(part, XRING, scatter_dimension=1, tiled=True)
    part = lax.psum_scatter(part.astype(jnp.float32), "y", scatter_dimension=2, tiled=True)
    part = lax.psum(part, "z").astype(jnp.bfloat16)
    part = lax.all_gather(part, "y", axis=2, tiled=True)
    part = lax.all_gather(part, "xh", axis=1, tiled=True)
    return lax.all_gather(part, "core", axis=0, tiled=True)


def swap_halves(own, split_axis):
    n = lax.axis_size(XRING)
    first, second = jnp.split(own, 2, axis=split_axis)
    from_left = lax.ppermute(first, XRING, perm=[(p, (p + 1) % n) for p in range(n)])
    from_right = lax.ppermute(second, XRING, perm=[(p, (p - 1) % n) for p in range(n)])
    return jnp.concatenate([from_left, from_right], axis=split_axis)


def place(own, other, axis):
    low = lax.axis_index("shard") == 0
    lo = jnp.where(low, own, other)
    hi = jnp.where(low, other, own)
    return jnp.concatenate([lo, hi], axis=axis)


def on_device(
    grad_xproj,
    grad_chan,
    grad_embed,
    weight_xproj,
    weight_chan,
    weight_embed,
    moment_xproj,
    moment_chan,
    moment_embed,
    second_xproj,
    second_chan,
    second_embed,
):
    n_core = lax.axis_size("core")
    n_xh = lax.axis_size("xh")
    n_y = lax.axis_size("y")
    n_s = lax.axis_size("shard")
    total = grad_xproj.shape[0] * lax.axis_size(AXES)
    layers, inner, xw = grad_xproj.shape[1:]
    ch = grad_chan.shape[2]
    rows_e, width = grad_embed.shape[1:]
    half = inner // n_s

    sx = jnp.sum(grad_xproj, axis=0, dtype=jnp.float32)
    sx = sx.reshape(layers, n_s, n_xh, n_y, half // (n_xh * n_y), xw)
    sx = jnp.transpose(sx, (0, 2, 1, 3, 4, 5)).reshape(layers, n_xh * n_s, n_y, half // (n_xh * n_y), xw)

    se = jnp.sum(grad_embed, axis=0, dtype=jnp.float32)
    re = rows_e // (n_s * n_core * n_xh * n_y)
    se = se.reshape(n_s, n_core, n_xh, n_y, re, width)
    se = jnp.transpose(se, (1, 2, 0, 3, 4, 5)).reshape(n_core, n_xh * n_s, n_y, re, width)

    sc = jnp.sum(grad_chan, axis=0, dtype=jnp.float32)
    step = n_xh * n_y * 8
    ch_pad = -(-ch // step) * step
    sc = jnp.pad(sc, ((0, 0), (0, ch_pad - ch), (0, 0)))
    rc = ch_pad // (n_xh * n_y)
    sc = sc.reshape(layers, n_xh, n_y, rc, n_s, half)
    sc = jnp.transpose(sc, (0, 1, 4, 2, 3, 5)).reshape(layers, n_xh * n_s, n_y, rc, half)

    inverse = 1.0 / total
    mean_x = reduce_block(sx).reshape(layers, half, xw).astype(jnp.float32) * inverse
    mean_c = reduce_block(sc).reshape(layers, ch_pad, half)[:, :ch, :].astype(jnp.float32) * inverse
    mean_e = reduce_block(se).reshape(rows_e // n_s, width).astype(jnp.float32) * inverse

    partial_squares = jnp.sum(mean_x * mean_x) + jnp.sum(mean_c * mean_c) + jnp.sum(mean_e * mean_e)
    squares = lax.psum(partial_squares, "shard")
    norm_value = jnp.sqrt(squares)
    clip_factor = jnp.minimum(1.0, 1.0 / (norm_value + 1e-06))
    wx, mx, vx = adamw_update(weight_xproj, moment_xproj, second_xproj, mean_x, clip_factor)
    wc, mc, vc = adamw_update(weight_chan, moment_chan, second_chan, mean_c, clip_factor)
    we, me, ve = adamw_update(weight_embed, moment_embed, second_embed, mean_e, clip_factor)
    bx = wx.astype(jnp.bfloat16)
    bc = wc.astype(jnp.bfloat16)
    be = we.astype(jnp.bfloat16)
    full_x = place(bx, swap_halves(bx, 0), 1)
    full_c = place(bc, swap_halves(bc, 0), 2)
    full_e = place(be, swap_halves(be, 0), 0)
    return (wx, wc, we, mx, mc, me, vx, vc, ve, full_x, full_c, full_e, jnp.reshape(norm_value, (1,)))


def solution(mesh):
    rep = mesh.shape["rep"]
    fine = Mesh(mesh.devices.reshape(rep // 16, 4, 2, 2, mesh.shape["shard"]), AXES)
    grads = ("z", "y", "xh", "core", "shard")
    placed = (
        P(grads, None, None, None),
        P(grads, None, None, None),
        P(grads, None, None),
        P(None, "shard", None),
        P(None, None, "shard"),
        P("shard", None),
        P(None, "shard", None),
        P(None, None, "shard"),
        P("shard", None),
        P(None, "shard", None),
        P(None, None, "shard"),
        P("shard", None),
    )
    return jax.shard_map(
        on_device,
        mesh=fine,
        in_specs=placed,
        out_specs=(
            P(None, "shard", None),
            P(None, None, "shard"),
            P("shard", None),
            P(None, "shard", None),
            P(None, None, "shard"),
            P("shard", None),
            P(None, "shard", None),
            P(None, None, "shard"),
            P("shard", None),
            P(),
            P(),
            P(),
            P(),
        ),
        check_vma=False,
    )
```

time: 957 us -> 378 us (0.39)
  waiting for transfers between devices: 862 us -> 196 us
  blocking collectives: 5.45 us -> 94.4 us
    psum x1 -> x0, waiting for transfers between devices: 649 us -> none  [on_device(): block_x = lax.psum(part_x, 'rep')[0]]
    reduce_scatter x1 -> x9, waiting for transfers between devices: 45 us -> 181 us  [the longest x3 74.9 us: reduce_block(): part = lax.psum_scatter(part, XRING, scatter_dimension=1, tiled=True)]
    unnamed x7 -> x10, waiting for transfers between devices: 84.8 us -> 0.16 us
    all_gather x3 -> x1, waiting for transfers between devices: 83.8 us -> 0.02 us  [reduce_block(): return lax.all_gather(part, 'core', axis=0, tiled=True)]
    all_gather x0 -> x8, blocking collectives: none -> 67.2 us  [the longest x3 36.8 us: reduce_block(): part = lax.all_gather(part, 'y', axis=2, tiled=True)]
    psum x0 -> x1, blocking collectives: none -> 21.8 us  [reduce_block(): part = lax.psum(part, 'z').astype(jnp.bfloat16)]
    ppermute x0 -> x6, waiting for transfers between devices: none -> 14.6 us  [the longest x3 13.2 us: swap_halves(): lax.ppermute(first, XRING, perm=[(p, (p + 1) % n) for p in range(n)])]
    unnamed x23, local copies, waits for them, and re-layouts: 21.6 us -> 10.9 us
  transfers between devices with their start and end apart: 6 -> 16, of which waited for: 6 -> 12; matrix products, arithmetic and copies ran while one was open for 4% -> 9% of each run, Pallas kernels for 0% -> 0%
where the time goes in v2:
time: 378 us; the launch traced here: 377 us
  waiting for transfers between devices  196 us (52%)
  blocking collectives  94.4 us (25%)
  other arithmetic  41.2 us (11%)
  between operations  18.3 us (5%)
  local copies, waits for them, and re-layouts  18.1 us (5%)
  starting transfers between devices  9.02 us (2%)
    reduce_scatter x3, waiting for transfers between devices, reduce_block(): part = lax.psum_scatter(part, XRING, scatter_dimension=1, tiled=True)  74.9 us
    reduce_scatter x3, waiting for transfers between devices, reduce_block(): lax.psum_scatter(part.astype(jnp.float32), 'y', scatter_dimension=2, tile...  70.6 us
    all_gather x3, blocking collectives, reduce_block(): part = lax.all_gather(part, 'y', axis=2, tiled=True)  36.8 us
    reduce_scatter x3, waiting for transfers between devices, reduce_block(): lax.psum_scatter(buf.astype(jnp.bfloat16), 'core', scatter_dimension=0, t...  35.9 us
    all_gather x3, blocking collectives, reduce_block(): part = lax.all_gather(part, 'xh', axis=1, tiled=True)  25.7 us
    psum x1, blocking collectives, reduce_block(): part = lax.psum(part, 'z').astype(jnp.bfloat16)  21.8 us
    ppermute x3, waiting for transfers between devices, swap_halves(): lax.ppermute(first, XRING, perm=[(p, (p + 1) % n) for p in range(n)])  13.2 us
    unnamed x23, local copies, waits for them, and re-layouts  10.9 us
  transfers between devices with their start and end apart: 16, of which 12 were waited for; matrix products, arithmetic and copies ran while one was open for 9% of the time, Pallas kernels for 0%

profile of v2, /device:TPU:0, one launch (start us, length us, event | category | flops | bytes accessed | tf_op | source)
XLA Modules:
  0.0 377.3 jit_solution(15918011315246353993)
XLA Ops:
  7.2 6.5 %reduce.4 = bf16[2,118,3072]{2,0,1:T(2,128)(2,1)S(1)} reduce(bf16[2,2,118,3072]{3,1,2,0:T(2,128)(2,1)} %param.13, bf16[]{:T(256)} %constant.16.clone.1), dimensions={0}, to_apply=%region_6.7.clone | reduce | flops 724992 | bytes 4349954 | tf_op jit(solution)/shard_map/reduce_sum | solution.py:85
  13.7 1.2 pad.5
  14.9 1.0 reshape.54
  16.0 1.5 copy.34
  17.5 2.9 reduce_sum.60
  20.4 1.3 copy.29
  21.8 6.1 %reduce_sum.64 = bf16[1024,1536]{1,0:T(8,128)(2,1)S(1)} reduce(bf16[2,1024,1536]{2,1,0:T(8,128)(2,1)} %param.14, bf16[]{:T(256)} %constant.16.clone.1), dimensions={0}, to_apply=%region_12.13 | reduce | flops 1572864 | bytes 9437186 | tf_op jit(solution)/shard_map/reduce_sum | solution.py:80
  27.9 1.9 copy.38
  29.9 1.8 reduce-scatter.16.cloned.1.call-done
  31.8 16.1 %reduce-scatter.10.cloned.1.call-done = bf16[1,4,4,192,128]{4,3,2,1,0:T(8,128)(2,1)} async-done(((bf16[2,4,4,192,128]{4,3,2,1,0:T(8,128)(2,1)}), bf16[1,4,4,192,128]{4,3,2,1,0:T(8,128)(2,1)}) %reduce-scatter.10.cloned.1.call-update) | async-done | bytes 786448 | tf_op jit(solution)/shard_map/reduce_scatter | solution.py:28
  48.0 17.9 %reduce-scatter.22.cloned.1.call-done = bf16[1,4,4,32,1536]{4,3,2,1,0:T(8,128)(2,1)} async-done(((bf16[2,4,4,32,1536]{4,3,2,1,0:T(8,128)(2,1)}), bf16[1,4,4,32,1536]{4,3,2,1,0:T(8,128)(2,1)}) %reduce-scatter.22.cloned.1.call-update) | async-done | bytes 1572880 | tf_op jit(solution)/shard_map/reduce_scatter | solution.py:28
  66.0 26.2 %reduce-scatter.18.cloned.1.call-done = bf16[1,1,4,16,1536]{4,3,2,1,0:T(8,128)(2,1)} async-done(((bf16[1,4,4,16,1536]{4,3,2,1,0:T(8,128)(2,1)}), bf16[1,1,4,16,1536]{4,3,2,1,0:T(8,128)(2,1)}) %reduce-scatter.18.cloned.1.call-update) | async-done | bytes 196624 | tf_op jit(solution)/shard_map/reduce_scatter | solution.py:29
  92.2 1.7 convert_element_type.87
  93.9 22.8 %reduce-scatter.12.cloned.1.call-done = bf16[1,1,4,192,128]{4,3,2,1,0:T(8,128)(2,1)} async-done(((bf16[1,4,4,192,128]{4,3,2,1,0:T(8,128)(2,1)}), bf16[1,1,4,192,128]{4,3,2,1,0:T(8,128)(2,1)}) %reduce-scatter.12.cloned.1.call-update) | async-done | bytes 196624 | tf_op jit(solution)/shard_map/reduce_scatter | solution.py:29
  116.8 1.7 convert_element_type.80
  118.5 0.2 reduce-scatter.26.cloned.1.call-start
  118.7 25.9 %reduce-scatter.24.cloned.1.call-done = bf16[1,1,4,32,1536]{4,3,2,1,0:T(8,128)(2,1)} async-done(((bf16[1,4,4,32,1536]{4,3,2,1,0:T(8,128)(2,1)}), bf16[1,1,4,32,1536]{4,3,2,1,0:T(8,128)(2,1)}) %reduce-scatter.24.cloned.1.call-update) | async-done | bytes 393232 | tf_op jit(solution)/shard_map/reduce_scatter | solution.py:29
  144.6 2.0 convert_element_type.93
  146.6 21.7 %reduce-scatter.20.cloned.1.call-done = f32[1,1,1,16,1536]{4,3,2,1,0:T(8,128)} async-done(((f32[1,1,4,16,1536]{4,3,2,1,0:T(8,128)}), f32[1,1,1,16,1536]{4,3,2,1,0:T(8,128)}) %reduce-scatter.20.cloned.1.call-update) | async-done | bytes 98320 | tf_op jit(solution)/shard_map/reduce_scatter | solution.py:30
  168.3 23.6 %reduce-scatter.14.cloned.1.call-done = f32[1,1,1,192,128]{4,3,2,1,0:T(8,128)} async-done(((f32[1,1,4,192,128]{4,3,2,1,0:T(8,128)}), f32[1,1,1,192,128]{4,3,2,1,0:T(8,128)}) %reduce-scatter.14.cloned.1.call-update) | async-done | bytes 98320 | tf_op jit(solution)/shard_map/reduce_scatter | solution.py:30
  191.9 25.4 %reduce-scatter.26.cloned.1.call-done = f32[1,1,1,32,1536]{4,3,2,1,0:T(8,128)} async-done(((f32[1,1,4,32,1536]{4,3,2,1,0:T(8,128)}), f32[1,1,1,32,1536]{4,3,2,1,0:T(8,128)}) %reduce-scatter.26.cloned.1.call-update) | async-done | bytes 196624 | tf_op jit(solution)/shard_map/reduce_scatter | solution.py:30
  217.2 21.8 %all-reduce.3 = (bf16[1,1,1,192,128]{4,3,2,1,0:T(8,128)(2,1)S(1)}, bf16[1,1,1,16,1536]{4,3,2,1,0:T(8,128)(2,1)S(1)}, bf16[1,1,1,32,1536]{4,3,2,1,0:T(8,128)(2,1)S(1)}) all-reduce(f32[1,1,1,192,128]{4,3,2,1,0:T(8,128)} %reduce-scatter.14.cloned.1.call-done, ...), channel_id=1, replica_groups=mesh['z'=4,'y'=4,'xh'=2,'core'=2,'shard'=2] {'z'}, use_global_device_ids=true, to_apply=%region_4.5 | all-reduce | flops 98304 | bytes 589824 | tf_op jit(solution)/shard_map/psum | solution.py:31
  239.0 12.5 %all_gather.33 = bf16[1,1,4,32,1536]{4,3,1,0,2:T(8,128)(2,1)S(1)} all-gather(bf16[1,1,1,32,1536]{4,3,1,0,2:T(8,128)(2,1)S(1)} %bitcast.58), channel_id=1, replica_groups=mesh['z'=4,'y'=4,'xh'=2,'core'=2,'shard'=2] {'y'}, dimensions={2}, use_global_device_ids=true | all-gather | bytes 491520 | tf_op jit(solution)/shard_map/all_gather | solution.py:32
  251.5 10.1 %all_gather.34 = bf16[1,2,4,32,1536]{4,3,2,0,1:T(8,128)(2,1)} all-gather(bf16[1,1,4,32,1536]{4,3,2,0,1:T(8,128)(2,1)S(1)} %bitcast.55), channel_id=1, replica_groups=mesh['z'=4,'y'=4,'xh'=2,'core'=2,'shard'=2] {'xh'}, dimensions={1}, use_global_device_ids=true | all-gather | bytes 1179648 | tf_op jit(solution)/shard_map/all_gather | solution.py:33
  261.6 12.1 %all_gather.30 = bf16[1,1,4,16,1536]{4,3,1,0,2:T(8,128)(2,1)S(1)} all-gather(bf16[1,1,1,16,1536]{4,3,1,0,2:T(8,128)(2,1)S(1)} %bitcast.60), channel_id=1, replica_groups=mesh['z'=4,'y'=4,'xh'=2,'core'=2,'shard'=2] {'y'}, dimensions={2}, use_global_device_ids=true | all-gather | bytes 245760 | tf_op jit(solution)/shard_map/all_gather | solution.py:32
  273.7 12.1 %all_gather.27 = bf16[1,1,4,192,128]{4,3,1,0,2:T(8,128)(2,1)S(1)} all-gather(bf16[1,1,1,192,128]{4,3,1,0,2:T(8,128)(2,1)S(1)} %bitcast.59), channel_id=1, replica_groups=mesh['z'=4,'y'=4,'xh'=2,'core'=2,'shard'=2] {'y'}, dimensions={2}, use_global_device_ids=true | all-gather | bytes 245760 | tf_op jit(solution)/shard_map/all_gather | solution.py:32
  285.9 7.8 %all_gather.31 = bf16[1,2,4,16,1536]{4,3,2,0,1:T(8,128)(2,1)S(1)} all-gather(bf16[1,1,4,16,1536]{4,3,2,0,1:T(8,128)(2,1)S(1)} %bitcast.56), channel_id=1, replica_groups=mesh['z'=4,'y'=4,'xh'=2,'core'=2,'shard'=2] {'xh'}, dimensions={1}, use_global_device_ids=true | all-gather | bytes 589824 | tf_op jit(solution)/shard_map/all_gather | solution.py:33
  293.7 7.8 %all_gather.28 = bf16[1,2,4,192,128]{4,3,2,0,1:T(8,128)(2,1)S(1)} all-gather(bf16[1,1,4,192,128]{4,3,2,0,1:T(8,128)(2,1)S(1)} %bitcast.57), channel_id=1, replica_groups=mesh['z'=4,'y'=4,'xh'=2,'core'=2,'shard'=2] {'xh'}, dimensions={1}, use_global_device_ids=true | all-gather | bytes 589824 | tf_op jit(solution)/shard_map/all_gather | solution.py:33
  301.5 2.4 all_gather.29
  303.9 1.0 fusion.6
  304.9 2.4 all_gather.32
  307.3 1.0 fusion.11
  309.6 2.8 fusion.1
  313.2 5.4 %psum.31 = f32[]{:T(128)} all-reduce(f32[]{:T(128)S(6)} %add.83), channel_id=1, replica_groups=mesh['z'=4,'y'=4,'xh'=2,'core'=2,'shard'=2] {'shard'}, use_global_device_ids=true, to_apply=%region_18.19 | all-reduce | flops 1 | bytes 8 | tf_op jit(solution)/shard_map/psum | solution.py:99
  319.3 0.2 convert_multiply_fusion.2
  319.5 0.4 convert_multiply_fusion
  320.0 1.5 copy-done.1
  321.4 6.6 %fusion.13 = (bf16[512,1536]{1,0:T(8,128)(2,1)S(1)}, f32[512,1536]{1,0:T(8,128)}, f32[512,1536]{1,0:T(8,128)}, f32[512,1536]{1,0:T(8,128)}) fusion(f32[512,1536]{1,0:T(8,128)S(1)} %copy-done.1, f32[2,2,4,32,1536]{4,3,2,1,0:T(8,128)S(1)} %convert_multiply_fusion, f32[512,1536]{1,0:T(8,128)} %param.20, f32[512,1536]{1,0:T(8,128)} %param.23), kind=kLoop, calls=%fused_computation.47 | loop fusion | flops 12582912 | bytes 23592960 | tf_op jit(solution)/shard_map/convert_element_type | solution.py:107
  328.0 0.1 fusion.22
  328.1 1.7 collective-permute-start.4
  329.8 1.6 collective-permute-start.5
  331.5 1.5 fusion.16
  333.0 0.5 collective-permute-start.2
  333.5 2.8 collective-permute-start.3
  336.3 3.0 fusion.19
  339.3 0.1 fusion.23
  339.4 0.3 collective-permute-start
  339.7 2.2 copy.46
  341.9 2.2 copy.47
  344.2 2.2 copy.48
  346.4 11.4 %collective-permute-done.2 = bf16[1,118,1536]{2,1,0:T(8,128)(2,1)S(1)} collective-permute-done((bf16[1,118,1536]{2,1,0:T(8,128)(2,1)S(1)}, bf16[1,118,1536]{2,1,0:T(8,128)(2,1)S(1)}, u32[]{:S(2)}, u32[]{:S(2)}) %collective-permute-start.2) | collective-permute-done | bytes 362528 | tf_op jit(solution)/shard_map/ppermute | solution.py:40
  357.8 1.5 collective-permute-start.1
  359.4 0.2 broadcast_select_fusion.5
  359.6 0.2 pad_maximum_fusion.2
  359.8 2.6 copy.49
  362.4 1.8 collective-permute-done
  364.2 1.4 collective-permute-done.1
  365.6 0.1 constant_dynamic-update-slice_fusion
  365.6 0.2 broadcast_select_fusion.3
  365.8 1.2 pad_maximum_fusion.1
  367.1 0.1 constant_dynamic-update-slice_fusion.5
  367.1 0.1 constant_dynamic-update-slice_fusion.4
  367.2 0.2 broadcast_select_fusion.1
  367.4 1.9 pad_maximum_fusion
  (42 shorter events, 0.7 us)
Async XLA Ops:
  7.2 24.5 %reduce-scatter.16.cloned.1.call-start = ((), (), s32[]{:S(2)}) async-start(), calls=%async_computation.12 | async-start | bytes 2359296 | tf_op jit(solution)/shard_map/reduce_scatter | solution.py:28
  17.4 30.4 %reduce-scatter.10.cloned.1.call-start = ((), (), s32[]{:S(2)}) async-start(), calls=%async_computation.9 | async-start | bytes 2359296 | tf_op jit(solution)/shard_map/reduce_scatter | solution.py:28
  21.8 44.1 %reduce-scatter.22.cloned.1.call-start = ((), (), s32[]{:S(2)}) async-start(), calls=%async_computation.15 | async-start | bytes 4718592 | tf_op jit(solution)/shard_map/reduce_scatter | solution.py:28
  29.8 62.3 %reduce-scatter.18.cloned.1.call-start = ((), (), s32[]{:S(2)}) async-start(), calls=%async_computation.13 | async-start | bytes 983040 | tf_op jit(solution)/shard_map/reduce_scatter | solution.py:29
  31.7 85.0 %reduce-scatter.12.cloned.1.call-start = ((), (), s32[]{:S(2)}) async-start(), calls=%async_computation.10 | async-start | bytes 983040 | tf_op jit(solution)/shard_map/reduce_scatter | solution.py:29
  47.9 96.7 %reduce-scatter.24.cloned.1.call-start = ((), (), s32[]{:S(2)}) async-start(), calls=%async_computation.16 | async-start | bytes 1966080 | tf_op jit(solution)/shard_map/reduce_scatter | solution.py:29
  65.9 102.4 %reduce-scatter.20.cloned.1.call-start = ((), (), s32[]{:S(2)}) async-start(), calls=%async_computation.14 | async-start | bytes 491520 | tf_op jit(solution)/shard_map/reduce_scatter | solution.py:30
  93.9 98.0 %reduce-scatter.14.cloned.1.call-start = ((), (), s32[]{:S(2)}) async-start(), calls=%async_computation.11 | async-start | bytes 491520 | tf_op jit(solution)/shard_map/reduce_scatter | solution.py:30
  118.5 98.8 %reduce-scatter.26.cloned.1.call-start = ((), (), s32[]{:S(2)}) async-start(), calls=%async_computation.17 | async-start | bytes 983040 | tf_op jit(solution)/shard_map/reduce_scatter | solution.py:30
  146.6 163.0 %all-gather.2.cloned.1.call-start = ((), (), s32[]{:S(2)}) async-start(), calls=%async_computation.18 | async-start | bytes 2359296 | tf_op jit(solution)/shard_map/all_gather | solution.py:34
  312.4 7.1 %copy-start = (bf16[2,2,4,32,1536]{4,3,2,1,0:T(8,128)(2,1)S(1)}, bf16[2,2,4,32,1536]{4,3,2,1,0:T(8,128)(2,1)}, u32[]{:S(2)}) copy-start(bf16[2,2,4,32,1536]{4,3,2,1,0:T(8,128)(2,1)} %all-gather.2.cloned.1.call-done) | copy-start | bytes 4718596
  319.5 1.9 copy-start.1
  321.4 10.0 %copy-start.7 = (f32[2,118,1536]{2,0,1:T(2,128)S(1)}, f32[2,118,1536]{2,0,1:T(2,128)}, u32[]{:S(2)}) copy-start(f32[2,118,1536]{2,0,1:T(2,128)} %param.22) | copy-start | bytes 4349956
  328.0 3.4 copy-start.5
  328.0 3.4 copy-start.6
  328.1 38.9 %collective-permute-start.4 = (bf16[256,1536]{1,0:T(8,128)(2,1)S(1)}, bf16[256,1536]{1,0:T(8,128)(2,1)S(1)}, u32[]{:S(2)}, u32[]{:S(2)}) collective-permute-start(bf16[256,1536]{1,0:T(8,128)(2,1)S(1)} %get-tuple-element.44), channel_id=1, source_target_pairs={{0,1},{1,4},{4,5},{5,0},{2,3},{3,6},{6,7},{7,2},{8,9},{9,12},{12,1... | collective-permute-start | bytes 2359304 | tf_op jit(solution)/shard_map/ppermute | solution.py:40
  329.8 37.3 %collective-permute-start.5 = (bf16[256,1536]{1,0:T(8,128)(2,1)S(1)}, bf16[256,1536]{1,0:T(8,128)(2,1)S(1)}, u32[]{:S(2)}, u32[]{:S(2)}) collective-permute-start(bf16[256,1536]{1,0:T(8,128)(2,1)S(1)} %get-tuple-element.43), channel_id=1, source_target_pairs={{0,5},{1,0},{4,1},{5,4},{2,7},{3,2},{6,3},{7,6},{8,13},{9,8},{12,9... | collective-permute-start | bytes 2359304 | tf_op jit(solution)/shard_map/ppermute | solution.py:41
  331.4 4.9 %copy-start.2 = (f32[2,1536,128]{2,1,0:T(8,128)S(1)}, f32[2,1536,128]{2,1,0:T(8,128)}, u32[]{:S(2)}) copy-start(f32[2,1536,128]{2,1,0:T(8,128)} %param.15) | copy-start | bytes 4718596
  331.4 4.9 %copy-start.3 = (f32[2,1536,128]{2,1,0:T(8,128)S(1)}, f32[2,1536,128]{2,1,0:T(8,128)}, u32[]{:S(2)}) copy-start(f32[2,1536,128]{2,1,0:T(8,128)} %param.18) | copy-start | bytes 4718596
  331.5 4.9 %copy-start.4 = (f32[2,1536,128]{2,1,0:T(8,128)S(1)}, f32[2,1536,128]{2,1,0:T(8,128)}, u32[]{:S(2)}) copy-start(f32[2,1536,128]{2,1,0:T(8,128)} %param.21) | copy-start | bytes 4718596
  333.0 24.8 %collective-permute-start.2 = (bf16[1,118,1536]{2,1,0:T(8,128)(2,1)S(1)}, bf16[1,118,1536]{2,1,0:T(8,128)(2,1)S(1)}, u32[]{:S(2)}, u32[]{:S(2)}) collective-permute-start(bf16[1,118,1536]{2,1,0:T(8,128)(2,1)S(1)} %get-tuple-element.52), channel_id=1, source_target_pairs={{0,1},{1,4},{4,5},{5,0},{2,3},{3,6},{6,7},{7,2},{8,9},{9,12},{12,1... | collective-permute-start | bytes 1087496 | tf_op jit(solution)/shard_map/ppermute | solution.py:40
  333.5 25.8 %collective-permute-start.3 = (bf16[1,118,1536]{2,1,0:T(8,128)(2,1)S(1)}, bf16[1,118,1536]{2,1,0:T(8,128)(2,1)S(1)}, u32[]{:S(2)}, u32[]{:S(2)}) collective-permute-start(bf16[1,118,1536]{2,1,0:T(8,128)(2,1)S(1)} %get-tuple-element.51), channel_id=1, source_target_pairs={{0,5},{1,0},{4,1},{5,4},{2,7},{3,2},{6,3},{7,6},{8,13},{9,8},{12,9... | collective-permute-start | bytes 1087496 | tf_op jit(solution)/shard_map/ppermute | solution.py:41
  339.4 24.8 %collective-permute-start = (bf16[1,1536,128]{2,1,0:T(8,128)(2,1)S(1)}, bf16[1,1536,128]{2,1,0:T(8,128)(2,1)S(1)}, u32[]{:S(2)}, u32[]{:S(2)}) collective-permute-start(bf16[1,1536,128]{2,1,0:T(8,128)(2,1)S(1)} %get-tuple-element.50), channel_id=1, source_target_pairs={{0,1},{1,4},{4,5},{5,0},{2,3},{3,6},{6,7},{7,2},{8,9},{9,12},{12,1... | collective-permute-start | bytes 1179656 | tf_op jit(solution)/shard_map/ppermute | solution.py:40
  357.8 7.8 %collective-permute-start.1 = (bf16[1,1536,128]{2,1,0:T(8,128)(2,1)S(1)}, bf16[1,1536,128]{2,1,0:T(8,128)(2,1)S(1)}, u32[]{:S(2)}, u32[]{:S(2)}) collective-permute-start(bf16[1,1536,128]{2,1,0:T(8,128)(2,1)S(1)} %get-tuple-element.49), channel_id=1, source_target_pairs={{0,5},{1,0},{4,1},{5,4},{2,7},{3,2},{6,3},{7,6},{8,13},{9,8},{12,9... | collective-permute-start | bytes 1179656 | tf_op jit(solution)/shard_map/ppermute | solution.py:41
Sparse Core Ops, SparseCore 0:
  17.6 14.0 reduce-scatter.15
  34.7 13.1 reduce-scatter.9
  50.8 15.0 reduce-scatter.21
  68.3 23.8 reduce-scatter.17
  94.5 22.1 reduce-scatter.11
  119.2 25.3 reduce-scatter.23
  147.7 20.5 reduce-scatter.19
  171.2 20.5 reduce-scatter.13
  195.0 22.1 reduce-scatter.25
  261.7 10.4 all-gather.1

commit v3 on v2

--- a/solution.py
+++ b/solution.py
@@ -24,14 +24,27 @@
     return (new_weight, new_moment, new_second)
 
 
-def reduce_block(buf):
-    part = lax.psum_scatter(buf.astype(jnp.bfloat16), "core", scatter_dimension=0, tiled=True)
-    part = lax.psum_scatter(part, XRING, scatter_dimension=1, tiled=True)
-    part = lax.psum_scatter(part.astype(jnp.float32), "y", scatter_dimension=2, tiled=True)
+def reduce_flat(buf):
+    part = lax.psum_scatter(buf.astype(jnp.bfloat16), "core", scatter_dimension=0, tiled=False)
+    part = lax.psum_scatter(part, XRING, scatter_dimension=0, tiled=False)
+    part = lax.psum_scatter(part.astype(jnp.float32), "y", scatter_dimension=0, tiled=False)
     part = lax.psum(part, "z").astype(jnp.bfloat16)
-    part = lax.all_gather(part, "y", axis=2, tiled=True)
-    part = lax.all_gather(part, "xh", axis=1, tiled=True)
-    return lax.all_gather(part, "core", axis=0, tiled=True)
+    part = lax.all_gather(part, "y", axis=0)
+    part = lax.all_gather(part, "xh", axis=0)
+    return lax.all_gather(part, "core", axis=0)
+
+
+def to_tiles(a):
+    *lead, r, c = a.shape
+    a = a.reshape(*lead, r // 8, 8, c // 128, 128)
+    n = len(lead)
+    return jnp.swapaxes(a, n + 1, n + 2)
+
+
+def from_tiles(t, r, c):
+    *lead, _, _, _, _ = t.shape
+    n = len(lead)
+    return jnp.swapaxes(t, n + 1, n + 2).reshape(*lead, r, c)
 
 
 def swap_halves(own, split_axis):
@@ -73,29 +86,41 @@
     rows_e, width = grad_embed.shape[1:]
     half = inner // n_s
 
-    sx = jnp.sum(grad_xproj, axis=0, dtype=jnp.float32)
-    sx = sx.reshape(layers, n_s, n_xh, n_y, half // (n_xh * n_y), xw)
-    sx = jnp.transpose(sx, (0, 2, 1, 3, 4, 5)).reshape(layers, n_xh * n_s, n_y, half // (n_xh * n_y), xw)
+    n_x = n_xh * n_s
+    cut = n_core * n_xh * n_y
+    sx = to_tiles(jnp.sum(grad_xproj, axis=0, dtype=jnp.float32))
+    tx = sx.reshape(layers, n_s, inner // (8 * n_s), 8, 128)
+    tx = jnp.transpose(tx, (1, 0, 2, 3, 4)).reshape(n_s, -1, 8, 128)
 
-    se = jnp.sum(grad_embed, axis=0, dtype=jnp.float32)
-    re = rows_e // (n_s * n_core * n_xh * n_y)
-    se = se.reshape(n_s, n_core, n_xh, n_y, re, width)
-    se = jnp.transpose(se, (1, 2, 0, 3, 4, 5)).reshape(n_core, n_xh * n_s, n_y, re, width)
+    ch_pad = -(-ch // 8) * 8
+    sc = jnp.sum(grad_chan, axis=0, dtype=jnp.float32)
+    sc = to_tiles(jnp.pad(sc, ((0, 0), (0, ch_pad - ch), (0, 0))))
+    lanes_c = half // 128
+    tc = sc.reshape(layers, ch_pad // 8, n_s, lanes_c, 8, 128)
+    tc = jnp.transpose(tc, (2, 0, 1, 3, 4, 5)).reshape(n_s, -1, 8, 128)
 
-    sc = jnp.sum(grad_chan, axis=0, dtype=jnp.float32)
-    step = n_xh * n_y * 8
-    ch_pad = -(-ch // step) * step
-    sc = jnp.pad(sc, ((0, 0), (0, ch_pad - ch), (0, 0)))
-    rc = ch_pad // (n_xh * n_y)
-    sc = sc.reshape(layers, n_xh, n_y, rc, n_s, half)
-    sc = jnp.transpose(sc, (0, 1, 4, 2, 3, 5)).reshape(layers, n_xh * n_s, n_y, rc, half)
+    se = to_tiles(jnp.sum(grad_embed, axis=0, dtype=jnp.float32))
+    te = se.reshape(n_s, -1, 8, 128)
 
+    counts = (tc.shape[1], tx.shape[1], te.shape[1])
+    used = sum(counts)
+    per = -(-used // cut)
+    pad = jnp.zeros((n_s, per * cut - used, 8, 128), jnp.float32)
+    tiles = jnp.concatenate([tc, tx, te, pad], axis=1)
+    buf = tiles.reshape(n_s, n_core, n_xh, n_y, per, 8, 128)
+    buf = jnp.transpose(buf, (1, 2, 0, 3, 4, 5, 6)).reshape(n_core, n_x, n_y, per, 8, 128)
+
+    mean_t = reduce_flat(buf).reshape(per * cut, 8, 128)
     inverse = 1.0 / total
-    mean_x = reduce_block(sx).reshape(layers, half, xw).astype(jnp.float32) * inverse
-    mean_c = reduce_block(sc).reshape(layers, ch_pad, half)[:, :ch, :].astype(jnp.float32) * inverse
-    mean_e = reduce_block(se).reshape(rows_e // n_s, width).astype(jnp.float32) * inverse
+    mt = mean_t.astype(jnp.float32) * inverse
+    gc = mt[: counts[0]].reshape(layers, ch_pad // 8, lanes_c, 8, 128)
+    mean_c = from_tiles(gc, ch_pad, half)[:, :ch, :]
+    gx = mt[counts[0] : counts[0] + counts[1]].reshape(layers, half // 8, 1, 8, 128)
+    mean_x = from_tiles(gx, half, xw)
+    ge = mt[counts[0] + counts[1] : used].reshape(rows_e // (8 * n_s), width // 128, 8, 128)
+    mean_e = from_tiles(ge, rows_e // n_s, width)
 
-    partial_squares = jnp.sum(mean_x * mean_x) + jnp.sum(mean_c * mean_c) + jnp.sum(mean_e * mean_e)
+    partial_squares = jnp.sum(mt * mt)
     squares = lax.psum(partial_squares, "shard")
     norm_value = jnp.sqrt(squares)
     clip_factor = jnp.minimum(1.0, 1.0 / (norm_value + 1e-06))

time: 378 us -> 297 us (0.79)
  blocking collectives: 94.4 us -> 42.4 us
  waiting for transfers between devices: 196 us -> 147 us
  other arithmetic: 41.2 us -> 61.4 us
    reduce_scatter x9 -> x2, waiting for transfers between devices: 181 us -> 61.4 us  [the longest x1 41.7 us: reduce_flat(): part = lax.psum_scatter(part, XRING, scatter_dimension=0, tiled=False)]
    all_gather x8 -> x1, blocking collectives: 67.2 us -> 15 us  [reduce_flat(): part = lax.all_gather(part, 'y', axis=0)]
    all_gather x1 -> x2, waiting for transfers between devices: 0.02 us -> 44.8 us  [the longest x1 29 us: reduce_flat(): part = lax.all_gather(part, 'xh', axis=0)]
    unnamed x10 -> x6, waiting for transfers between devices: 0.16 us -> 26.2 us
    concatenate x0 -> x1, other arithmetic: none -> 19.7 us  [on_device(): tiles = jnp.concatenate([tc, tx, te, pad], axis=1)]
    reduce_sum x5 -> x3, other arithmetic: 13.8 us -> 15.7 us  [the longest x1 6.66 us: on_device(): partial_squares = jnp.sum(mt * mt)]
    unnamed x23 -> x25, local copies, waits for them, and re-layouts: 10.9 us -> 10.5 us
  transfers between devices with their start and end apart: 16 -> 11, of which waited for: 12 -> 8; matrix products, arithmetic and copies ran while one was open for 9% -> 5% of each run, Pallas kernels for 0% -> 0%
where the time goes in v3:
time: 297 us; the launch traced here: 296 us
  waiting for transfers between devices  147 us (49%)
  other arithmetic  61.4 us (21%)
  blocking collectives  42.4 us (14%)
  local copies, waits for them, and re-layouts  20.6 us (7%)
  between operations  15.9 us (5%)
  starting transfers between devices  8.96 us (3%)
    reduce_scatter x1, waiting for transfers between devices, reduce_flat(): part = lax.psum_scatter(part, XRING, scatter_dimension=0, tiled=False)  41.7 us
    all_gather x1, waiting for transfers between devices, reduce_flat(): part = lax.all_gather(part, 'xh', axis=0)  29 us
    unnamed x6, waiting for transfers between devices  26.2 us
    psum x1, blocking collectives, reduce_flat(): part = lax.psum(part, 'z').astype(jnp.bfloat16)  21.8 us
    concatenate x1, other arithmetic, on_device(): tiles = jnp.concatenate([tc, tx, te, pad], axis=1)  19.7 us
    reduce_scatter x1, waiting for transfers between devices, reduce_flat(): lax.psum_scatter(buf.astype(jnp.bfloat16), 'core', scatter_dimension=0, t...  19.6 us
    all_gather x1, waiting for transfers between devices, reduce_flat(): return lax.all_gather(part, 'core', axis=0)  15.8 us
    all_gather x1, blocking collectives, reduce_flat(): part = lax.all_gather(part, 'y', axis=0)  15 us
  transfers between devices with their start and end apart: 11, of which 8 were waited for; matrix products, arithmetic and copies ran while one was open for 5% of the time, Pallas kernels for 0%

profile of v3, /device:TPU:0, one launch (start us, length us, event | category | flops | bytes accessed | tf_op | source)
XLA Modules:
  0.0 296.2 jit_solution(2719723821293284881)
XLA Ops:
  7.2 0.0 reduce-scatter.6.cloned.1.call-start
  7.2 6.5 %reduce.1 = bf16[2,118,3072]{2,0,1:T(2,128)(2,1)S(1)} reduce(bf16[2,2,118,3072]{3,1,2,0:T(2,128)(2,1)} %param.13, bf16[]{:T(256)} %constant.18.clone.1), dimensions={0}, to_apply=%region_0.0.clone | reduce | flops 724992 | bytes 4349954 | tf_op jit(solution)/shard_map/reduce_sum | solution.py:96
  13.7 1.1 pad.5
  14.9 1.2 reshape.77
  16.0 0.4 copy.44
  16.4 1.2 copy.45
  17.6 2.9 reduce.2
  20.6 1.2 copy.46
  21.8 6.1 %reduce.3 = bf16[1024,1536]{1,0:T(8,128)(2,1)S(1)} reduce(bf16[2,1024,1536]{2,1,0:T(8,128)(2,1)} %param.14, bf16[]{:T(256)} %constant.18.clone.1), dimensions={0}, to_apply=%region_2.3.clone | reduce | flops 1572864 | bytes 9437186 | tf_op jit(solution)/shard_map/reduce_sum | solution.py:102
  27.9 0.1 pad.15.clone
  28.0 19.7 %maximum_maximum_fusion = bf16[2,1520,8,128]{3,2,1,0:T(8,128)(2,1)S(1)} fusion(bf16[2,768,8,128]{3,2,1,0:T(8,128)(2,1)S(1)} %bitcast.53, bf16[2,384,8,128]{3,2,1,0:T(8,128)(2,1)} %bitcast.56, bf16[2,360,8,128]{3,2,1,0:T(8,128)(2,1)} %bitcast.59, bf16[1520]{0:T(1024)(128)(2,1)S(1)} %pad.15.clone), kind=kLoop, calls=%fused_computation | loop fusion | flops 9338880 | bytes 12422112 | tf_op jit(solution)/shard_map/concatenate | solution.py:109
  47.7 3.2 %copy.47 = bf16[2,2,2,4,95,8,128]{6,5,4,3,2,1,0:T(8,128)(2,1)} copy(bf16[2,2,2,4,95,8,128]{6,5,4,3,1,0,2:T(8,128)(2,1)S(1)} %bitcast.49) | data formatting | bytes 12451840 | tf_op jit(solution)/shard_map/convert_element_type | solution.py:28
  50.9 0.0 reduce-scatter.6.cloned.1.call-update
  50.9 0.0 reduce-scatter.8.cloned.1.call-start
  50.9 19.6 %reduce-scatter.6.cloned.1.call-done = bf16[1,4,4,95,8,128]{5,4,3,2,1,0:T(8,128)(2,1)} async-done(((bf16[2,4,4,95,8,128]{5,4,3,2,1,0:T(8,128)(2,1)}), bf16[1,4,4,95,8,128]{5,4,3,2,1,0:T(8,128)(2,1)}) %reduce-scatter.6.cloned.1.call-update) | async-done | bytes 3112976 | tf_op jit(solution)/shard_map/reduce_scatter | solution.py:28
  70.6 0.0 reduce-scatter.8.cloned.1.call-update
  70.6 0.0 reduce-scatter.10.cloned.1.call-start
  70.6 41.7 %reduce-scatter.8.cloned.1.call-done = bf16[1,4,95,8,128]{4,3,2,1,0:T(8,128)(2,1)} async-done(((bf16[4,4,95,8,128]{4,3,2,1,0:T(8,128)(2,1)}), bf16[1,4,95,8,128]{4,3,2,1,0:T(8,128)(2,1)}) %reduce-scatter.8.cloned.1.call-update) | async-done | bytes 778256 | tf_op jit(solution)/shard_map/reduce_scatter | solution.py:29
  112.4 2.4 bitcast_convert_fusion
  114.7 0.0 reduce-scatter.10.cloned.1.call-update
  114.8 0.0 all-gather.6.cloned.1.call-start
  114.8 26.1 %reduce-scatter.10.cloned.1.call-done = f32[1,95,8,128]{3,2,1,0:T(8,128)} async-done(((f32[4,95,8,128]{3,2,1,0:T(8,128)}), f32[1,95,8,128]{3,2,1,0:T(8,128)}) %reduce-scatter.10.cloned.1.call-update) | async-done | bytes 389136
  140.9 21.8 %all-reduce.3 = bf16[95,8,128]{2,1,0:T(8,128)(2,1)S(1)} all-reduce(f32[95,8,128]{2,1,0:T(8,128)} %bitcast.64), channel_id=1, replica_groups=mesh['z'=4,'y'=4,'xh'=2,'core'=2,'shard'=2] {'z'}, use_global_device_ids=true, to_apply=%region_6.7 | all-reduce | flops 97280 | bytes 583680 | tf_op jit(solution)/shard_map/psum | solution.py:31
  162.8 15.0 %all-gather = bf16[380,8,128]{2,1,0:T(8,128)(2,1)} all-gather(bf16[95,8,128]{2,1,0:T(8,128)(2,1)S(1)} %all-reduce.3), channel_id=2, replica_groups=mesh['z'=4,'y'=4,'xh'=2,'core'=2,'shard'=2] {'y'}, dimensions={0}, use_global_device_ids=true | all-gather | bytes 972800 | tf_op jit(solution)/shard_map/all_gather | solution.py:32
  177.8 0.0 all-gather.6.cloned.1.call-update
  177.8 0.3 all-gather.8.cloned.1.call-start
  178.1 29.0 %all-gather.6.cloned.1.call-done = bf16[8,95,8,128]{3,2,1,0:T(8,128)(2,1)} async-done(((bf16[4,95,8,128]{3,2,1,0:T(8,128)(2,1)}), bf16[8,95,8,128]{3,2,1,0:T(8,128)(2,1)}) %all-gather.6.cloned.1.call-update) | async-done | bytes 1556496 | tf_op jit(solution)/shard_map/all_gather | solution.py:33
  207.1 0.0 all-gather.8.cloned.1.call-update
  207.1 15.8 %all-gather.8.cloned.1.call-done = bf16[4,4,95,8,128]{4,3,2,1,0:T(8,128)(2,1)} async-done(((bf16[2,4,95,8,128]{4,3,2,1,0:T(8,128)(2,1)}), bf16[4,4,95,8,128]{4,3,2,1,0:T(8,128)(2,1)}) %all-gather.8.cloned.1.call-update) | async-done | bytes 3112976 | tf_op jit(solution)/shard_map/all_gather | solution.py:34
  222.9 6.7 %multiply_reduce_fusion = (f32[]{:T(128)}, f32[4,4,95,8,128]{4,3,2,1,0:T(8,128)}) fusion(bf16[4,4,95,8,128]{4,3,2,1,0:T(8,128)(2,1)} %all-gather.8.cloned.1.call-done), kind=kLoop, calls=%fused_computation.1 | loop fusion | flops 6225919 | bytes 9338884 | tf_op jit(solution)/shard_map/reduce_sum | solution.py:123
  229.6 5.5 %psum.15 = f32[]{:T(128)} all-reduce(f32[]{:T(128)} %get-tuple-element.66), channel_id=1, replica_groups=mesh['z'=4,'y'=4,'xh'=2,'core'=2,'shard'=2] {'shard'}, use_global_device_ids=true, to_apply=%region_8.9 | all-reduce | flops 1 | bytes 8 | tf_op jit(solution)/shard_map/psum | solution.py:124
  235.9 1.5 slice.17
  237.3 0.0 copy-start.1
  237.4 2.2 slice_multiply_fusion
  239.6 2.0 slice_multiply_fusion.1
  241.7 1.0 copy-done
  242.7 4.6 %fusion.5 = (bf16[512,1536]{1,0:T(8,128)(2,1)S(1)}, f32[512,1536]{1,0:T(8,128)}, f32[512,1536]{1,0:T(8,128)}, f32[512,1536]{1,0:T(8,128)}) fusion(f32[512,1536]{1,0:T(8,128)S(1)} %copy-done, f32[512,1536]{1,0:T(8,128)S(1)} %bitcast.54, f32[512,1536]{1,0:T(8,128)S(1)} %copy-done.1, f32[512,1536]{1,0:T(8,128)S(1)} %copy-done.2), kind=kLoop, calls=%fused_computation.37 | loop fusion | flops 12582912 | bytes 23592960 | tf_op jit(solution)/shard_map/convert_element_type | solution.py:132
  247.3 0.1 fusion.13
  247.4 1.6 collective-permute-start.4
  249.1 1.7 collective-permute-start.5
  250.8 1.5 fusion.7
  252.2 0.1 fusion.15
  252.3 0.4 collective-permute-start.2
  252.7 2.9 collective-permute-start.3
  255.6 3.0 %fusion.10 = (bf16[2,1536,128]{2,1,0:T(8,128)(2,1)S(1)}, f32[2,1536,128]{2,1,0:T(8,128)}, f32[2,1536,128]{2,1,0:T(8,128)}, f32[2,1536,128]{2,1,0:T(8,128)}) fusion(f32[2,1536,128]{2,1,0:T(8,128)S(1)} %copy-done.3, f32[2,1536,128]{2,1,0:T(8,128)S(1)} %copy-done.4, f32[2,1536,128]{2,1,0:T(8,128)S(1)} %copy-done.5, f32[2,1536,128]{2,1,0:T(8,128)S(1)} %bitcast.57), kind=kLoop, calls=%fused_computation.39 | loop fusion | flops 6291456 | bytes 11796480 | tf_op jit(solution)/shard_map/convert_element_type | solution.py:130
  258.6 0.1 fusion.14
  258.7 0.3 collective-permute-start
  259.0 2.2 copy.52
  261.2 2.2 copy.53
  263.5 2.2 copy.54
  265.7 11.4 %collective-permute-done.2 = bf16[1,118,1536]{2,1,0:T(8,128)(2,1)S(1)} collective-permute-done((bf16[1,118,1536]{2,1,0:T(8,128)(2,1)S(1)}, bf16[1,118,1536]{2,1,0:T(8,128)(2,1)S(1)}, u32[]{:S(2)}, u32[]{:S(2)}) %collective-permute-start.2) | collective-permute-done | bytes 362528 | tf_op jit(solution)/shard_map/ppermute | solution.py:53
  277.1 1.6 collective-permute-start.1
  278.7 0.1 broadcast_select_fusion.5
  278.8 0.2 pad_maximum_fusion.2
  279.0 2.6 copy.55
  281.6 2.0 collective-permute-done
  283.6 1.2 collective-permute-done.1
  284.8 0.1 constant_dynamic-update-slice_fusion
  284.9 0.2 broadcast_select_fusion.3
  285.1 1.2 pad_maximum_fusion.1
  286.3 0.1 constant_dynamic-update-slice_fusion.5
  286.4 0.1 constant_dynamic-update-slice_fusion.4
  286.5 0.2 broadcast_select_fusion.1
  286.7 1.9 pad_maximum_fusion
  (23 shorter events, 0.1 us)
Async XLA Ops:
  7.2 63.4 %reduce-scatter.6.cloned.1.call-start = ((), (), s32[]{:S(2)}) async-start(), calls=%async_computation.3 | async-start | bytes 9338880 | tf_op jit(solution)/shard_map/reduce_scatter | solution.py:28
  50.9 61.5 %reduce-scatter.8.cloned.1.call-start = ((), (), s32[]{:S(2)}) async-start(), calls=%async_computation.4 | async-start | bytes 3891200 | tf_op jit(solution)/shard_map/reduce_scatter | solution.py:29
  70.6 70.3 %reduce-scatter.10.cloned.1.call-start = ((), (), s32[]{:S(2)}) async-start(), calls=%async_computation.7 | async-start | bytes 1945600
  114.8 92.3 %all-gather.6.cloned.1.call-start = ((), (), s32[]{:S(2)}) async-start(), calls=%async_computation.5 | async-start | bytes 2334720 | tf_op jit(solution)/shard_map/all_gather | solution.py:33
  177.8 45.1 %all-gather.8.cloned.1.call-start = ((), (), s32[]{:S(2)}) async-start(), calls=%async_computation.6 | async-start | bytes 4669440 | tf_op jit(solution)/shard_map/all_gather | solution.py:34
  237.3 4.3 %copy-start.1 = (f32[512,1536]{1,0:T(8,128)S(1)}, f32[512,1536]{1,0:T(8,128)}, u32[]{:S(2)}) copy-start(f32[512,1536]{1,0:T(8,128)} %param.20) | copy-start | bytes 9437188
  237.4 4.3 %copy-start.2 = (f32[512,1536]{1,0:T(8,128)S(1)}, f32[512,1536]{1,0:T(8,128)}, u32[]{:S(2)}) copy-start(f32[512,1536]{1,0:T(8,128)} %param.23) | copy-start | bytes 9437188
  239.6 3.1 %copy-start = (f32[512,1536]{1,0:T(8,128)S(1)}, f32[512,1536]{1,0:T(8,128)}, u32[]{:S(2)}) copy-start(f32[512,1536]{1,0:T(8,128)} %param.17) | copy-start | bytes 9437188
  242.7 8.0 %copy-start.8 = (f32[2,118,1536]{2,0,1:T(2,128)S(1)}, f32[2,118,1536]{2,0,1:T(2,128)}, u32[]{:S(2)}) copy-start(f32[2,118,1536]{2,0,1:T(2,128)} %param.22) | copy-start | bytes 4349956
  247.3 3.4 %copy-start.6 = (f32[2,118,1536]{2,0,1:T(2,128)S(1)}, f32[2,118,1536]{2,0,1:T(2,128)}, u32[]{:S(2)}) copy-start(f32[2,118,1536]{2,0,1:T(2,128)} %param.16) | copy-start | bytes 4349956
  247.3 3.4 %copy-start.7 = (f32[2,118,1536]{2,0,1:T(2,128)S(1)}, f32[2,118,1536]{2,0,1:T(2,128)}, u32[]{:S(2)}) copy-start(f32[2,118,1536]{2,0,1:T(2,128)} %param.19) | copy-start | bytes 4349956
  247.4 38.9 %collective-permute-start.4 = (bf16[256,1536]{1,0:T(8,128)(2,1)S(1)}, bf16[256,1536]{1,0:T(8,128)(2,1)S(1)}, u32[]{:S(2)}, u32[]{:S(2)}) collective-permute-start(bf16[256,1536]{1,0:T(8,128)(2,1)S(1)} %get-tuple-element.69), channel_id=1, source_target_pairs={{0,1},{1,4},{4,5},{5,0},{2,3},{3,6},{6,7},{7,2},{8,9},{9,12},{12,1... | collective-permute-start | bytes 2359304 | tf_op jit(solution)/shard_map/ppermute | solution.py:53
  249.1 37.4 %collective-permute-start.5 = (bf16[256,1536]{1,0:T(8,128)(2,1)S(1)}, bf16[256,1536]{1,0:T(8,128)(2,1)S(1)}, u32[]{:S(2)}, u32[]{:S(2)}) collective-permute-start(bf16[256,1536]{1,0:T(8,128)(2,1)S(1)} %get-tuple-element.68), channel_id=1, source_target_pairs={{0,5},{1,0},{4,1},{5,4},{2,7},{3,2},{6,3},{7,6},{8,13},{9,8},{12,9... | collective-permute-start | bytes 2359304 | tf_op jit(solution)/shard_map/ppermute | solution.py:54
  250.7 4.9 %copy-start.3 = (f32[2,1536,128]{2,1,0:T(8,128)S(1)}, f32[2,1536,128]{2,1,0:T(8,128)}, u32[]{:S(2)}) copy-start(f32[2,1536,128]{2,1,0:T(8,128)} %param.15) | copy-start | bytes 4718596
  250.7 4.9 %copy-start.4 = (f32[2,1536,128]{2,1,0:T(8,128)S(1)}, f32[2,1536,128]{2,1,0:T(8,128)}, u32[]{:S(2)}) copy-start(f32[2,1536,128]{2,1,0:T(8,128)} %param.18) | copy-start | bytes 4718596
  250.7 4.9 %copy-start.5 = (f32[2,1536,128]{2,1,0:T(8,128)S(1)}, f32[2,1536,128]{2,1,0:T(8,128)}, u32[]{:S(2)}) copy-start(f32[2,1536,128]{2,1,0:T(8,128)} %param.21) | copy-start | bytes 4718596
  252.3 24.8 %collective-permute-start.2 = (bf16[1,118,1536]{2,1,0:T(8,128)(2,1)S(1)}, bf16[1,118,1536]{2,1,0:T(8,128)(2,1)S(1)}, u32[]{:S(2)}, u32[]{:S(2)}) collective-permute-start(bf16[1,118,1536]{2,1,0:T(8,128)(2,1)S(1)} %get-tuple-element.77), channel_id=1, source_target_pairs={{0,1},{1,4},{4,5},{5,0},{2,3},{3,6},{6,7},{7,2},{8,9},{9,12},{12,1... | collective-permute-start | bytes 1087496 | tf_op jit(solution)/shard_map/ppermute | solution.py:53
  252.7 26.0 %collective-permute-start.3 = (bf16[1,118,1536]{2,1,0:T(8,128)(2,1)S(1)}, bf16[1,118,1536]{2,1,0:T(8,128)(2,1)S(1)}, u32[]{:S(2)}, u32[]{:S(2)}) collective-permute-start(bf16[1,118,1536]{2,1,0:T(8,128)(2,1)S(1)} %get-tuple-element.76), channel_id=1, source_target_pairs={{0,5},{1,0},{4,1},{5,4},{2,7},{3,2},{6,3},{7,6},{8,13},{9,8},{12,9... | collective-permute-start | bytes 1087496 | tf_op jit(solution)/shard_map/ppermute | solution.py:54
  258.7 24.9 %collective-permute-start = (bf16[1,1536,128]{2,1,0:T(8,128)(2,1)S(1)}, bf16[1,1536,128]{2,1,0:T(8,128)(2,1)S(1)}, u32[]{:S(2)}, u32[]{:S(2)}) collective-permute-start(bf16[1,1536,128]{2,1,0:T(8,128)(2,1)S(1)} %get-tuple-element.75), channel_id=1, source_target_pairs={{0,1},{1,4},{4,5},{5,0},{2,3},{3,6},{6,7},{7,2},{8,9},{9,12},{12,1... | collective-permute-start | bytes 1179656 | tf_op jit(solution)/shard_map/ppermute | solution.py:53
  277.1 7.8 %collective-permute-start.1 = (bf16[1,1536,128]{2,1,0:T(8,128)(2,1)S(1)}, bf16[1,1536,128]{2,1,0:T(8,128)(2,1)S(1)}, u32[]{:S(2)}, u32[]{:S(2)}) collective-permute-start(bf16[1,1536,128]{2,1,0:T(8,128)(2,1)S(1)} %get-tuple-element.74), channel_id=1, source_target_pairs={{0,5},{1,0},{4,1},{5,4},{2,7},{3,2},{6,3},{7,6},{8,13},{9,8},{12,9... | collective-permute-start | bytes 1179656 | tf_op jit(solution)/shard_map/ppermute | solution.py:54
Sparse Core Ops, SparseCore 0:
  51.0 19.4 reduce-scatter.5
  73.0 39.3 reduce-scatter.7
  115.5 25.3 reduce-scatter.9
  177.9 29.1 all-gather.5
  208.7 14.1 all-gather.7

commit v4 on v3

--- a/solution.py
+++ b/solution.py
@@ -32,6 +32,14 @@
     part = lax.all_gather(part, "y", axis=0)
     part = lax.all_gather(part, "xh", axis=0)
     return lax.all_gather(part, "core", axis=0)
+
+
+def reduce_staged(buf):
+    part = lax.psum_scatter(buf.astype(jnp.bfloat16), "core", scatter_dimension=0, tiled=False)
+    part = lax.psum_scatter(part, XRING, scatter_dimension=0, tiled=False)
+    part = lax.psum_scatter(part.astype(jnp.float32), "y", scatter_dimension=0, tiled=False)
+    part = lax.psum_scatter(part, "z", scatter_dimension=0, tiled=False)
+    return lax.all_gather(part.astype(jnp.bfloat16), AXES[:-1], axis=0)
 
 
 def to_tiles(a):
@@ -87,7 +95,8 @@
     half = inner // n_s
 
     n_x = n_xh * n_s
-    cut = n_core * n_xh * n_y
+    n_rep = lax.axis_size(AXES[:-1])
+    cut = n_rep
     sx = to_tiles(jnp.sum(grad_xproj, axis=0, dtype=jnp.float32))
     tx = sx.reshape(layers, n_s, inner // (8 * n_s), 8, 128)
     tx = jnp.transpose(tx, (1, 0, 2, 3, 4)).reshape(n_s, -1, 8, 128)
@@ -107,10 +116,11 @@
     per = -(-used // cut)
     pad = jnp.zeros((n_s, per * cut - used, 8, 128), jnp.float32)
     tiles = jnp.concatenate([tc, tx, te, pad], axis=1)
-    buf = tiles.reshape(n_s, n_core, n_xh, n_y, per, 8, 128)
-    buf = jnp.transpose(buf, (1, 2, 0, 3, 4, 5, 6)).reshape(n_core, n_x, n_y, per, 8, 128)
+    n_z = lax.axis_size("z")
+    buf = tiles.reshape(n_s, n_z, n_y, n_xh, n_core, per, 8, 128)
+    buf = jnp.transpose(buf, (4, 3, 0, 2, 1, 5, 6, 7)).reshape(n_core, n_x, n_y, n_z, per, 8, 128)
 
-    mean_t = reduce_flat(buf).reshape(per * cut, 8, 128)
+    mean_t = reduce_staged(buf).reshape(per * cut, 8, 128)
     inverse = 1.0 / total
     mt = mean_t.astype(jnp.float32) * inverse
     gc = mt[: counts[0]].reshape(layers, ch_pad // 8, lanes_c, 8, 128)

time: 297 us -> 311 us (1.047)
  waiting for transfers between devices: 147 us -> 198 us
  blocking collectives: 42.4 us -> 5.55 us
    reduce_scatter x2 -> x4, waiting for transfers between devices: 61.4 us -> 111 us  [the longest x1 42.1 us: reduce_staged(): part = lax.psum_scatter(part, XRING, scatter_dimension=0, tiled=False)]
    all_gather x2 -> x1, waiting for transfers between devices: 44.8 us -> 71.2 us  [reduce_staged(): return lax.all_gather(part.astype(jnp.bfloat16), AXES[:-1], axis=0)]
    unnamed x6 -> x5, waiting for transfers between devices: 26.2 us -> 0.08 us
    psum x1 -> x0, blocking collectives: 21.8 us -> none  [reduce_flat(): part = lax.psum(part, 'z').astype(jnp.bfloat16)]
    all_gather x1 -> x0, blocking collectives: 15 us -> none  [reduce_flat(): part = lax.all_gather(part, 'y', axis=0)]
where the time goes in v4:
time: 311 us
  waiting for transfers between devices  198 us (64%)
  other arithmetic  63.2 us (20%)
  local copies, waits for them, and re-layouts  20.5 us (7%)
  between operations  15.9 us (5%)
  starting transfers between devices  7.36 us (2%)
  blocking collectives  5.55 us (2%)
    all_gather x1, waiting for transfers between devices, reduce_staged(): return lax.all_gather(part.astype(jnp.bfloat16), AXES[:-1], axis=0)  71.2 us
    reduce_scatter x1, waiting for transfers between devices, reduce_staged(): part = lax.psum_scatter(part, XRING, scatter_dimension=0, tiled=False)  42.1 us
    reduce_scatter x1, waiting for transfers between devices, reduce_staged(): lax.psum_scatter(part.astype(jnp.float32), 'y', scatter_dimension=0, tile...  26.1 us
    reduce_scatter x1, waiting for transfers between devices, reduce_staged(): part = lax.psum_scatter(part, 'z', scatter_dimension=0, tiled=False)  23 us
    concatenate x1, other arithmetic, on_device(): tiles = jnp.concatenate([tc, tx, te, pad], axis=1)  19.8 us
    reduce_scatter x1, waiting for transfers between devices, reduce_staged(): lax.psum_scatter(buf.astype(jnp.bfloat16), 'core', scatter_dimension=0, t...  19.7 us
    ppermute x3, waiting for transfers between devices, swap_halves(): lax.ppermute(first, XRING, perm=[(p, (p + 1) % n) for p in range(n)])  15 us
    unnamed x25, local copies, waits for them, and re-layouts  10.4 us
  transfers between devices with their start and end apart: 11, of which 8 were waited for; matrix products, arithmetic and copies ran while one was open for 5% of the time, Pallas kernels for 0%

profile of v4, /device:TPU:0, one launch (start us, length us, event | category | flops | bytes accessed | tf_op | source)
XLA Modules:
  0.0 310.9 jit_solution(2396413224249320493)
XLA Ops:
  7.2 0.0 reduce-scatter.5.cloned.1.call-start
  7.2 6.5 %reduce.1 = bf16[2,118,3072]{2,0,1:T(2,128)(2,1)S(1)} reduce(bf16[2,2,118,3072]{3,1,2,0:T(2,128)(2,1)} %param.13, bf16[]{:T(256)} %constant.18.clone.1), dimensions={0}, to_apply=%region_0.0.clone | reduce | flops 724992 | bytes 4349954 | tf_op jit(solution)/shard_map/reduce_sum | solution.py:105
  13.7 1.1 pad.5
  14.9 1.2 reshape.85
  16.0 0.4 copy.44
  16.4 1.2 copy.45
  17.6 2.9 reduce.2
  20.6 1.2 copy.46
  21.8 6.1 %reduce.3 = bf16[1024,1536]{1,0:T(8,128)(2,1)S(1)} reduce(bf16[2,1024,1536]{2,1,0:T(8,128)(2,1)} %param.14, bf16[]{:T(256)} %constant.18.clone.1), dimensions={0}, to_apply=%region_2.3.clone | reduce | flops 1572864 | bytes 9437186 | tf_op jit(solution)/shard_map/reduce_sum | solution.py:111
  27.9 0.1 pad.15.clone
  28.0 19.8 %maximum_maximum_fusion = bf16[2,1536,8,128]{3,2,1,0:T(8,128)(2,1)S(1)} fusion(bf16[2,768,8,128]{3,2,1,0:T(8,128)(2,1)S(1)} %bitcast.40, bf16[2,384,8,128]{3,2,1,0:T(8,128)(2,1)} %bitcast.43, bf16[2,360,8,128]{3,2,1,0:T(8,128)(2,1)} %bitcast.46, bf16[1536]{0:T(1024)(128)(2,1)S(1)} %pad.15.clone), kind=kLoop, calls=%fused_computation | loop fusion | flops 9437184 | bytes 12487680 | tf_op jit(solution)/shard_map/concatenate | solution.py:118
  47.8 3.1 copy.47
  50.9 0.0 reduce-scatter.5.cloned.1.call-update
  50.9 0.0 reduce-scatter.7.cloned.1.call-start
  51.0 19.7 %reduce-scatter.5.cloned.1.call-done = bf16[1,4,4,4,24,8,128]{6,5,4,3,2,1,0:T(8,128)(2,1)} async-done(((bf16[2,4,4,4,24,8,128]{6,5,4,3,2,1,0:T(8,128)(2,1)}), bf16[1,4,4,4,24,8,128]{6,5,4,3,2,1,0:T(8,128)(2,1)}) %reduce-scatter.5.cloned.1.call-update) | async-done | bytes 3145744 | tf_op jit(solution)/shard_map/reduce_scatter | solution.py:38
  70.6 0.0 reduce-scatter.7.cloned.1.call-update
  70.7 0.0 reduce-scatter.9.cloned.1.call-start
  70.7 42.1 %reduce-scatter.7.cloned.1.call-done = bf16[1,4,4,24,8,128]{5,4,3,2,1,0:T(8,128)(2,1)} async-done(((bf16[4,4,4,24,8,128]{5,4,3,2,1,0:T(8,128)(2,1)}), bf16[1,4,4,24,8,128]{5,4,3,2,1,0:T(8,128)(2,1)}) %reduce-scatter.7.cloned.1.call-update) | async-done | bytes 786448 | tf_op jit(solution)/shard_map/reduce_scatter | solution.py:39
  112.9 2.4 bitcast_convert_fusion
  115.3 0.0 reduce-scatter.9.cloned.1.call-update
  115.3 0.0 reduce-scatter.11.cloned.1.call-start
  115.4 26.1 %reduce-scatter.9.cloned.1.call-done = f32[1,4,24,8,128]{4,3,2,1,0:T(8,128)} async-done(((f32[4,4,24,8,128]{4,3,2,1,0:T(8,128)}), f32[1,4,24,8,128]{4,3,2,1,0:T(8,128)}) %reduce-scatter.9.cloned.1.call-update) | async-done | bytes 393232 | tf_op jit(solution)/shard_map/reduce_scatter | solution.py:40
  141.5 0.0 reduce-scatter.11.cloned.1.call-update
  141.5 0.3 all-gather.2.cloned.1.call-start
  141.8 23.0 %reduce-scatter.11.cloned.1.call-done = f32[1,24,8,128]{3,2,1,0:T(8,128)} async-done(((f32[4,24,8,128]{3,2,1,0:T(8,128)}), f32[1,24,8,128]{3,2,1,0:T(8,128)}) %reduce-scatter.11.cloned.1.call-update) | async-done | bytes 98320 | tf_op jit(solution)/shard_map/reduce_scatter | solution.py:41
  164.8 1.5 convert_element_type.53
  166.3 0.0 all-gather.2.cloned.1.call-update
  166.4 71.2 %all-gather.2.cloned.1.call-done = bf16[64,24,8,128]{3,2,1,0:T(8,128)(2,1)} async-done(((bf16[1,24,8,128]{3,2,1,0:T(8,128)(2,1)}), bf16[64,24,8,128]{3,2,1,0:T(8,128)(2,1)}) %all-gather.2.cloned.1.call-update) | async-done | bytes 3145744 | tf_op jit(solution)/shard_map/all_gather | solution.py:42
  237.5 6.7 %multiply_reduce_fusion = (f32[]{:T(128)}, f32[64,24,8,128]{3,2,1,0:T(8,128)}) fusion(bf16[64,24,8,128]{3,2,1,0:T(8,128)(2,1)} %all-gather.2.cloned.1.call-done), kind=kLoop, calls=%fused_computation.1 | loop fusion | flops 6291455 | bytes 9437188 | tf_op jit(solution)/shard_map/reduce_sum | solution.py:133
  244.3 5.5 %psum.7 = f32[]{:T(128)} all-reduce(f32[]{:T(128)} %get-tuple-element.66), channel_id=1, replica_groups=mesh['z'=4,'y'=4,'xh'=2,'core'=2,'shard'=2] {'shard'}, use_global_device_ids=true, to_apply=%region_8.9 | all-reduce | flops 1 | bytes 8 | tf_op jit(solution)/shard_map/psum | solution.py:134
  250.6 1.5 slice.20
  252.0 0.0 copy-start.1
  252.0 0.0 copy-start.2
  252.1 2.2 slice_multiply_fusion
  254.3 2.1 slice_multiply_fusion.1
  256.4 1.0 copy-done
  257.4 4.6 %fusion.4 = (bf16[512,1536]{1,0:T(8,128)(2,1)S(1)}, f32[512,1536]{1,0:T(8,128)}, f32[512,1536]{1,0:T(8,128)}, f32[512,1536]{1,0:T(8,128)}) fusion(f32[512,1536]{1,0:T(8,128)S(1)} %copy-done, f32[512,1536]{1,0:T(8,128)S(1)} %bitcast.41, f32[512,1536]{1,0:T(8,128)S(1)} %copy-done.1, f32[512,1536]{1,0:T(8,128)S(1)} %copy-done.2), kind=kLoop, calls=%fused_computation.36 | loop fusion | flops 12582912 | bytes 23592960 | tf_op jit(solution)/shard_map/convert_element_type | solution.py:142
  262.0 0.1 fusion.11
  262.1 0.6 collective-permute-start.4
  262.7 2.7 collective-permute-start.5
  265.4 0.0 copy-start.4
  265.4 1.5 fusion.6
  266.9 0.1 fusion.13
  267.0 0.1 collective-permute-start.2
  267.1 3.2 %collective-permute-start.3 = (bf16[1,118,1536]{2,1,0:T(8,128)(2,1)S(1)}, bf16[1,118,1536]{2,1,0:T(8,128)(2,1)S(1)}, u32[]{:S(2)}, u32[]{:S(2)}) collective-permute-start(bf16[1,118,1536]{2,1,0:T(8,128)(2,1)S(1)} %get-tuple-element.76), channel_id=1, source_target_pairs={{0,5},{1,0},{4,1},{5,4},{2,7},{3,2},{6,3},{7,6},{8,13},{9,8},{12,9... | collective-permute-start | bytes 1087496 | tf_op jit(solution)/shard_map/ppermute | solution.py:62
  270.3 3.0 fusion.9
  273.3 0.1 fusion.12
  273.4 0.3 collective-permute-start
  273.7 2.2 copy.52
  275.9 2.2 copy.53
  278.1 2.2 copy.54
  280.4 11.4 %collective-permute-done.2 = bf16[1,118,1536]{2,1,0:T(8,128)(2,1)S(1)} collective-permute-done((bf16[1,118,1536]{2,1,0:T(8,128)(2,1)S(1)}, bf16[1,118,1536]{2,1,0:T(8,128)(2,1)S(1)}, u32[]{:S(2)}, u32[]{:S(2)}) %collective-permute-start.2) | collective-permute-done | bytes 362528 | tf_op jit(solution)/shard_map/ppermute | solution.py:61
  291.8 0.1 broadcast_select_fusion.5
  291.9 0.2 pad_maximum_fusion.2
  292.1 2.6 copy.55
  294.7 3.6 %collective-permute-done = bf16[1,1536,128]{2,1,0:T(8,128)(2,1)S(1)} collective-permute-done((bf16[1,1536,128]{2,1,0:T(8,128)(2,1)S(1)}, bf16[1,1536,128]{2,1,0:T(8,128)(2,1)S(1)}, u32[]{:S(2)}, u32[]{:S(2)}) %collective-permute-start) | collective-permute-done | bytes 393248 | tf_op jit(solution)/shard_map/ppermute | solution.py:61
  298.3 1.2 collective-permute-done.1
  299.5 0.1 constant_dynamic-update-slice_fusion
  299.6 0.2 broadcast_select_fusion.3
  299.8 1.2 pad_maximum_fusion.1
  301.0 0.1 constant_dynamic-update-slice_fusion.5
  301.1 0.1 constant_dynamic-update-slice_fusion.4
  301.2 0.2 broadcast_select_fusion.1
  301.4 1.9 pad_maximum_fusion
  (22 shorter events, 0.1 us)
Async XLA Ops:
  7.2 63.5 %reduce-scatter.5.cloned.1.call-start = ((), (), s32[]{:S(2)}) async-start(), calls=%async_computation.4 | async-start | bytes 9437184 | tf_op jit(solution)/shard_map/reduce_scatter | solution.py:38
  50.9 61.9 %reduce-scatter.7.cloned.1.call-start = ((), (), s32[]{:S(2)}) async-start(), calls=%async_computation.5 | async-start | bytes 3932160 | tf_op jit(solution)/shard_map/reduce_scatter | solution.py:39
  70.7 70.8 %reduce-scatter.9.cloned.1.call-start = ((), (), s32[]{:S(2)}) async-start(), calls=%async_computation.6 | async-start | bytes 1966080 | tf_op jit(solution)/shard_map/reduce_scatter | solution.py:40
  115.3 49.5 %reduce-scatter.11.cloned.1.call-start = ((), (), s32[]{:S(2)}) async-start(), calls=%async_computation.7 | async-start | bytes 491520 | tf_op jit(solution)/shard_map/reduce_scatter | solution.py:41
  141.5 96.0 %all-gather.2.cloned.1.call-start = ((), (), s32[]{:S(2)}) async-start(), calls=%async_computation.8 | async-start | bytes 3194880 | tf_op jit(solution)/shard_map/all_gather | solution.py:42
  252.0 4.4 %copy-start.1 = (f32[512,1536]{1,0:T(8,128)S(1)}, f32[512,1536]{1,0:T(8,128)}, u32[]{:S(2)}) copy-start(f32[512,1536]{1,0:T(8,128)} %param.20) | copy-start | bytes 9437188
  252.0 4.4 %copy-start.2 = (f32[512,1536]{1,0:T(8,128)S(1)}, f32[512,1536]{1,0:T(8,128)}, u32[]{:S(2)}) copy-start(f32[512,1536]{1,0:T(8,128)} %param.23) | copy-start | bytes 9437188
  254.3 3.1 %copy-start = (f32[512,1536]{1,0:T(8,128)S(1)}, f32[512,1536]{1,0:T(8,128)}, u32[]{:S(2)}) copy-start(f32[512,1536]{1,0:T(8,128)} %param.17) | copy-start | bytes 9437188
  257.4 8.0 %copy-start.8 = (f32[2,118,1536]{2,0,1:T(2,128)S(1)}, f32[2,118,1536]{2,0,1:T(2,128)}, u32[]{:S(2)}) copy-start(f32[2,118,1536]{2,0,1:T(2,128)} %param.22) | copy-start | bytes 4349956
  262.0 3.4 %copy-start.6 = (f32[2,118,1536]{2,0,1:T(2,128)S(1)}, f32[2,118,1536]{2,0,1:T(2,128)}, u32[]{:S(2)}) copy-start(f32[2,118,1536]{2,0,1:T(2,128)} %param.16) | copy-start | bytes 4349956
  262.0 3.4 %copy-start.7 = (f32[2,118,1536]{2,0,1:T(2,128)S(1)}, f32[2,118,1536]{2,0,1:T(2,128)}, u32[]{:S(2)}) copy-start(f32[2,118,1536]{2,0,1:T(2,128)} %param.19) | copy-start | bytes 4349956
  262.1 38.9 %collective-permute-start.4 = (bf16[256,1536]{1,0:T(8,128)(2,1)S(1)}, bf16[256,1536]{1,0:T(8,128)(2,1)S(1)}, u32[]{:S(2)}, u32[]{:S(2)}) collective-permute-start(bf16[256,1536]{1,0:T(8,128)(2,1)S(1)} %get-tuple-element.69), channel_id=1, source_target_pairs={{0,1},{1,4},{4,5},{5,0},{2,3},{3,6},{6,7},{7,2},{8,9},{9,12},{12,1... | collective-permute-start | bytes 2359304 | tf_op jit(solution)/shard_map/ppermute | solution.py:61
  262.7 38.4 %collective-permute-start.5 = (bf16[256,1536]{1,0:T(8,128)(2,1)S(1)}, bf16[256,1536]{1,0:T(8,128)(2,1)S(1)}, u32[]{:S(2)}, u32[]{:S(2)}) collective-permute-start(bf16[256,1536]{1,0:T(8,128)(2,1)S(1)} %get-tuple-element.68), channel_id=1, source_target_pairs={{0,5},{1,0},{4,1},{5,4},{2,7},{3,2},{6,3},{7,6},{8,13},{9,8},{12,9... | collective-permute-start | bytes 2359304 | tf_op jit(solution)/shard_map/ppermute | solution.py:62
  265.4 4.9 %copy-start.3 = (f32[2,1536,128]{2,1,0:T(8,128)S(1)}, f32[2,1536,128]{2,1,0:T(8,128)}, u32[]{:S(2)}) copy-start(f32[2,1536,128]{2,1,0:T(8,128)} %param.15) | copy-start | bytes 4718596
  265.4 4.9 %copy-start.4 = (f32[2,1536,128]{2,1,0:T(8,128)S(1)}, f32[2,1536,128]{2,1,0:T(8,128)}, u32[]{:S(2)}) copy-start(f32[2,1536,128]{2,1,0:T(8,128)} %param.18) | copy-start | bytes 4718596
  265.4 4.9 %copy-start.5 = (f32[2,1536,128]{2,1,0:T(8,128)S(1)}, f32[2,1536,128]{2,1,0:T(8,128)}, u32[]{:S(2)}) copy-start(f32[2,1536,128]{2,1,0:T(8,128)} %param.21) | copy-start | bytes 4718596
  267.0 24.8 %collective-permute-start.2 = (bf16[1,118,1536]{2,1,0:T(8,128)(2,1)S(1)}, bf16[1,118,1536]{2,1,0:T(8,128)(2,1)S(1)}, u32[]{:S(2)}, u32[]{:S(2)}) collective-permute-start(bf16[1,118,1536]{2,1,0:T(8,128)(2,1)S(1)} %get-tuple-element.77), channel_id=1, source_target_pairs={{0,1},{1,4},{4,5},{5,0},{2,3},{3,6},{6,7},{7,2},{8,9},{9,12},{12,1... | collective-permute-start | bytes 1087496 | tf_op jit(solution)/shard_map/ppermute | solution.py:61
  267.1 24.7 %collective-permute-start.3 = (bf16[1,118,1536]{2,1,0:T(8,128)(2,1)S(1)}, bf16[1,118,1536]{2,1,0:T(8,128)(2,1)S(1)}, u32[]{:S(2)}, u32[]{:S(2)}) collective-permute-start(bf16[1,118,1536]{2,1,0:T(8,128)(2,1)S(1)} %get-tuple-element.76), channel_id=1, source_target_pairs={{0,5},{1,0},{4,1},{5,4},{2,7},{3,2},{6,3},{7,6},{8,13},{9,8},{12,9... | collective-permute-start | bytes 1087496 | tf_op jit(solution)/shard_map/ppermute | solution.py:62
  273.4 24.9 %collective-permute-start = (bf16[1,1536,128]{2,1,0:T(8,128)(2,1)S(1)}, bf16[1,1536,128]{2,1,0:T(8,128)(2,1)S(1)}, u32[]{:S(2)}, u32[]{:S(2)}) collective-permute-start(bf16[1,1536,128]{2,1,0:T(8,128)(2,1)S(1)} %get-tuple-element.75), channel_id=1, source_target_pairs={{0,1},{1,4},{4,5},{5,0},{2,3},{3,6},{6,7},{7,2},{8,9},{9,12},{12,1... | collective-permute-start | bytes 1179656 | tf_op jit(solution)/shard_map/ppermute | solution.py:61
  291.7 7.8 %collective-permute-start.1 = (bf16[1,1536,128]{2,1,0:T(8,128)(2,1)S(1)}, bf16[1,1536,128]{2,1,0:T(8,128)(2,1)S(1)}, u32[]{:S(2)}, u32[]{:S(2)}) collective-permute-start(bf16[1,1536,128]{2,1,0:T(8,128)(2,1)S(1)} %get-tuple-element.74), channel_id=1, source_target_pairs={{0,5},{1,0},{4,1},{5,4},{2,7},{3,2},{6,3},{7,6},{8,13},{9,8},{12,9... | collective-permute-start | bytes 1179656 | tf_op jit(solution)/shard_map/ppermute | solution.py:62
Sparse Core Ops, SparseCore 0:
  51.0 19.5 reduce-scatter.4
  73.2 39.6 reduce-scatter.6
  116.0 25.4 reduce-scatter.8
  143.9 20.9 reduce-scatter.10
  168.3 69.2 all-gather.1

commit v5 on v3

--- a/solution.py
+++ b/solution.py
@@ -28,10 +28,18 @@
     part = lax.psum_scatter(buf.astype(jnp.bfloat16), "core", scatter_dimension=0, tiled=False)
     part = lax.psum_scatter(part, XRING, scatter_dimension=0, tiled=False)
     part = lax.psum_scatter(part.astype(jnp.float32), "y", scatter_dimension=0, tiled=False)
-    part = lax.psum(part, "z").astype(jnp.bfloat16)
-    part = lax.all_gather(part, "y", axis=0)
+    part = lax.psum(part, "z")
+    squares = lax.psum(jnp.sum(part * part), ("y", "xh", "core", "shard"))
+    part = lax.all_gather(part.astype(jnp.bfloat16), "y", axis=0)
     part = lax.all_gather(part, "xh", axis=0)
-    return lax.all_gather(part, "core", axis=0)
+    return lax.all_gather(part, "core", axis=0), squares
+
+
+def micro_sum(g):
+    acc = g[0].astype(jnp.float32)
+    for k in range(1, g.shape[0]):
+        acc = acc + g[k].astype(jnp.float32)
+    return acc
 
 
 def to_tiles(a):
@@ -88,18 +96,18 @@
 
     n_x = n_xh * n_s
     cut = n_core * n_xh * n_y
-    sx = to_tiles(jnp.sum(grad_xproj, axis=0, dtype=jnp.float32))
+    sx = to_tiles(micro_sum(grad_xproj))
     tx = sx.reshape(layers, n_s, inner // (8 * n_s), 8, 128)
     tx = jnp.transpose(tx, (1, 0, 2, 3, 4)).reshape(n_s, -1, 8, 128)
 
     ch_pad = -(-ch // 8) * 8
-    sc = jnp.sum(grad_chan, axis=0, dtype=jnp.float32)
+    sc = micro_sum(grad_chan)
     sc = to_tiles(jnp.pad(sc, ((0, 0), (0, ch_pad - ch), (0, 0))))
     lanes_c = half // 128
     tc = sc.reshape(layers, ch_pad // 8, n_s, lanes_c, 8, 128)
     tc = jnp.transpose(tc, (2, 0, 1, 3, 4, 5)).reshape(n_s, -1, 8, 128)
 
-    se = to_tiles(jnp.sum(grad_embed, axis=0, dtype=jnp.float32))
+    se = to_tiles(micro_sum(grad_embed))
     te = se.reshape(n_s, -1, 8, 128)
 
     counts = (tc.shape[1], tx.shape[1], te.shape[1])
@@ -110,7 +118,8 @@
     buf = tiles.reshape(n_s, n_core, n_xh, n_y, per, 8, 128)
     buf = jnp.transpose(buf, (1, 2, 0, 3, 4, 5, 6)).reshape(n_core, n_x, n_y, per, 8, 128)
 
-    mean_t = reduce_flat(buf).reshape(per * cut, 8, 128)
+    summed_t, sum_squares = reduce_flat(buf)
+    mean_t = summed_t.reshape(per * cut, 8, 128)
     inverse = 1.0 / total
     mt = mean_t.astype(jnp.float32) * inverse
     gc = mt[: counts[0]].reshape(layers, ch_pad // 8, lanes_c, 8, 128)
@@ -120,8 +129,7 @@
     ge = mt[counts[0] + counts[1] : used].reshape(rows_e // (8 * n_s), width // 128, 8, 128)
     mean_e = from_tiles(ge, rows_e // n_s, width)
 
-    partial_squares = jnp.sum(mt * mt)
-    squares = lax.psum(partial_squares, "shard")
+    squares = sum_squares * (inverse * inverse)
     norm_value = jnp.sqrt(squares)
     clip_factor = jnp.minimum(1.0, 1.0 / (norm_value + 1e-06))
     wx, mx, vx = adamw_update(weight_xproj, moment_xproj, second_xproj, mean_x, clip_factor)

time: 297 us -> 360 us (1.21)
  blocking collectives: 42.4 us -> 81.6 us
  waiting for transfers between devices: 147 us -> 179 us
  other arithmetic: 61.4 us -> 57.6 us
    psum x0 -> x1, waiting for transfers between devices: none -> 44.6 us  [reduce_flat(): part = lax.psum(part, 'z')]
    psum x2 -> x1, blocking collectives: 27.4 us -> 66.3 us  [reduce_flat(): squares = lax.psum(jnp.sum(part * part), ('y', 'xh', 'core', 'shard'))]
    reduce_sum x4 -> x1, other arithmetic: 22.2 us -> 1.82 us  [reduce_flat(): squares = lax.psum(jnp.sum(part * part), ('y', 'xh', 'core', 'shard'))]
    all_gather x1, waiting for transfers between devices: 15.8 us -> 0.02 us  [reduce_flat(): return (lax.all_gather(part, 'core', axis=0), squares)]
    concatenate x1, other arithmetic: 19.7 us -> 30.5 us  [on_device(): tiles = jnp.concatenate([tc, tx, te, pad], axis=1)]
    another operation x0 -> x2, other arithmetic: none -> 4.23 us
    mul x2, other arithmetic: 4.29 us -> 0.31 us  [adamw_update(): clipped = clip_factor * gradient]
    unnamed x25 -> x27, local copies, waits for them, and re-layouts: 10.5 us -> 12.9 us
  transfers between devices with their start and end apart: 11 -> 12, of which waited for: 8 -> 8; matrix products, arithmetic and copies ran while one was open for 5% -> 4% of each run, Pallas kernels for 0% -> 0%
where the time goes in v5:
time: 360 us
  waiting for transfers between devices  179 us (50%)
  blocking collectives  81.6 us (23%)
  other arithmetic  57.6 us (16%)
  local copies, waits for them, and re-layouts  19.2 us (5%)
  between operations  16.3 us (5%)
  starting transfers between devices  6.91 us (2%)
    psum x1, blocking collectives, reduce_flat(): squares = lax.psum(jnp.sum(part * part), ('y', 'xh', 'core', 'shard'))  66.3 us
    psum x1, waiting for transfers between devices, reduce_flat(): part = lax.psum(part, 'z')  44.6 us
    reduce_scatter x1, waiting for transfers between devices, reduce_flat(): part = lax.psum_scatter(part, XRING, scatter_dimension=0, tiled=False)  41.7 us
    concatenate x1, other arithmetic, on_device(): tiles = jnp.concatenate([tc, tx, te, pad], axis=1)  30.5 us
    all_gather x1, waiting for transfers between devices, reduce_flat(): part = lax.all_gather(part, 'xh', axis=0)  30 us
    unnamed x7, waiting for transfers between devices  26.2 us
    reduce_scatter x1, waiting for transfers between devices, reduce_flat(): lax.psum_scatter(buf.astype(jnp.bfloat16), 'core', scatter_dimension=0, t...  19.6 us
    all_gather x1, blocking collectives, reduce_flat(): part = lax.all_gather(part.astype(jnp.bfloat16), 'y', axis=0)  15.4 us
  transfers between devices with their start and end apart: 12, of which 8 were waited for; matrix products, arithmetic and copies ran while one was open for 4% of the time, Pallas kernels for 0%

profile of v5, /device:TPU:0, one launch (start us, length us, event | category | flops | bytes accessed | tf_op | source)
XLA Modules:
  0.0 360.2 jit_solution(1409658442178175323)
XLA Ops:
  7.2 0.0 reduce-scatter.6.cloned.1.call-start
  7.2 3.3 fusion.5
  10.5 1.1 pad.5
  11.7 1.0 reshape.107
  12.6 0.4 copy.48
  13.0 0.1 copy.49
  13.2 3.8 %add_convert_fusion = bf16[1,1024,1536]{2,1,0:T(8,128)(2,1)S(1)} fusion(bf16[2,1024,1536]{2,1,0:T(8,128)(2,1)} %param.14), kind=kLoop, calls=%fused_computation | loop fusion | flops 6291456 | bytes 9437184 | tf_op jit(solution)/shard_map/convert.7
  17.0 0.4 add_convert_fusion.1
  17.4 0.1 copy.50
  17.5 0.1 pad.15.clone
  17.6 30.5 %maximum_maximum_fusion = bf16[2,1520,8,128]{3,2,1,0:T(8,128)(2,1)S(1)} fusion(bf16[2,768,8,128]{3,2,1,0:T(8,128)(2,1)S(1)} %bitcast.55, bf16[2,384,8,128]{3,2,1,0:T(8,128)(2,1)S(1)} %bitcast.58, bf16[2,360,8,128]{3,2,1,0:T(8,128)(2,1)S(1)} %bitcast.61, bf16[1520]{0:T(1024)(128)(2,1)S(1)} %pad.15.clone), kind=kLoop, calls=%fused_computation.1 | loop fusion | flops 9338880 | bytes 12422112 | tf_op jit(solution)/shard_map/concatenate | solution.py:117
  48.1 3.1 copy.51
  51.2 0.0 reduce-scatter.6.cloned.1.call-update
  51.3 0.0 reduce-scatter.8.cloned.1.call-start
  51.3 19.6 %reduce-scatter.6.cloned.1.call-done = bf16[1,4,4,95,8,128]{5,4,3,2,1,0:T(8,128)(2,1)} async-done(((bf16[2,4,4,95,8,128]{5,4,3,2,1,0:T(8,128)(2,1)}), bf16[1,4,4,95,8,128]{5,4,3,2,1,0:T(8,128)(2,1)}) %reduce-scatter.6.cloned.1.call-update) | async-done | bytes 3112976 | tf_op jit(solution)/shard_map/reduce_scatter | solution.py:28
  70.9 0.0 reduce-scatter.8.cloned.1.call-update
  70.9 0.0 reduce-scatter.10.cloned.1.call-start
  71.0 41.7 %reduce-scatter.8.cloned.1.call-done = bf16[1,4,95,8,128]{4,3,2,1,0:T(8,128)(2,1)} async-done(((bf16[4,4,95,8,128]{4,3,2,1,0:T(8,128)(2,1)}), bf16[1,4,95,8,128]{4,3,2,1,0:T(8,128)(2,1)}) %reduce-scatter.8.cloned.1.call-update) | async-done | bytes 778256 | tf_op jit(solution)/shard_map/reduce_scatter | solution.py:29
  112.7 2.4 bitcast_convert_fusion
  115.1 0.0 all-reduce.4.cloned.1.call-start
  115.2 26.1 %reduce-scatter.10.cloned.1.call-done = f32[1,95,8,128]{3,2,1,0:T(8,128)} async-done(((f32[4,95,8,128]{3,2,1,0:T(8,128)}), f32[1,95,8,128]{3,2,1,0:T(8,128)}) %reduce-scatter.10.cloned.1.call-update) | async-done | bytes 389136
  141.3 0.0 all-gather.6.cloned.1.call-start
  141.4 44.6 %all-reduce.4.cloned.1.call-done = f32[95,8,128]{2,1,0:T(8,128)} async-done(((f32[95,8,128]{2,1,0:T(8,128)}), f32[95,8,128]{2,1,0:T(8,128)}) %all-reduce.4.cloned.1.call-update) | async-done | bytes 389136 | tf_op jit(solution)/shard_map/psum | solution.py:31
  185.9 1.8 multiply_reduce_fusion
  187.8 15.4 %all-gather = bf16[380,8,128]{2,1,0:T(8,128)(2,1)} all-gather(bf16[95,8,128]{2,1,0:T(8,128)(2,1)S(1)} %get-tuple-element.77), channel_id=2, replica_groups=mesh['z'=4,'y'=4,'xh'=2,'core'=2,'shard'=2] {'y'}, dimensions={0}, use_global_device_ids=true | all-gather | bytes 972800 | tf_op jit(solution)/shard_map/all_gather | solution.py:33
  203.1 0.0 all-gather.6.cloned.1.call-update
  203.2 0.0 all-gather.8.cloned.1.call-start
  203.2 30.0 %all-gather.6.cloned.1.call-done = bf16[8,95,8,128]{3,2,1,0:T(8,128)(2,1)} async-done(((bf16[4,95,8,128]{3,2,1,0:T(8,128)(2,1)}), bf16[8,95,8,128]{3,2,1,0:T(8,128)(2,1)}) %all-gather.6.cloned.1.call-update) | async-done | bytes 1556496 | tf_op jit(solution)/shard_map/all_gather | solution.py:34
  233.2 66.3 %psum.15 = f32[]{:T(128)} all-reduce(f32[]{:T(128)} %get-tuple-element.76), channel_id=1, replica_groups=mesh['z'=4,'y'=4,'xh'=2,'core'=2,'shard'=2] {'y','xh','core','shard'}, use_global_device_ids=true, to_apply=%region_5.6 | all-reduce | flops 1 | bytes 8 | tf_op jit(solution)/shard_map/psum | solution.py:32
  300.2 0.0 all-gather.8.cloned.1.call-done
  300.2 2.3 convert_multiply_fusion
  302.5 0.1 slice.41
  302.6 0.2 slice_multiply_fusion
  302.8 0.1 slice_multiply_fusion.1
  303.0 1.5 copy-done.2
  304.5 1.0 copy-done.3
  305.5 1.0 copy-done.1
  306.4 4.5 %fusion.6 = (bf16[512,1536]{1,0:T(8,128)(2,1)S(1)}, f32[512,1536]{1,0:T(8,128)}, f32[512,1536]{1,0:T(8,128)}, f32[512,1536]{1,0:T(8,128)}) fusion(f32[512,1536]{1,0:T(8,128)S(1)} %copy-done.1, f32[512,1536]{1,0:T(8,128)S(1)} %bitcast.56, f32[512,1536]{1,0:T(8,128)S(1)} %copy-done.2, f32[512,1536]{1,0:T(8,128)S(1)} %copy-done.3), kind=kLoop, calls=%fused_computation.41 | loop fusion | flops 12582912 | bytes 23592960 | tf_op jit(solution)/shard_map/convert_element_type | solution.py:140
  311.0 0.1 fusion.14
  311.1 0.1 collective-permute-start.4
  311.2 3.2 collective-permute-start.5
  314.4 1.5 fusion.8
  315.9 0.1 fusion.16
  316.0 0.1 collective-permute-start.2
  316.0 3.2 collective-permute-start.3
  319.3 3.0 fusion.11
  322.3 0.1 fusion.15
  322.3 0.1 collective-permute-start
  322.4 2.2 copy.56
  324.6 2.2 copy.57
  326.9 2.2 copy.58
  329.1 11.6 %collective-permute-done.2 = bf16[1,118,1536]{2,1,0:T(8,128)(2,1)S(1)} collective-permute-done((bf16[1,118,1536]{2,1,0:T(8,128)(2,1)S(1)}, bf16[1,118,1536]{2,1,0:T(8,128)(2,1)S(1)}, u32[]{:S(2)}, u32[]{:S(2)}) %collective-permute-start.2) | collective-permute-done | bytes 362528 | tf_op jit(solution)/shard_map/ppermute | solution.py:61
  340.8 0.1 broadcast_select_fusion.5
  340.9 0.2 pad_maximum_fusion.2
  341.1 2.6 copy.59
  343.7 1.8 collective-permute-done
  345.5 3.0 collective-permute-done.1
  348.5 0.1 constant_dynamic-update-slice_fusion
  348.6 0.2 broadcast_select_fusion.3
  348.8 1.2 pad_maximum_fusion.1
  350.0 0.1 constant_dynamic-update-slice_fusion.5
  350.1 0.1 constant_dynamic-update-slice_fusion.4
  350.1 0.2 broadcast_select_fusion.1
  350.4 1.9 pad_maximum_fusion
  (28 shorter events, 0.2 us)
Async XLA Ops:
  7.2 63.7 %reduce-scatter.6.cloned.1.call-start = ((), (), s32[]{:S(2)}) async-start(), calls=%async_computation.3 | async-start | bytes 9338880 | tf_op jit(solution)/shard_map/reduce_scatter | solution.py:28
  13.1 3.8 %copy-start = (bf16[2,2,3072,128]{3,2,1,0:T(8,128)(2,1)S(1)}, bf16[2,2,3072,128]{3,2,1,0:T(8,128)(2,1)}, u32[]{:S(2)}) copy-start(bf16[2,2,3072,128]{3,2,1,0:T(8,128)(2,1)} %param.12) | copy-start | bytes 9437188
  51.3 61.5 %reduce-scatter.8.cloned.1.call-start = ((), (), s32[]{:S(2)}) async-start(), calls=%async_computation.4 | async-start | bytes 3891200 | tf_op jit(solution)/shard_map/reduce_scatter | solution.py:29
  70.9 70.3 %reduce-scatter.10.cloned.1.call-start = ((), (), s32[]{:S(2)}) async-start(), calls=%async_computation.8 | async-start | bytes 1945600
  115.1 70.8 %all-reduce.4.cloned.1.call-start = ((), (), s32[]{:S(2)}) async-start(), calls=%async_computation.5 | async-start | bytes 778240 | tf_op jit(solution)/shard_map/psum | solution.py:31
  141.3 91.8 %all-gather.6.cloned.1.call-start = ((), (), s32[]{:S(2)}) async-start(), calls=%async_computation.6 | async-start | bytes 2334720 | tf_op jit(solution)/shard_map/all_gather | solution.py:34
  203.2 97.0 %all-gather.8.cloned.1.call-start = ((), (), s32[]{:S(2)}) async-start(), calls=%async_computation.7 | async-start | bytes 4669440 | tf_op jit(solution)/shard_map/all_gather | solution.py:35
  302.6 1.9 copy-start.2
  302.6 2.8 copy-start.3
  302.8 3.6 copy-start.1
  306.4 8.0 %copy-start.9 = (f32[2,118,1536]{2,0,1:T(2,128)S(1)}, f32[2,118,1536]{2,0,1:T(2,128)}, u32[]{:S(2)}) copy-start(f32[2,118,1536]{2,0,1:T(2,128)} %param.22) | copy-start | bytes 4349956
  311.0 3.4 copy-start.7
  311.0 3.4 copy-start.8
  311.1 38.9 %collective-permute-start.4 = (bf16[256,1536]{1,0:T(8,128)(2,1)S(1)}, bf16[256,1536]{1,0:T(8,128)(2,1)S(1)}, u32[]{:S(2)}, u32[]{:S(2)}) collective-permute-start(bf16[256,1536]{1,0:T(8,128)(2,1)S(1)} %get-tuple-element.67), channel_id=1, source_target_pairs={{0,1},{1,4},{4,5},{5,0},{2,3},{3,6},{6,7},{7,2},{8,9},{9,12},{12,1... | collective-permute-start | bytes 2359304 | tf_op jit(solution)/shard_map/ppermute | solution.py:61
  311.2 38.9 %collective-permute-start.5 = (bf16[256,1536]{1,0:T(8,128)(2,1)S(1)}, bf16[256,1536]{1,0:T(8,128)(2,1)S(1)}, u32[]{:S(2)}, u32[]{:S(2)}) collective-permute-start(bf16[256,1536]{1,0:T(8,128)(2,1)S(1)} %get-tuple-element.66), channel_id=1, source_target_pairs={{0,5},{1,0},{4,1},{5,4},{2,7},{3,2},{6,3},{7,6},{8,13},{9,8},{12,9... | collective-permute-start | bytes 2359304 | tf_op jit(solution)/shard_map/ppermute | solution.py:62
  314.4 4.9 %copy-start.4 = (f32[2,1536,128]{2,1,0:T(8,128)S(1)}, f32[2,1536,128]{2,1,0:T(8,128)}, u32[]{:S(2)}) copy-start(f32[2,1536,128]{2,1,0:T(8,128)} %param.15) | copy-start | bytes 4718596
  314.4 4.9 %copy-start.5 = (f32[2,1536,128]{2,1,0:T(8,128)S(1)}, f32[2,1536,128]{2,1,0:T(8,128)}, u32[]{:S(2)}) copy-start(f32[2,1536,128]{2,1,0:T(8,128)} %param.18) | copy-start | bytes 4718596
  314.4 4.9 %copy-start.6 = (f32[2,1536,128]{2,1,0:T(8,128)S(1)}, f32[2,1536,128]{2,1,0:T(8,128)}, u32[]{:S(2)}) copy-start(f32[2,1536,128]{2,1,0:T(8,128)} %param.21) | copy-start | bytes 4718596
  316.0 24.8 %collective-permute-start.2 = (bf16[1,118,1536]{2,1,0:T(8,128)(2,1)S(1)}, bf16[1,118,1536]{2,1,0:T(8,128)(2,1)S(1)}, u32[]{:S(2)}, u32[]{:S(2)}) collective-permute-start(bf16[1,118,1536]{2,1,0:T(8,128)(2,1)S(1)} %get-tuple-element.75), channel_id=1, source_target_pairs={{0,1},{1,4},{4,5},{5,0},{2,3},{3,6},{6,7},{7,2},{8,9},{9,12},{12,1... | collective-permute-start | bytes 1087496 | tf_op jit(solution)/shard_map/ppermute | solution.py:61
  316.0 24.7 %collective-permute-start.3 = (bf16[1,118,1536]{2,1,0:T(8,128)(2,1)S(1)}, bf16[1,118,1536]{2,1,0:T(8,128)(2,1)S(1)}, u32[]{:S(2)}, u32[]{:S(2)}) collective-permute-start(bf16[1,118,1536]{2,1,0:T(8,128)(2,1)S(1)} %get-tuple-element.74), channel_id=1, source_target_pairs={{0,5},{1,0},{4,1},{5,4},{2,7},{3,2},{6,3},{7,6},{8,13},{9,8},{12,9... | collective-permute-start | bytes 1087496 | tf_op jit(solution)/shard_map/ppermute | solution.py:62
  322.3 23.2 %collective-permute-start = (bf16[1,1536,128]{2,1,0:T(8,128)(2,1)S(1)}, bf16[1,1536,128]{2,1,0:T(8,128)(2,1)S(1)}, u32[]{:S(2)}, u32[]{:S(2)}) collective-permute-start(bf16[1,1536,128]{2,1,0:T(8,128)(2,1)S(1)} %get-tuple-element.73), channel_id=1, source_target_pairs={{0,1},{1,4},{4,5},{5,0},{2,3},{3,6},{6,7},{7,2},{8,9},{9,12},{12,1... | collective-permute-start | bytes 1179656 | tf_op jit(solution)/shard_map/ppermute | solution.py:61
  340.7 7.8 %collective-permute-start.1 = (bf16[1,1536,128]{2,1,0:T(8,128)(2,1)S(1)}, bf16[1,1536,128]{2,1,0:T(8,128)(2,1)S(1)}, u32[]{:S(2)}, u32[]{:S(2)}) collective-permute-start(bf16[1,1536,128]{2,1,0:T(8,128)(2,1)S(1)} %get-tuple-element.72), channel_id=1, source_target_pairs={{0,5},{1,0},{4,1},{5,4},{2,7},{3,2},{6,3},{7,6},{8,13},{9,8},{12,9... | collective-permute-start | bytes 1179656 | tf_op jit(solution)/shard_map/ppermute | solution.py:62
Sparse Core Ops, SparseCore 0:
  51.4 19.4 reduce-scatter.5
  73.4 39.3 reduce-scatter.7
  115.9 25.3 reduce-scatter.9
  143.6 42.2 all-reduce.3
  203.3 29.8 all-gather.5
  234.7 14.1 all-gather.7

commit v6 on v3

--- a/solution.py
+++ b/solution.py
@@ -34,9 +34,12 @@
     return lax.all_gather(part, "core", axis=0)
 
 
+TR = 16
+
+
 def to_tiles(a):
     *lead, r, c = a.shape
-    a = a.reshape(*lead, r // 8, 8, c // 128, 128)
+    a = a.reshape(*lead, r // TR, TR, c // 128, 128)
     n = len(lead)
     return jnp.swapaxes(a, n + 1, n + 2)
 
@@ -89,35 +92,37 @@
     n_x = n_xh * n_s
     cut = n_core * n_xh * n_y
     sx = to_tiles(jnp.sum(grad_xproj, axis=0, dtype=jnp.float32))
-    tx = sx.reshape(layers, n_s, inner // (8 * n_s), 8, 128)
-    tx = jnp.transpose(tx, (1, 0, 2, 3, 4)).reshape(n_s, -1, 8, 128)
+    tx = sx.reshape(layers, n_s, inner // (TR * n_s), TR, 128)
+    tx = jnp.transpose(tx, (1, 0, 2, 3, 4)).reshape(n_s, -1, TR, 128)
 
-    ch_pad = -(-ch // 8) * 8
+    ch_pad = -(-ch // TR) * TR
     sc = jnp.sum(grad_chan, axis=0, dtype=jnp.float32)
     sc = to_tiles(jnp.pad(sc, ((0, 0), (0, ch_pad - ch), (0, 0))))
     lanes_c = half // 128
-    tc = sc.reshape(layers, ch_pad // 8, n_s, lanes_c, 8, 128)
-    tc = jnp.transpose(tc, (2, 0, 1, 3, 4, 5)).reshape(n_s, -1, 8, 128)
+    tc = sc.reshape(layers, ch_pad // TR, n_s, lanes_c, TR, 128)
+    tc = jnp.transpose(tc, (2, 0, 1, 3, 4, 5)).reshape(n_s, -1, TR, 128)
 
     se = to_tiles(jnp.sum(grad_embed, axis=0, dtype=jnp.float32))
-    te = se.reshape(n_s, -1, 8, 128)
+    te = se.reshape(n_s, -1, TR, 128)
 
     counts = (tc.shape[1], tx.shape[1], te.shape[1])
     used = sum(counts)
     per = -(-used // cut)
-    pad = jnp.zeros((n_s, per * cut - used, 8, 128), jnp.float32)
-    tiles = jnp.concatenate([tc, tx, te, pad], axis=1)
-    buf = tiles.reshape(n_s, n_core, n_xh, n_y, per, 8, 128)
-    buf = jnp.transpose(buf, (1, 2, 0, 3, 4, 5, 6)).reshape(n_core, n_x, n_y, per, 8, 128)
+    parts = [tc, tx, te]
+    if per * cut > used:
+        parts.append(jnp.zeros((n_s, per * cut - used, TR, 128), jnp.float32))
+    tiles = jnp.concatenate(parts, axis=1)
+    buf = tiles.reshape(n_s, n_core, n_xh, n_y, per, TR, 128)
+    buf = jnp.transpose(buf, (1, 2, 0, 3, 4, 5, 6)).reshape(n_core, n_x, n_y, per, TR, 128)
 
-    mean_t = reduce_flat(buf).reshape(per * cut, 8, 128)
+    mean_t = reduce_flat(buf).reshape(per * cut, TR, 128)
     inverse = 1.0 / total
     mt = mean_t.astype(jnp.float32) * inverse
-    gc = mt[: counts[0]].reshape(layers, ch_pad // 8, lanes_c, 8, 128)
+    gc = mt[: counts[0]].reshape(layers, ch_pad // TR, lanes_c, TR, 128)
     mean_c = from_tiles(gc, ch_pad, half)[:, :ch, :]
-    gx = mt[counts[0] : counts[0] + counts[1]].reshape(layers, half // 8, 1, 8, 128)
+    gx = mt[counts[0] : counts[0] + counts[1]].reshape(layers, half // TR, 1, TR, 128)
     mean_x = from_tiles(gx, half, xw)
-    ge = mt[counts[0] + counts[1] : used].reshape(rows_e // (8 * n_s), width // 128, 8, 128)
+    ge = mt[counts[0] + counts[1] : used].reshape(rows_e // (TR * n_s), width // 128, TR, 128)
     mean_e = from_tiles(ge, rows_e // n_s, width)
 
     partial_squares = jnp.sum(mt * mt)

time: 297 us -> 295 us (level)
  other arithmetic: 61.4 us -> 44.9 us
  local copies, waits for them, and re-layouts: 20.6 us -> 34.7 us
    reduce_scatter x0 -> x1, waiting for transfers between devices: none -> 26.1 us  [reduce_flat(): lax.psum_scatter(part.astype(jnp.float32), 'y', scatter_dimension=0, tile...]
    unnamed x6 -> x5, waiting for transfers between devices: 26.2 us -> 0.08 us
    concatenate x1, other arithmetic: 19.7 us -> 2.5 us  [on_device(): tiles = jnp.concatenate(parts, axis=1)]
    reshape x2 -> x3, local copies, waits for them, and re-layouts: 1.54 us -> 7.47 us  [the longest x2 4.89 us: to_tiles(): a = a.reshape(*lead, r // TR, TR, c // 128, 128)]
    transpose x2 -> x5, local copies, waits for them, and re-layouts: 2.47 us -> 8.09 us  [the longest x2 3.4 us: to_tiles(): return jnp.swapaxes(a, n + 1, n + 2)]
    ppermute x3, starting transfers between devices: 6.12 us -> 9.46 us  [swap_halves(): lax.ppermute(second, XRING, perm=[(p, (p - 1) % n) for p in range(n)])]
    unnamed x25 -> x31, local copies, waits for them, and re-layouts: 10.5 us -> 12.2 us
  transfers between devices with their start and end apart: 11 -> 11, of which waited for: 8 -> 6; matrix products, arithmetic and copies ran while one was open for 5% -> 6% of each run, Pallas kernels for 0% -> 0%
where the time goes in v6:
time: 295 us
  waiting for transfers between devices  147 us (50%)
  other arithmetic  44.9 us (15%)
  blocking collectives  42.6 us (14%)
  local copies, waits for them, and re-layouts  34.7 us (12%)
  between operations  15.9 us (5%)
  starting transfers between devices  9.67 us (3%)
    reduce_scatter x1, waiting for transfers between devices, reduce_flat(): part = lax.psum_scatter(part, XRING, scatter_dimension=0, tiled=False)  42.1 us
    all_gather x1, waiting for transfers between devices, reduce_flat(): part = lax.all_gather(part, 'xh', axis=0)  29.4 us
    reduce_scatter x1, waiting for transfers between devices, reduce_flat(): lax.psum_scatter(part.astype(jnp.float32), 'y', scatter_dimension=0, tile...  26.1 us
    psum x1, blocking collectives, reduce_flat(): part = lax.psum(part, 'z').astype(jnp.bfloat16)  21.8 us
    reduce_scatter x1, waiting for transfers between devices, reduce_flat(): lax.psum_scatter(buf.astype(jnp.bfloat16), 'core', scatter_dimension=0, t...  19.7 us
    all_gather x1, waiting for transfers between devices, reduce_flat(): return lax.all_gather(part, 'core', axis=0)  15.9 us
    all_gather x1, blocking collectives, reduce_flat(): part = lax.all_gather(part, 'y', axis=0)  15.1 us
    ppermute x3, waiting for transfers between devices, swap_halves(): lax.ppermute(first, XRING, perm=[(p, (p + 1) % n) for p in range(n)])  13.8 us
  transfers between devices with their start and end apart: 11, of which 6 were waited for; matrix products, arithmetic and copies ran while one was open for 6% of the time, Pallas kernels for 0%

profile of v6, /device:TPU:0, one launch (start us, length us, event | category | flops | bytes accessed | tf_op | source)
XLA Modules:
  0.0 294.8 jit_solution(643250732976625092)
XLA Ops:
  7.2 0.0 reduce-scatter.4.cloned.1.call-start
  7.2 6.5 %reduce.1 = bf16[2,118,3072]{2,0,1:T(2,128)(2,1)S(1)} reduce(bf16[2,2,118,3072]{3,1,2,0:T(2,128)(2,1)} %param.13, bf16[]{:T(256)} %constant.18.clone.1), dimensions={0}, to_apply=%region_0.0.clone | reduce | flops 724992 | bytes 4349954 | tf_op jit(solution)/shard_map/reduce_sum | solution.py:99
  13.7 1.2 pad.5
  14.9 1.2 reshape.107
  16.1 0.4 copy.53
  16.6 1.4 copy.54
  18.0 2.9 reduce.2
  20.9 1.4 copy.55
  22.4 6.1 %reduce.3 = bf16[1024,1536]{1,0:T(8,128)(2,1)S(1)} reduce(bf16[2,1024,1536]{2,1,0:T(8,128)(2,1)} %param.14, bf16[]{:T(256)} %constant.18.clone.1), dimensions={0}, to_apply=%region_2.3.clone | reduce | flops 1572864 | bytes 9437186 | tf_op jit(solution)/shard_map/reduce_sum | solution.py:105
  28.4 3.7 %reshape.83 = bf16[64,16,12,128]{3,2,1,0:T(8,128)(2,1)} reshape(bf16[1024,1536]{1,0:T(8,128)(2,1)S(1)} %reduce.3) | data formatting | bytes 6291456 | tf_op jit(solution)/shard_map/reshape | solution.py:42
  32.1 3.0 %copy.56 = bf16[64,12,16,128]{3,2,1,0:T(8,128)(2,1)S(1)} copy(bf16[64,12,16,128]{3,1,2,0:T(8,128)(2,1)} %bitcast.44) | data formatting | bytes 6291456 | tf_op jit(solution)/shard_map/transpose | solution.py:44
  35.1 2.5 pad_maximum_fusion
  37.6 4.1 %copy.57 = bf16[2,2,2,4,48,16,128]{6,5,4,3,2,1,0:T(8,128)(2,1)} copy(bf16[2,2,2,4,48,16,128]{6,5,4,3,1,0,2:T(8,128)(2,1)S(1)} %bitcast.43) | data formatting | bytes 12582912 | tf_op jit(solution)/shard_map/convert_element_type | solution.py:28
  41.7 0.0 reduce-scatter.4.cloned.1.call-update
  41.7 0.0 reduce-scatter.6.cloned.1.call-start
  41.8 19.7 %reduce-scatter.4.cloned.1.call-done = bf16[1,4,4,48,16,128]{5,4,3,2,1,0:T(8,128)(2,1)} async-done(((bf16[2,4,4,48,16,128]{5,4,3,2,1,0:T(8,128)(2,1)}), bf16[1,4,4,48,16,128]{5,4,3,2,1,0:T(8,128)(2,1)}) %reduce-scatter.4.cloned.1.call-update) | async-done | bytes 3145744 | tf_op jit(solution)/shard_map/reduce_scatter | solution.py:28
  61.5 0.0 reduce-scatter.6.cloned.1.call-update
  61.5 0.0 reduce-scatter.8.cloned.1.call-start
  61.5 42.1 %reduce-scatter.6.cloned.1.call-done = bf16[1,4,48,16,128]{4,3,2,1,0:T(8,128)(2,1)} async-done(((bf16[4,4,48,16,128]{4,3,2,1,0:T(8,128)(2,1)}), bf16[1,4,48,16,128]{4,3,2,1,0:T(8,128)(2,1)}) %reduce-scatter.6.cloned.1.call-update) | async-done | bytes 786448 | tf_op jit(solution)/shard_map/reduce_scatter | solution.py:29
  103.7 2.4 bitcast_convert_fusion
  106.1 0.0 reduce-scatter.8.cloned.1.call-update
  106.1 0.0 all-gather.6.cloned.1.call-start
  106.2 26.1 %reduce-scatter.8.cloned.1.call-done = f32[1,48,16,128]{3,2,1,0:T(8,128)} async-done(((f32[4,48,16,128]{3,2,1,0:T(8,128)}), f32[1,48,16,128]{3,2,1,0:T(8,128)}) %reduce-scatter.8.cloned.1.call-update) | async-done | bytes 393232 | tf_op jit(solution)/shard_map/reduce_scatter | solution.py:30
  132.3 21.8 %all-reduce.2 = bf16[48,16,128]{2,1,0:T(8,128)(2,1)S(1)} all-reduce(f32[48,16,128]{2,1,0:T(8,128)} %bitcast.58), channel_id=1, replica_groups=mesh['z'=4,'y'=4,'xh'=2,'core'=2,'shard'=2] {'z'}, use_global_device_ids=true, to_apply=%region_6.7 | all-reduce | flops 98304 | bytes 589824 | tf_op jit(solution)/shard_map/psum | solution.py:31
  154.1 15.1 %all-gather = bf16[192,16,128]{2,1,0:T(8,128)(2,1)} all-gather(bf16[48,16,128]{2,1,0:T(8,128)(2,1)S(1)} %all-reduce.2), channel_id=2, replica_groups=mesh['z'=4,'y'=4,'xh'=2,'core'=2,'shard'=2] {'y'}, dimensions={0}, use_global_device_ids=true | all-gather | bytes 983040 | tf_op jit(solution)/shard_map/all_gather | solution.py:32
  169.2 0.0 all-gather.6.cloned.1.call-update
  169.2 0.0 all-gather.8.cloned.1.call-start
  169.2 29.4 %all-gather.6.cloned.1.call-done = bf16[8,48,16,128]{3,2,1,0:T(8,128)(2,1)} async-done(((bf16[4,48,16,128]{3,2,1,0:T(8,128)(2,1)}), bf16[8,48,16,128]{3,2,1,0:T(8,128)(2,1)}) %all-gather.6.cloned.1.call-update) | async-done | bytes 1572880 | tf_op jit(solution)/shard_map/all_gather | solution.py:33
  198.6 0.0 all-gather.8.cloned.1.call-update
  198.6 15.9 %all-gather.8.cloned.1.call-done = bf16[4,4,48,16,128]{4,3,2,1,0:T(8,128)(2,1)} async-done(((bf16[2,4,48,16,128]{4,3,2,1,0:T(8,128)(2,1)}), bf16[4,4,48,16,128]{4,3,2,1,0:T(8,128)(2,1)}) %all-gather.8.cloned.1.call-update) | async-done | bytes 3145744 | tf_op jit(solution)/shard_map/all_gather | solution.py:34
  214.5 6.7 %multiply_reduce_fusion = (f32[]{:T(128)}, f32[4,4,48,16,128]{4,3,2,1,0:T(8,128)}) fusion(bf16[4,4,48,16,128]{4,3,2,1,0:T(8,128)(2,1)} %all-gather.8.cloned.1.call-done), kind=kLoop, calls=%fused_computation.1 | loop fusion | flops 6291455 | bytes 9437188 | tf_op jit(solution)/shard_map/reduce_sum | solution.py:128
  221.2 5.8 %psum.15 = f32[]{:T(128)} all-reduce(f32[]{:T(128)} %get-tuple-element.68), channel_id=1, replica_groups=mesh['z'=4,'y'=4,'xh'=2,'core'=2,'shard'=2] {'shard'}, use_global_device_ids=true, to_apply=%region_8.9 | all-reduce | flops 1 | bytes 8 | tf_op jit(solution)/shard_map/psum | solution.py:129
  227.7 2.3 slice_multiply_fusion
  230.1 1.4 copy-done
  231.5 1.4 fusion.13
  232.9 1.8 copy.59
  234.7 2.6 reshape.86
  237.3 1.3 copy.63
  238.6 0.1 copy-done.2
  238.7 0.4 copy-done.9
  239.1 0.4 copy-done.10
  239.6 0.4 copy-done.11
  240.0 1.5 fusion.8
  241.5 2.2 copy.64
  243.8 2.9 collective-permute-start.3
  246.6 2.2 copy.65
  248.9 2.2 copy.66
  251.1 3.0 %fusion.11 = (bf16[2,1536,128]{2,1,0:T(8,128)(2,1)S(1)}, f32[2,1536,128]{2,1,0:T(8,128)}, f32[2,1536,128]{2,1,0:T(8,128)}, f32[2,1536,128]{2,1,0:T(8,128)}) fusion(f32[2,1536,128]{2,1,0:T(8,128)S(1)} %copy-done.6, f32[2,1536,128]{2,1,0:T(8,128)S(1)} %bitcast.54, f32[2,1536,128]{2,1,0:T(8,128)S(1)} %copy-done.7, f32[2,1536,128]{2,1,0:T(8,128)S(1)} %copy-done.8), kind=kLoop, calls=%fused_computation.39 | loop fusion | flops 6291456 | bytes 11796480 | tf_op jit(solution)/shard_map/convert_element_type | solution.py:135
  254.1 0.1 fusion.15
  254.2 3.3 %collective-permute-start.1 = (bf16[1,1536,128]{2,1,0:T(8,128)(2,1)S(1)}, bf16[1,1536,128]{2,1,0:T(8,128)(2,1)S(1)}, u32[]{:S(2)}, u32[]{:S(2)}) collective-permute-start(bf16[1,1536,128]{2,1,0:T(8,128)(2,1)S(1)} %get-tuple-element.76), channel_id=1, source_target_pairs={{0,5},{1,0},{4,1},{5,4},{2,7},{3,2},{6,3},{7,6},{8,13},{9,8},{12,9... | collective-permute-start | bytes 1179656 | tf_op jit(solution)/shard_map/ppermute | solution.py:57
  257.5 5.6 %fusion.5 = (bf16[512,1536]{1,0:T(8,128)(2,1)S(1)}, f32[512,1536]{1,0:T(8,128)}, f32[512,1536]{1,0:T(8,128)}, f32[512,1536]{1,0:T(8,128)}) fusion(f32[512,1536]{1,0:T(8,128)S(1)} %copy-done.3, f32[64,8,12,128]{3,2,1,0:T(8,128)S(1)} %bitcast.45, f32[512,1536]{1,0:T(8,128)S(1)} %copy-done.4, f32[512,1536]{1,0:T(8,128)S(1)} %copy-done.5), kind=kLoop, calls=%fused_computation.37 | loop fusion | flops 12582912 | bytes 23592960 | tf_op jit(solution)/shard_map/convert_element_type | solution.py:137
  263.2 0.1 fusion.14
  263.3 3.3 %collective-permute-start.5 = (bf16[256,1536]{1,0:T(8,128)(2,1)S(1)}, bf16[256,1536]{1,0:T(8,128)(2,1)S(1)}, u32[]{:S(2)}, u32[]{:S(2)}) collective-permute-start(bf16[256,1536]{1,0:T(8,128)(2,1)S(1)} %get-tuple-element.70), channel_id=1, source_target_pairs={{0,5},{1,0},{4,1},{5,4},{2,7},{3,2},{6,3},{7,6},{8,13},{9,8},{12,9... | collective-permute-start | bytes 2359304 | tf_op jit(solution)/shard_map/ppermute | solution.py:57
  266.6 0.2 broadcast_select_fusion.5
  266.8 0.2 pad_maximum_fusion.3
  267.0 2.6 copy.67
  269.6 0.1 constant_dynamic-update-slice_fusion
  269.7 0.2 broadcast_select_fusion.3
  269.9 1.2 pad_maximum_fusion.2
  271.2 13.8 %collective-permute-done.4 = bf16[256,1536]{1,0:T(8,128)(2,1)S(1)} collective-permute-done((bf16[256,1536]{1,0:T(8,128)(2,1)S(1)}, bf16[256,1536]{1,0:T(8,128)(2,1)S(1)}, u32[]{:S(2)}, u32[]{:S(2)}) %collective-permute-start.4) | collective-permute-done | bytes 786464 | tf_op jit(solution)/shard_map/ppermute | solution.py:56
  285.0 0.1 constant_dynamic-update-slice_fusion.5
  285.0 0.1 constant_dynamic-update-slice_fusion.4
  285.1 0.2 broadcast_select_fusion.1
  285.3 1.9 pad_maximum_fusion.1
  (31 shorter events, 0.2 us)
Async XLA Ops:
  7.2 54.3 %reduce-scatter.4.cloned.1.call-start = ((), (), s32[]{:S(2)}) async-start(), calls=%async_computation.3 | async-start | bytes 9437184 | tf_op jit(solution)/shard_map/reduce_scatter | solution.py:28
  41.7 61.9 %reduce-scatter.6.cloned.1.call-start = ((), (), s32[]{:S(2)}) async-start(), calls=%async_computation.4 | async-start | bytes 3932160 | tf_op jit(solution)/shard_map/reduce_scatter | solution.py:29
  61.5 70.8 %reduce-scatter.8.cloned.1.call-start = ((), (), s32[]{:S(2)}) async-start(), calls=%async_computation.5 | async-start | bytes 1966080 | tf_op jit(solution)/shard_map/reduce_scatter | solution.py:30
  106.1 92.5 %all-gather.6.cloned.1.call-start = ((), (), s32[]{:S(2)}) async-start(), calls=%async_computation.6 | async-start | bytes 2359296 | tf_op jit(solution)/shard_map/all_gather | solution.py:33
  169.2 45.3 %all-gather.8.cloned.1.call-start = ((), (), s32[]{:S(2)}) async-start(), calls=%async_computation.7 | async-start | bytes 4718592 | tf_op jit(solution)/shard_map/all_gather | solution.py:34
  227.7 3.7 %copy-start = (f32[4,4,48,16,128]{4,3,2,1,0:T(8,128)S(1)}, f32[4,4,48,16,128]{4,3,2,1,0:T(8,128)}, u32[]{:S(2)}) copy-start(f32[4,4,48,16,128]{4,3,2,1,0:T(8,128)} %get-tuple-element.69) | copy-start | bytes 18874372
  237.3 1.4 copy-start.2
  237.3 1.8 copy-start.9
  237.3 2.3 copy-start.10
  237.3 2.7 copy-start.11
  243.7 7.4 %copy-start.8 = (f32[2,1536,128]{2,1,0:T(8,128)S(1)}, f32[2,1536,128]{2,1,0:T(8,128)}, u32[]{:S(2)}) copy-start(f32[2,1536,128]{2,1,0:T(8,128)} %param.21) | copy-start | bytes 4718596
  243.8 22.8 %collective-permute-start.3 = (bf16[1,118,1536]{2,1,0:T(8,128)(2,1)S(1)}, bf16[1,118,1536]{2,1,0:T(8,128)(2,1)S(1)}, u32[]{:S(2)}, u32[]{:S(2)}) collective-permute-start(bf16[1,118,1536]{2,1,0:T(8,128)(2,1)S(1)} %get-tuple-element.78), channel_id=1, source_target_pairs={{0,5},{1,0},{4,1},{5,4},{2,7},{3,2},{6,3},{7,6},{8,13},{9,8},{12,9... | collective-permute-start | bytes 1087496 | tf_op jit(solution)/shard_map/ppermute | solution.py:57
  246.6 19.9 %collective-permute-start.2 = (bf16[1,118,1536]{2,1,0:T(8,128)(2,1)S(1)}, bf16[1,118,1536]{2,1,0:T(8,128)(2,1)S(1)}, u32[]{:S(2)}, u32[]{:S(2)}) collective-permute-start(bf16[1,118,1536]{2,1,0:T(8,128)(2,1)S(1)} %get-tuple-element.79), channel_id=1, source_target_pairs={{0,1},{1,4},{4,5},{5,0},{2,3},{3,6},{6,7},{7,2},{8,9},{9,12},{12,1... | collective-permute-start | bytes 1087496 | tf_op jit(solution)/shard_map/ppermute | solution.py:56
  246.6 4.5 %copy-start.6 = (f32[2,1536,128]{2,1,0:T(8,128)S(1)}, f32[2,1536,128]{2,1,0:T(8,128)}, u32[]{:S(2)}) copy-start(f32[2,1536,128]{2,1,0:T(8,128)} %param.15) | copy-start | bytes 4718596
  246.6 4.5 %copy-start.7 = (f32[2,1536,128]{2,1,0:T(8,128)S(1)}, f32[2,1536,128]{2,1,0:T(8,128)}, u32[]{:S(2)}) copy-start(f32[2,1536,128]{2,1,0:T(8,128)} %param.18) | copy-start | bytes 4718596
  248.9 2.2 copy-start.1
  251.1 6.4 %copy-start.3 = (f32[512,1536]{1,0:T(8,128)S(1)}, f32[512,1536]{1,0:T(8,128)}, u32[]{:S(2)}) copy-start(f32[512,1536]{1,0:T(8,128)} %param.17) | copy-start | bytes 9437188
  251.1 6.4 %copy-start.4 = (f32[512,1536]{1,0:T(8,128)S(1)}, f32[512,1536]{1,0:T(8,128)}, u32[]{:S(2)}) copy-start(f32[512,1536]{1,0:T(8,128)} %param.20) | copy-start | bytes 9437188
  251.1 6.4 %copy-start.5 = (f32[512,1536]{1,0:T(8,128)S(1)}, f32[512,1536]{1,0:T(8,128)}, u32[]{:S(2)}) copy-start(f32[512,1536]{1,0:T(8,128)} %param.23) | copy-start | bytes 9437188
  254.2 15.4 %collective-permute-start.1 = (bf16[1,1536,128]{2,1,0:T(8,128)(2,1)S(1)}, bf16[1,1536,128]{2,1,0:T(8,128)(2,1)S(1)}, u32[]{:S(2)}, u32[]{:S(2)}) collective-permute-start(bf16[1,1536,128]{2,1,0:T(8,128)(2,1)S(1)} %get-tuple-element.76), channel_id=1, source_target_pairs={{0,5},{1,0},{4,1},{5,4},{2,7},{3,2},{6,3},{7,6},{8,13},{9,8},{12,9... | collective-permute-start | bytes 1179656 | tf_op jit(solution)/shard_map/ppermute | solution.py:57
  257.5 12.1 %collective-permute-start = (bf16[1,1536,128]{2,1,0:T(8,128)(2,1)S(1)}, bf16[1,1536,128]{2,1,0:T(8,128)(2,1)S(1)}, u32[]{:S(2)}, u32[]{:S(2)}) collective-permute-start(bf16[1,1536,128]{2,1,0:T(8,128)(2,1)S(1)} %get-tuple-element.77), channel_id=1, source_target_pairs={{0,1},{1,4},{4,5},{5,0},{2,3},{3,6},{6,7},{7,2},{8,9},{9,12},{12,1... | collective-permute-start | bytes 1179656 | tf_op jit(solution)/shard_map/ppermute | solution.py:56
  263.3 21.8 %collective-permute-start.5 = (bf16[256,1536]{1,0:T(8,128)(2,1)S(1)}, bf16[256,1536]{1,0:T(8,128)(2,1)S(1)}, u32[]{:S(2)}, u32[]{:S(2)}) collective-permute-start(bf16[256,1536]{1,0:T(8,128)(2,1)S(1)} %get-tuple-element.70), channel_id=1, source_target_pairs={{0,5},{1,0},{4,1},{5,4},{2,7},{3,2},{6,3},{7,6},{8,13},{9,8},{12,9... | collective-permute-start | bytes 2359304 | tf_op jit(solution)/shard_map/ppermute | solution.py:57
  266.6 18.4 %collective-permute-start.4 = (bf16[256,1536]{1,0:T(8,128)(2,1)S(1)}, bf16[256,1536]{1,0:T(8,128)(2,1)S(1)}, u32[]{:S(2)}, u32[]{:S(2)}) collective-permute-start(bf16[256,1536]{1,0:T(8,128)(2,1)S(1)} %get-tuple-element.71), channel_id=1, source_target_pairs={{0,1},{1,4},{4,5},{5,0},{2,3},{3,6},{6,7},{7,2},{8,9},{9,12},{12,1... | collective-permute-start | bytes 2359304 | tf_op jit(solution)/shard_map/ppermute | solution.py:56
Sparse Core Ops, SparseCore 0:
  41.9 19.5 reduce-scatter.3
  64.0 39.6 reduce-scatter.5
  106.8 25.4 reduce-scatter.7
  169.3 29.2 all-gather.5
  200.2 14.2 all-gather.7

commit v7 on v6

--- a/solution.py
+++ b/solution.py
@@ -29,9 +29,14 @@
     part = lax.psum_scatter(part, XRING, scatter_dimension=0, tiled=False)
     part = lax.psum_scatter(part.astype(jnp.float32), "y", scatter_dimension=0, tiled=False)
     part = lax.psum(part, "z").astype(jnp.bfloat16)
+    wide = part.astype(jnp.float32)
+    squares = jnp.sum(wide * wide)
     part = lax.all_gather(part, "y", axis=0)
     part = lax.all_gather(part, "xh", axis=0)
-    return lax.all_gather(part, "core", axis=0)
+    part = lax.all_gather(part, "core", axis=0)
+    for axis in ("y", XRING, "core"):
+        squares = lax.psum(squares, axis)
+    return part, squares
 
 
 TR = 16
@@ -115,7 +120,8 @@
     buf = tiles.reshape(n_s, n_core, n_xh, n_y, per, TR, 128)
     buf = jnp.transpose(buf, (1, 2, 0, 3, 4, 5, 6)).reshape(n_core, n_x, n_y, per, TR, 128)
 
-    mean_t = reduce_flat(buf).reshape(per * cut, TR, 128)
+    summed_t, sum_squares = reduce_flat(buf)
+    mean_t = summed_t.reshape(per * cut, TR, 128)
     inverse = 1.0 / total
     mt = mean_t.astype(jnp.float32) * inverse
     gc = mt[: counts[0]].reshape(layers, ch_pad // TR, lanes_c, TR, 128)
@@ -125,8 +131,7 @@
     ge = mt[counts[0] + counts[1] : used].reshape(rows_e // (TR * n_s), width // 128, TR, 128)
     mean_e = from_tiles(ge, rows_e // n_s, width)
 
-    partial_squares = jnp.sum(mt * mt)
-    squares = lax.psum(partial_squares, "shard")
+    squares = sum_squares * (inverse * inverse)
     norm_value = jnp.sqrt(squares)
     clip_factor = jnp.minimum(1.0, 1.0 / (norm_value + 1e-06))
     wx, mx, vx = adamw_update(weight_xproj, moment_xproj, second_xproj, mean_x, clip_factor)

time: 295 us -> 290 us (0.983)
  blocking collectives: 42.6 us -> 60.5 us
  waiting for transfers between devices: 147 us -> 132 us
  other arithmetic: 44.9 us -> 39.4 us
    psum x1 -> x3, blocking collectives: 5.77 us -> 23.7 us  [reduce_flat(): squares = lax.psum(squares, axis)]
    all_gather x1, waiting for transfers between devices: 15.9 us -> 0.02 us  [reduce_flat(): part = lax.all_gather(part, 'core', axis=0)]
    reduce_sum x1, other arithmetic: 6.73 us -> 0.7 us  [reduce_flat(): squares = jnp.sum(wide * wide)]
    ppermute x3, starting transfers between devices: 9.46 us -> 6.35 us  [swap_halves(): lax.ppermute(second, XRING, perm=[(p, (p - 1) % n) for p in range(n)])]
    unnamed x31 -> x29, local copies, waits for them, and re-layouts: 12.2 us -> 11 us
  transfers between devices with their start and end apart: 11 -> 11, of which waited for: 6 -> 5; matrix products, arithmetic and copies ran while one was open for 6% -> 6% of each run, Pallas kernels for 0% -> 0%
where the time goes in v7:
time: 290 us; the launch traced here: 289 us
  waiting for transfers between devices  132 us (46%)
  blocking collectives  60.5 us (21%)
  other arithmetic  39.4 us (14%)
  local copies, waits for them, and re-layouts  33.5 us (12%)
  between operations  15.9 us (5%)
  starting transfers between devices  7.72 us (3%)
    reduce_scatter x1, waiting for transfers between devices, reduce_flat(): part = lax.psum_scatter(part, XRING, scatter_dimension=0, tiled=False)  42.1 us
    all_gather x1, waiting for transfers between devices, reduce_flat(): part = lax.all_gather(part, 'xh', axis=0)  29.4 us
    reduce_scatter x1, waiting for transfers between devices, reduce_flat(): lax.psum_scatter(part.astype(jnp.float32), 'y', scatter_dimension=0, tile...  26.1 us
    psum x3, blocking collectives, reduce_flat(): squares = lax.psum(squares, axis)  23.7 us
    psum x1, blocking collectives, reduce_flat(): part = lax.psum(part, 'z').astype(jnp.bfloat16)  21.8 us
    reduce_scatter x1, waiting for transfers between devices, reduce_flat(): lax.psum_scatter(buf.astype(jnp.bfloat16), 'core', scatter_dimension=0, t...  19.7 us
    all_gather x1, blocking collectives, reduce_flat(): part = lax.all_gather(part, 'y', axis=0)  15.1 us
    ppermute x3, waiting for transfers between devices, swap_halves(): lax.ppermute(first, XRING, perm=[(p, (p + 1) % n) for p in range(n)])  14.8 us
  transfers between devices with their start and end apart: 11, of which 5 were waited for; matrix products, arithmetic and copies ran while one was open for 6% of the time, Pallas kernels for 0%

profile of v7, /device:TPU:0, one launch (start us, length us, event | category | flops | bytes accessed | tf_op | source)
XLA Modules:
  0.0 289.3 jit_solution(4471787818880077175)
XLA Ops:
  7.2 0.0 reduce-scatter.4.cloned.1.call-start
  7.2 6.5 %reduce = bf16[2,118,3072]{2,0,1:T(2,128)(2,1)S(1)} reduce(bf16[2,2,118,3072]{3,1,2,0:T(2,128)(2,1)} %param.13, bf16[]{:T(256)} %constant.19.clone.1), dimensions={0}, to_apply=%region_0.0.clone | reduce | flops 724992 | bytes 4349954 | tf_op jit(solution)/shard_map/reduce_sum | solution.py:104
  13.7 1.2 pad.5
  14.9 1.2 reshape.106
  16.1 0.4 copy.53
  16.6 1.4 copy.54
  18.0 2.9 %reduce.1 = bf16[2,3072,128]{2,1,0:T(8,128)(2,1)S(1)} reduce(bf16[2,2,3072,128]{3,2,1,0:T(8,128)(2,1)} %param.12, bf16[]{:T(256)} %constant.19.clone.1), dimensions={0}, to_apply=%region_1.0.clone | reduce | flops 786432 | bytes 4718594 | tf_op jit(solution)/shard_map/reduce_sum | solution.py:99
  20.9 1.4 copy.55
  22.4 6.1 %reduce.2 = bf16[1024,1536]{1,0:T(8,128)(2,1)S(1)} reduce(bf16[2,1024,1536]{2,1,0:T(8,128)(2,1)} %param.14, bf16[]{:T(256)} %constant.19.clone.1), dimensions={0}, to_apply=%region_2.3.clone | reduce | flops 1572864 | bytes 9437186 | tf_op jit(solution)/shard_map/reduce_sum | solution.py:110
  28.4 3.7 %reshape.83 = bf16[64,16,12,128]{3,2,1,0:T(8,128)(2,1)} reshape(bf16[1024,1536]{1,0:T(8,128)(2,1)S(1)} %reduce.2) | data formatting | bytes 6291456 | tf_op jit(solution)/shard_map/reshape | solution.py:47
  32.1 3.0 %copy.56 = bf16[64,12,16,128]{3,2,1,0:T(8,128)(2,1)S(1)} copy(bf16[64,12,16,128]{3,1,2,0:T(8,128)(2,1)} %bitcast.44) | data formatting | bytes 6291456 | tf_op jit(solution)/shard_map/transpose | solution.py:49
  35.1 2.5 pad_maximum_fusion
  37.6 4.1 %copy.57 = bf16[2,2,2,4,48,16,128]{6,5,4,3,2,1,0:T(8,128)(2,1)} copy(bf16[2,2,2,4,48,16,128]{6,5,4,3,1,0,2:T(8,128)(2,1)S(1)} %bitcast.43) | data formatting | bytes 12582912 | tf_op jit(solution)/shard_map/convert_element_type | solution.py:28
  41.7 0.0 reduce-scatter.6.cloned.1.call-start
  41.8 19.7 %reduce-scatter.4.cloned.1.call-done = bf16[1,4,4,48,16,128]{5,4,3,2,1,0:T(8,128)(2,1)} async-done(((bf16[2,4,4,48,16,128]{5,4,3,2,1,0:T(8,128)(2,1)}), bf16[1,4,4,48,16,128]{5,4,3,2,1,0:T(8,128)(2,1)}) %reduce-scatter.4.cloned.1.call-update) | async-done | bytes 3145744 | tf_op jit(solution)/shard_map/reduce_scatter | solution.py:28
  61.5 0.0 reduce-scatter.8.cloned.1.call-start
  61.5 42.1 %reduce-scatter.6.cloned.1.call-done = bf16[1,4,48,16,128]{4,3,2,1,0:T(8,128)(2,1)} async-done(((bf16[4,4,48,16,128]{4,3,2,1,0:T(8,128)(2,1)}), bf16[1,4,48,16,128]{4,3,2,1,0:T(8,128)(2,1)}) %reduce-scatter.6.cloned.1.call-update) | async-done | bytes 786448 | tf_op jit(solution)/shard_map/reduce_scatter | solution.py:29
  103.7 2.4 bitcast_convert_fusion
  106.1 0.0 all-gather.6.cloned.1.call-start
  106.2 26.1 %reduce-scatter.8.cloned.1.call-done = f32[1,48,16,128]{3,2,1,0:T(8,128)} async-done(((f32[4,48,16,128]{3,2,1,0:T(8,128)}), f32[1,48,16,128]{3,2,1,0:T(8,128)}) %reduce-scatter.8.cloned.1.call-update) | async-done | bytes 393232 | tf_op jit(solution)/shard_map/reduce_scatter | solution.py:30
  132.3 21.8 %all-reduce.2 = bf16[48,16,128]{2,1,0:T(8,128)(2,1)S(1)} all-reduce(f32[48,16,128]{2,1,0:T(8,128)} %bitcast.58), channel_id=1, replica_groups=mesh['z'=4,'y'=4,'xh'=2,'core'=2,'shard'=2] {'z'}, use_global_device_ids=true, to_apply=%region_6.7 | all-reduce | flops 98304 | bytes 589824 | tf_op jit(solution)/shard_map/psum | solution.py:31
  154.1 15.1 %all-gather = bf16[192,16,128]{2,1,0:T(8,128)(2,1)} all-gather(bf16[48,16,128]{2,1,0:T(8,128)(2,1)S(1)} %all-reduce.2), channel_id=2, replica_groups=mesh['z'=4,'y'=4,'xh'=2,'core'=2,'shard'=2] {'y'}, dimensions={0}, use_global_device_ids=true | all-gather | bytes 983040 | tf_op jit(solution)/shard_map/all_gather | solution.py:34
  169.2 0.0 all-gather.6.cloned.1.call-update
  169.2 0.0 all-gather.8.cloned.1.call-start
  169.3 29.4 %all-gather.6.cloned.1.call-done = bf16[8,48,16,128]{3,2,1,0:T(8,128)(2,1)} async-done(((bf16[4,48,16,128]{3,2,1,0:T(8,128)(2,1)}), bf16[8,48,16,128]{3,2,1,0:T(8,128)(2,1)}) %all-gather.6.cloned.1.call-update) | async-done | bytes 1572880 | tf_op jit(solution)/shard_map/all_gather | solution.py:35
  198.6 0.7 multiply_reduce_fusion
  199.3 11.1 %psum.29 = f32[]{:T(128)} all-reduce(f32[]{:T(128)} %multiply_reduce_fusion), channel_id=1, replica_groups=mesh['z'=4,'y'=4,'xh'=2,'core'=2,'shard'=2] {'y'}, use_global_device_ids=true, to_apply=%region_8.9 | all-reduce | flops 1 | bytes 8 | tf_op jit(solution)/shard_map/psum | solution.py:38
  210.4 9.5 %psum.30 = f32[]{:T(128)} all-reduce(f32[]{:T(128)} %psum.29), channel_id=1, replica_groups=mesh['z'=4,'y'=4,'xh'=2,'core'=2,'shard'=2] {'xh','shard'}, use_global_device_ids=true, to_apply=%region_9.10 | all-reduce | flops 1 | bytes 8 | tf_op jit(solution)/shard_map/psum | solution.py:38
  219.9 3.1 %psum.31 = f32[]{:T(128)} all-reduce(f32[]{:T(128)} %psum.30), channel_id=1, replica_groups=mesh['z'=4,'y'=4,'xh'=2,'core'=2,'shard'=2] {'core'}, use_global_device_ids=true, to_apply=%region_10.11 | all-reduce | flops 1 | bytes 8 | tf_op jit(solution)/shard_map/psum | solution.py:38
  223.7 0.0 all-gather.8.cloned.1.call-done
  223.8 2.5 convert_multiply_fusion
  226.3 0.3 slice_multiply_fusion
  226.6 1.5 fusion.13
  228.0 1.8 copy.59
  229.9 2.6 reshape.86
  232.5 1.3 copy.63
  233.7 0.1 copy-done.1
  233.8 0.4 copy-done.8
  234.3 0.4 copy-done.9
  234.7 0.4 copy-done.10
  235.2 1.5 fusion.8
  236.6 2.2 copy.64
  238.9 0.9 collective-permute-start.3
  239.8 1.2 collective-permute-start.2
  241.0 2.2 copy.65
  243.2 2.2 copy.66
  245.5 3.0 %fusion.11 = (bf16[2,1536,128]{2,1,0:T(8,128)(2,1)S(1)}, f32[2,1536,128]{2,1,0:T(8,128)}, f32[2,1536,128]{2,1,0:T(8,128)}, f32[2,1536,128]{2,1,0:T(8,128)}) fusion(f32[2,1536,128]{2,1,0:T(8,128)S(1)} %copy-done.5, f32[2,1536,128]{2,1,0:T(8,128)S(1)} %bitcast.54, f32[2,1536,128]{2,1,0:T(8,128)S(1)} %copy-done.6, f32[2,1536,128]{2,1,0:T(8,128)S(1)} %copy-done.7), kind=kLoop, calls=%fused_computation.39 | loop fusion | flops 6291456 | bytes 11796480 | tf_op jit(solution)/shard_map/convert_element_type | solution.py:140
  248.5 0.1 fusion.15
  248.6 2.1 collective-permute-start.1
  250.7 0.2 copy-done.4
  250.9 5.7 %fusion.5 = (bf16[512,1536]{1,0:T(8,128)(2,1)S(1)}, f32[512,1536]{1,0:T(8,128)}, f32[512,1536]{1,0:T(8,128)}, f32[512,1536]{1,0:T(8,128)}) fusion(f32[512,1536]{1,0:T(8,128)S(1)} %copy-done.2, f32[64,8,12,128]{3,2,1,0:T(8,128)S(1)} %bitcast.45, f32[512,1536]{1,0:T(8,128)S(1)} %copy-done.3, f32[512,1536]{1,0:T(8,128)S(1)} %copy-done.4), kind=kLoop, calls=%fused_computation.37 | loop fusion | flops 12582912 | bytes 23592960 | tf_op jit(solution)/shard_map/convert_element_type | solution.py:142
  256.6 0.1 fusion.14
  256.7 3.3 %collective-permute-start.5 = (bf16[256,1536]{1,0:T(8,128)(2,1)S(1)}, bf16[256,1536]{1,0:T(8,128)(2,1)S(1)}, u32[]{:S(2)}, u32[]{:S(2)}) collective-permute-start(bf16[256,1536]{1,0:T(8,128)(2,1)S(1)} %get-tuple-element.68), channel_id=1, source_target_pairs={{0,5},{1,0},{4,1},{5,4},{2,7},{3,2},{6,3},{7,6},{8,13},{9,8},{12,9... | collective-permute-start | bytes 2359304 | tf_op jit(solution)/shard_map/ppermute | solution.py:62
  260.1 0.2 broadcast_select_fusion.5
  260.3 0.2 pad_maximum_fusion.3
  260.5 2.6 copy.67
  263.1 0.1 constant_dynamic-update-slice_fusion
  263.2 0.2 broadcast_select_fusion.3
  263.4 1.2 pad_maximum_fusion.2
  264.6 14.8 %collective-permute-done.4 = bf16[256,1536]{1,0:T(8,128)(2,1)S(1)} collective-permute-done((bf16[256,1536]{1,0:T(8,128)(2,1)S(1)}, bf16[256,1536]{1,0:T(8,128)(2,1)S(1)}, u32[]{:S(2)}, u32[]{:S(2)}) %collective-permute-start.4) | collective-permute-done | bytes 786464 | tf_op jit(solution)/shard_map/ppermute | solution.py:61
  279.4 0.1 constant_dynamic-update-slice_fusion.5
  279.5 0.1 constant_dynamic-update-slice_fusion.4
  279.6 0.2 broadcast_select_fusion.1
  279.8 1.9 pad_maximum_fusion.1
  (32 shorter events, 0.2 us)
Async XLA Ops:
  7.2 54.3 %reduce-scatter.4.cloned.1.call-start = ((), (), s32[]{:S(2)}) async-start(), calls=%async_computation.3 | async-start | bytes 9437184 | tf_op jit(solution)/shard_map/reduce_scatter | solution.py:28
  41.7 61.9 %reduce-scatter.6.cloned.1.call-start = ((), (), s32[]{:S(2)}) async-start(), calls=%async_computation.4 | async-start | bytes 3932160 | tf_op jit(solution)/shard_map/reduce_scatter | solution.py:29
  61.5 70.8 %reduce-scatter.8.cloned.1.call-start = ((), (), s32[]{:S(2)}) async-start(), calls=%async_computation.5 | async-start | bytes 1966080 | tf_op jit(solution)/shard_map/reduce_scatter | solution.py:30
  106.1 92.5 %all-gather.6.cloned.1.call-start = ((), (), s32[]{:S(2)}) async-start(), calls=%async_computation.6 | async-start | bytes 2359296 | tf_op jit(solution)/shard_map/all_gather | solution.py:35
  169.2 54.5 %all-gather.8.cloned.1.call-start = ((), (), s32[]{:S(2)}) async-start(), calls=%async_computation.7 | async-start | bytes 4718592 | tf_op jit(solution)/shard_map/all_gather | solution.py:36
  232.4 1.4 copy-start.1
  232.4 1.8 copy-start.8
  232.4 2.3 copy-start.9
  232.4 2.7 copy-start.10
  238.9 6.6 %copy-start.7 = (f32[2,1536,128]{2,1,0:T(8,128)S(1)}, f32[2,1536,128]{2,1,0:T(8,128)}, u32[]{:S(2)}) copy-start(f32[2,1536,128]{2,1,0:T(8,128)} %param.21) | copy-start | bytes 4718596
  238.9 21.1 %collective-permute-start.3 = (bf16[1,118,1536]{2,1,0:T(8,128)(2,1)S(1)}, bf16[1,118,1536]{2,1,0:T(8,128)(2,1)S(1)}, u32[]{:S(2)}, u32[]{:S(2)}) collective-permute-start(bf16[1,118,1536]{2,1,0:T(8,128)(2,1)S(1)} %get-tuple-element.76), channel_id=1, source_target_pairs={{0,5},{1,0},{4,1},{5,4},{2,7},{3,2},{6,3},{7,6},{8,13},{9,8},{12,9... | collective-permute-start | bytes 1087496 | tf_op jit(solution)/shard_map/ppermute | solution.py:62
  239.8 20.2 %collective-permute-start.2 = (bf16[1,118,1536]{2,1,0:T(8,128)(2,1)S(1)}, bf16[1,118,1536]{2,1,0:T(8,128)(2,1)S(1)}, u32[]{:S(2)}, u32[]{:S(2)}) collective-permute-start(bf16[1,118,1536]{2,1,0:T(8,128)(2,1)S(1)} %get-tuple-element.77), channel_id=1, source_target_pairs={{0,1},{1,4},{4,5},{5,0},{2,3},{3,6},{6,7},{7,2},{8,9},{9,12},{12,1... | collective-permute-start | bytes 1087496 | tf_op jit(solution)/shard_map/ppermute | solution.py:61
  241.0 4.5 %copy-start.5 = (f32[2,1536,128]{2,1,0:T(8,128)S(1)}, f32[2,1536,128]{2,1,0:T(8,128)}, u32[]{:S(2)}) copy-start(f32[2,1536,128]{2,1,0:T(8,128)} %param.15) | copy-start | bytes 4718596
  241.0 4.5 %copy-start.6 = (f32[2,1536,128]{2,1,0:T(8,128)S(1)}, f32[2,1536,128]{2,1,0:T(8,128)}, u32[]{:S(2)}) copy-start(f32[2,1536,128]{2,1,0:T(8,128)} %param.18) | copy-start | bytes 4718596
  243.2 2.2 copy-start
  245.5 5.2 %copy-start.2 = (f32[512,1536]{1,0:T(8,128)S(1)}, f32[512,1536]{1,0:T(8,128)}, u32[]{:S(2)}) copy-start(f32[512,1536]{1,0:T(8,128)} %param.17) | copy-start | bytes 9437188
  245.5 5.2 %copy-start.3 = (f32[512,1536]{1,0:T(8,128)S(1)}, f32[512,1536]{1,0:T(8,128)}, u32[]{:S(2)}) copy-start(f32[512,1536]{1,0:T(8,128)} %param.20) | copy-start | bytes 9437188
  245.5 5.4 %copy-start.4 = (f32[512,1536]{1,0:T(8,128)S(1)}, f32[512,1536]{1,0:T(8,128)}, u32[]{:S(2)}) copy-start(f32[512,1536]{1,0:T(8,128)} %param.23) | copy-start | bytes 9437188
  248.6 14.5 %collective-permute-start.1 = (bf16[1,1536,128]{2,1,0:T(8,128)(2,1)S(1)}, bf16[1,1536,128]{2,1,0:T(8,128)(2,1)S(1)}, u32[]{:S(2)}, u32[]{:S(2)}) collective-permute-start(bf16[1,1536,128]{2,1,0:T(8,128)(2,1)S(1)} %get-tuple-element.74), channel_id=1, source_target_pairs={{0,5},{1,0},{4,1},{5,4},{2,7},{3,2},{6,3},{7,6},{8,13},{9,8},{12,9... | collective-permute-start | bytes 1179656 | tf_op jit(solution)/shard_map/ppermute | solution.py:62
  250.7 12.4 %collective-permute-start = (bf16[1,1536,128]{2,1,0:T(8,128)(2,1)S(1)}, bf16[1,1536,128]{2,1,0:T(8,128)(2,1)S(1)}, u32[]{:S(2)}, u32[]{:S(2)}) collective-permute-start(bf16[1,1536,128]{2,1,0:T(8,128)(2,1)S(1)} %get-tuple-element.75), channel_id=1, source_target_pairs={{0,1},{1,4},{4,5},{5,0},{2,3},{3,6},{6,7},{7,2},{8,9},{9,12},{12,1... | collective-permute-start | bytes 1179656 | tf_op jit(solution)/shard_map/ppermute | solution.py:61
  256.7 22.8 %collective-permute-start.5 = (bf16[256,1536]{1,0:T(8,128)(2,1)S(1)}, bf16[256,1536]{1,0:T(8,128)(2,1)S(1)}, u32[]{:S(2)}, u32[]{:S(2)}) collective-permute-start(bf16[256,1536]{1,0:T(8,128)(2,1)S(1)} %get-tuple-element.68), channel_id=1, source_target_pairs={{0,5},{1,0},{4,1},{5,4},{2,7},{3,2},{6,3},{7,6},{8,13},{9,8},{12,9... | collective-permute-start | bytes 2359304 | tf_op jit(solution)/shard_map/ppermute | solution.py:62
  260.0 19.4 %collective-permute-start.4 = (bf16[256,1536]{1,0:T(8,128)(2,1)S(1)}, bf16[256,1536]{1,0:T(8,128)(2,1)S(1)}, u32[]{:S(2)}, u32[]{:S(2)}) collective-permute-start(bf16[256,1536]{1,0:T(8,128)(2,1)S(1)} %get-tuple-element.69), channel_id=1, source_target_pairs={{0,1},{1,4},{4,5},{5,0},{2,3},{3,6},{6,7},{7,2},{8,9},{9,12},{12,1... | collective-permute-start | bytes 2359304 | tf_op jit(solution)/shard_map/ppermute | solution.py:61
Sparse Core Ops, SparseCore 0:
  41.9 19.5 reduce-scatter.3
  64.0 39.6 reduce-scatter.5
  106.8 25.4 reduce-scatter.7
  169.3 29.2 all-gather.5
  200.2 14.2 all-gather.7

commit v8 on v7

--- a/solution.py
+++ b/solution.py
@@ -31,11 +31,12 @@
     part = lax.psum(part, "z").astype(jnp.bfloat16)
     wide = part.astype(jnp.float32)
     squares = jnp.sum(wide * wide)
+    for axis in ("core", XRING, "y"):
+        squares = lax.psum(squares, axis)
     part = lax.all_gather(part, "y", axis=0)
     part = lax.all_gather(part, "xh", axis=0)
+    part, squares = lax.optimization_barrier((part, squares))
     part = lax.all_gather(part, "core", axis=0)
-    for axis in ("y", XRING, "core"):
-        squares = lax.psum(squares, axis)
     return part, squares
 
 

time: 290 us -> 283 us (0.976)
  waiting for transfers between devices: 132 us -> 123 us
    all_gather x1, waiting for transfers between devices: 29.4 us -> 4.55 us  [reduce_flat(): part = lax.all_gather(part, 'xh', axis=0)]
    all_gather x1, waiting for transfers between devices: 0.02 us -> 15 us  [reduce_flat(): part = lax.all_gather(part, 'core', axis=0)]
    ppermute x3, starting transfers between devices: 6.35 us -> 9.45 us  [swap_halves(): lax.ppermute(second, XRING, perm=[(p, (p - 1) % n) for p in range(n)])]
  transfers between devices with their start and end apart: 11 -> 11, of which waited for: 5 -> 6; matrix products, arithmetic and copies ran while one was open for 6% -> 7% of each run, Pallas kernels for 0% -> 0%
where the time goes in v8:
time: 283 us; the launch traced here: 282 us
  waiting for transfers between devices  123 us (43%)
  blocking collectives  61.1 us (22%)
  other arithmetic  39.6 us (14%)
  local copies, waits for them, and re-layouts  33.3 us (12%)
  between operations  15.9 us (6%)
  starting transfers between devices  9.66 us (3%)
    reduce_scatter x1, waiting for transfers between devices, reduce_flat(): part = lax.psum_scatter(part, XRING, scatter_dimension=0, tiled=False)  42.1 us
    reduce_scatter x1, waiting for transfers between devices, reduce_flat(): lax.psum_scatter(part.astype(jnp.float32), 'y', scatter_dimension=0, tile...  26.1 us
    psum x3, blocking collectives, reduce_flat(): squares = lax.psum(squares, axis)  24.2 us
    psum x1, blocking collectives, reduce_flat(): part = lax.psum(part, 'z').astype(jnp.bfloat16)  21.8 us
    reduce_scatter x1, waiting for transfers between devices, reduce_flat(): lax.psum_scatter(buf.astype(jnp.bfloat16), 'core', scatter_dimension=0, t...  19.7 us
    all_gather x1, blocking collectives, reduce_flat(): part = lax.all_gather(part, 'y', axis=0)  15.1 us
    all_gather x1, waiting for transfers between devices, reduce_flat(): part = lax.all_gather(part, 'core', axis=0)  15 us
    ppermute x3, waiting for transfers between devices, swap_halves(): lax.ppermute(first, XRING, perm=[(p, (p + 1) % n) for p in range(n)])  15 us
  transfers between devices with their start and end apart: 11, of which 6 were waited for; matrix products, arithmetic and copies ran while one was open for 7% of the time, Pallas kernels for 0%

profile of v8, /device:TPU:0, one launch (start us, length us, event | category | flops | bytes accessed | tf_op | source)
XLA Modules:
  0.0 282.1 jit_solution(11950851051112908496)
XLA Ops:
  7.2 0.0 reduce-scatter.4.cloned.1.call-start
  7.2 6.5 %reduce = bf16[2,118,3072]{2,0,1:T(2,128)(2,1)S(1)} reduce(bf16[2,2,118,3072]{3,1,2,0:T(2,128)(2,1)} %param.13, bf16[]{:T(256)} %constant.19.clone.1), dimensions={0}, to_apply=%region_0.0.clone | reduce | flops 724992 | bytes 4349954 | tf_op jit(solution)/shard_map/reduce_sum | solution.py:105
  13.7 1.2 pad.5
  14.9 1.2 reshape.106
  16.1 0.4 copy.53
  16.6 1.4 copy.54
  18.0 2.9 %reduce.1 = bf16[2,3072,128]{2,1,0:T(8,128)(2,1)S(1)} reduce(bf16[2,2,3072,128]{3,2,1,0:T(8,128)(2,1)} %param.12, bf16[]{:T(256)} %constant.19.clone.1), dimensions={0}, to_apply=%region_1.0.clone | reduce | flops 786432 | bytes 4718594 | tf_op jit(solution)/shard_map/reduce_sum | solution.py:100
  20.9 1.4 copy.55
  22.4 6.1 %reduce.2 = bf16[1024,1536]{1,0:T(8,128)(2,1)S(1)} reduce(bf16[2,1024,1536]{2,1,0:T(8,128)(2,1)} %param.14, bf16[]{:T(256)} %constant.19.clone.1), dimensions={0}, to_apply=%region_2.3.clone | reduce | flops 1572864 | bytes 9437186 | tf_op jit(solution)/shard_map/reduce_sum | solution.py:111
  28.4 3.7 %reshape.83 = bf16[64,16,12,128]{3,2,1,0:T(8,128)(2,1)} reshape(bf16[1024,1536]{1,0:T(8,128)(2,1)S(1)} %reduce.2) | data formatting | bytes 6291456 | tf_op jit(solution)/shard_map/reshape | solution.py:48
  32.1 3.0 %copy.56 = bf16[64,12,16,128]{3,2,1,0:T(8,128)(2,1)S(1)} copy(bf16[64,12,16,128]{3,1,2,0:T(8,128)(2,1)} %bitcast.44) | data formatting | bytes 6291456 | tf_op jit(solution)/shard_map/transpose | solution.py:50
  35.1 2.5 pad_maximum_fusion
  37.6 4.1 %copy.57 = bf16[2,2,2,4,48,16,128]{6,5,4,3,2,1,0:T(8,128)(2,1)} copy(bf16[2,2,2,4,48,16,128]{6,5,4,3,1,0,2:T(8,128)(2,1)S(1)} %bitcast.43) | data formatting | bytes 12582912 | tf_op jit(solution)/shard_map/convert_element_type | solution.py:28
  41.7 0.0 reduce-scatter.4.cloned.1.call-update
  41.7 0.0 reduce-scatter.6.cloned.1.call-start
  41.8 19.7 %reduce-scatter.4.cloned.1.call-done = bf16[1,4,4,48,16,128]{5,4,3,2,1,0:T(8,128)(2,1)} async-done(((bf16[2,4,4,48,16,128]{5,4,3,2,1,0:T(8,128)(2,1)}), bf16[1,4,4,48,16,128]{5,4,3,2,1,0:T(8,128)(2,1)}) %reduce-scatter.4.cloned.1.call-update) | async-done | bytes 3145744 | tf_op jit(solution)/shard_map/reduce_scatter | solution.py:28
  61.5 0.0 reduce-scatter.6.cloned.1.call-update
  61.5 0.0 reduce-scatter.8.cloned.1.call-start
  61.5 42.1 %reduce-scatter.6.cloned.1.call-done = bf16[1,4,48,16,128]{4,3,2,1,0:T(8,128)(2,1)} async-done(((bf16[4,4,48,16,128]{4,3,2,1,0:T(8,128)(2,1)}), bf16[1,4,48,16,128]{4,3,2,1,0:T(8,128)(2,1)}) %reduce-scatter.6.cloned.1.call-update) | async-done | bytes 786448 | tf_op jit(solution)/shard_map/reduce_scatter | solution.py:29
  103.7 2.4 bitcast_convert_fusion
  106.1 0.0 all-gather.6.cloned.1.call-start
  106.2 26.1 %reduce-scatter.8.cloned.1.call-done = f32[1,48,16,128]{3,2,1,0:T(8,128)} async-done(((f32[4,48,16,128]{3,2,1,0:T(8,128)}), f32[1,48,16,128]{3,2,1,0:T(8,128)}) %reduce-scatter.8.cloned.1.call-update) | async-done | bytes 393232 | tf_op jit(solution)/shard_map/reduce_scatter | solution.py:30
  132.3 21.8 %all-reduce.2 = bf16[48,16,128]{2,1,0:T(8,128)(2,1)S(1)} all-reduce(f32[48,16,128]{2,1,0:T(8,128)} %bitcast.58), channel_id=1, replica_groups=mesh['z'=4,'y'=4,'xh'=2,'core'=2,'shard'=2] {'z'}, use_global_device_ids=true, to_apply=%region_6.7 | all-reduce | flops 98304 | bytes 589824 | tf_op jit(solution)/shard_map/psum | solution.py:31
  154.1 15.1 %all-gather = bf16[192,16,128]{2,1,0:T(8,128)(2,1)} all-gather(bf16[48,16,128]{2,1,0:T(8,128)(2,1)S(1)} %all-reduce.2), channel_id=2, replica_groups=mesh['z'=4,'y'=4,'xh'=2,'core'=2,'shard'=2] {'y'}, dimensions={0}, use_global_device_ids=true | all-gather | bytes 983040 | tf_op jit(solution)/shard_map/all_gather | solution.py:36
  169.2 0.0 all-gather.6.cloned.1.call-update
  169.2 0.0 all-gather.8.cloned.1.call-start
  169.3 0.7 multiply_reduce_fusion
  170.0 3.1 %psum.29 = f32[]{:T(128)} all-reduce(f32[]{:T(128)} %multiply_reduce_fusion), channel_id=1, replica_groups=mesh['z'=4,'y'=4,'xh'=2,'core'=2,'shard'=2] {'core'}, use_global_device_ids=true, to_apply=%region_8.9 | all-reduce | flops 1 | bytes 8 | tf_op jit(solution)/shard_map/psum | solution.py:35
  173.0 11.4 %psum.30 = f32[]{:T(128)} all-reduce(f32[]{:T(128)} %psum.29), channel_id=1, replica_groups=mesh['z'=4,'y'=4,'xh'=2,'core'=2,'shard'=2] {'xh','shard'}, use_global_device_ids=true, to_apply=%region_9.10 | all-reduce | flops 1 | bytes 8 | tf_op jit(solution)/shard_map/psum | solution.py:35
  184.4 9.8 %psum.31 = f32[]{:T(128)} all-reduce(f32[]{:T(128)} %psum.30), channel_id=1, replica_groups=mesh['z'=4,'y'=4,'xh'=2,'core'=2,'shard'=2] {'y'}, use_global_device_ids=true, to_apply=%region_10.11 | all-reduce | flops 1 | bytes 8 | tf_op jit(solution)/shard_map/psum | solution.py:35
  194.2 4.5 %all-gather.6.cloned.1.call-done = bf16[8,48,16,128]{3,2,1,0:T(8,128)(2,1)} async-done(((bf16[4,48,16,128]{3,2,1,0:T(8,128)(2,1)}), bf16[8,48,16,128]{3,2,1,0:T(8,128)(2,1)}) %all-gather.6.cloned.1.call-update) | async-done | bytes 1572880 | tf_op jit(solution)/shard_map/all_gather | solution.py:37
  199.5 15.0 %all-gather.8.cloned.1.call-done = bf16[4,4,48,16,128]{4,3,2,1,0:T(8,128)(2,1)} async-done(((bf16[2,4,48,16,128]{4,3,2,1,0:T(8,128)(2,1)}), bf16[4,4,48,16,128]{4,3,2,1,0:T(8,128)(2,1)}) %all-gather.8.cloned.1.call-update) | async-done | bytes 3145744 | tf_op jit(solution)/shard_map/all_gather | solution.py:39
  214.5 2.5 convert_multiply_fusion
  217.0 0.3 slice_multiply_fusion
  217.3 1.5 fusion.13
  218.8 1.8 copy.59
  220.6 2.6 reshape.86
  223.2 1.3 copy.63
  224.5 0.1 copy-done.1
  224.6 0.4 copy-done.8
  225.0 0.4 copy-done.9
  225.4 0.4 copy-done.10
  225.9 1.5 fusion.8
  227.4 2.2 copy.64
  229.6 2.9 %collective-permute-start.3 = (bf16[1,118,1536]{2,1,0:T(8,128)(2,1)S(1)}, bf16[1,118,1536]{2,1,0:T(8,128)(2,1)S(1)}, u32[]{:S(2)}, u32[]{:S(2)}) collective-permute-start(bf16[1,118,1536]{2,1,0:T(8,128)(2,1)S(1)} %get-tuple-element.80), channel_id=1, source_target_pairs={{0,5},{1,0},{4,1},{5,4},{2,7},{3,2},{6,3},{7,6},{8,13},{9,8},{12,9... | collective-permute-start | bytes 1087496 | tf_op jit(solution)/shard_map/ppermute | solution.py:63
  232.5 2.2 copy.65
  234.7 2.2 copy.66
  237.0 3.0 %fusion.11 = (bf16[2,1536,128]{2,1,0:T(8,128)(2,1)S(1)}, f32[2,1536,128]{2,1,0:T(8,128)}, f32[2,1536,128]{2,1,0:T(8,128)}, f32[2,1536,128]{2,1,0:T(8,128)}) fusion(f32[2,1536,128]{2,1,0:T(8,128)S(1)} %copy-done.5, f32[2,1536,128]{2,1,0:T(8,128)S(1)} %bitcast.54, f32[2,1536,128]{2,1,0:T(8,128)S(1)} %copy-done.6, f32[2,1536,128]{2,1,0:T(8,128)S(1)} %copy-done.7), kind=kLoop, calls=%fused_computation.39 | loop fusion | flops 6291456 | bytes 11796480 | tf_op jit(solution)/shard_map/convert_element_type | solution.py:141
  240.0 0.1 fusion.15
  240.1 3.3 %collective-permute-start.1 = (bf16[1,1536,128]{2,1,0:T(8,128)(2,1)S(1)}, bf16[1,1536,128]{2,1,0:T(8,128)(2,1)S(1)}, u32[]{:S(2)}, u32[]{:S(2)}) collective-permute-start(bf16[1,1536,128]{2,1,0:T(8,128)(2,1)S(1)} %get-tuple-element.78), channel_id=1, source_target_pairs={{0,5},{1,0},{4,1},{5,4},{2,7},{3,2},{6,3},{7,6},{8,13},{9,8},{12,9... | collective-permute-start | bytes 1179656 | tf_op jit(solution)/shard_map/ppermute | solution.py:63
  243.4 5.9 %fusion.5 = (bf16[512,1536]{1,0:T(8,128)(2,1)S(1)}, f32[512,1536]{1,0:T(8,128)}, f32[512,1536]{1,0:T(8,128)}, f32[512,1536]{1,0:T(8,128)}) fusion(f32[512,1536]{1,0:T(8,128)S(1)} %copy-done.2, f32[64,8,12,128]{3,2,1,0:T(8,128)S(1)} %bitcast.45, f32[512,1536]{1,0:T(8,128)S(1)} %copy-done.3, f32[512,1536]{1,0:T(8,128)S(1)} %copy-done.4), kind=kLoop, calls=%fused_computation.37 | loop fusion | flops 12582912 | bytes 23592960 | tf_op jit(solution)/shard_map/convert_element_type | solution.py:143
  249.3 0.1 fusion.14
  249.4 3.3 %collective-permute-start.5 = (bf16[256,1536]{1,0:T(8,128)(2,1)S(1)}, bf16[256,1536]{1,0:T(8,128)(2,1)S(1)}, u32[]{:S(2)}, u32[]{:S(2)}) collective-permute-start(bf16[256,1536]{1,0:T(8,128)(2,1)S(1)} %get-tuple-element.72), channel_id=1, source_target_pairs={{0,5},{1,0},{4,1},{5,4},{2,7},{3,2},{6,3},{7,6},{8,13},{9,8},{12,9... | collective-permute-start | bytes 2359304 | tf_op jit(solution)/shard_map/ppermute | solution.py:63
  252.8 0.2 broadcast_select_fusion.5
  252.9 0.2 pad_maximum_fusion.3
  253.1 2.6 copy.67
  255.8 0.1 constant_dynamic-update-slice_fusion
  255.8 0.2 broadcast_select_fusion.3
  256.0 1.2 pad_maximum_fusion.2
  257.3 15.0 %collective-permute-done.4 = bf16[256,1536]{1,0:T(8,128)(2,1)S(1)} collective-permute-done((bf16[256,1536]{1,0:T(8,128)(2,1)S(1)}, bf16[256,1536]{1,0:T(8,128)(2,1)S(1)}, u32[]{:S(2)}, u32[]{:S(2)}) %collective-permute-start.4) | collective-permute-done | bytes 786464 | tf_op jit(solution)/shard_map/ppermute | solution.py:62
  272.2 0.1 constant_dynamic-update-slice_fusion.5
  272.3 0.1 constant_dynamic-update-slice_fusion.4
  272.4 0.2 broadcast_select_fusion.1
  272.6 1.9 pad_maximum_fusion.1
  (32 shorter events, 0.2 us)
Async XLA Ops:
  7.2 54.3 %reduce-scatter.4.cloned.1.call-start = ((), (), s32[]{:S(2)}) async-start(), calls=%async_computation.3 | async-start | bytes 9437184 | tf_op jit(solution)/shard_map/reduce_scatter | solution.py:28
  41.7 61.9 %reduce-scatter.6.cloned.1.call-start = ((), (), s32[]{:S(2)}) async-start(), calls=%async_computation.4 | async-start | bytes 3932160 | tf_op jit(solution)/shard_map/reduce_scatter | solution.py:29
  61.5 70.8 %reduce-scatter.8.cloned.1.call-start = ((), (), s32[]{:S(2)}) async-start(), calls=%async_computation.5 | async-start | bytes 1966080 | tf_op jit(solution)/shard_map/reduce_scatter | solution.py:30
  106.1 92.6 %all-gather.6.cloned.1.call-start = ((), (), s32[]{:S(2)}) async-start(), calls=%async_computation.6 | async-start | bytes 2359296 | tf_op jit(solution)/shard_map/all_gather | solution.py:37
  169.2 45.3 %all-gather.8.cloned.1.call-start = ((), (), s32[]{:S(2)}) async-start(), calls=%async_computation.7 | async-start | bytes 4718592 | tf_op jit(solution)/shard_map/all_gather | solution.py:39
  223.2 1.4 copy-start.1
  223.2 1.8 copy-start.8
  223.2 2.3 copy-start.9
  223.2 2.7 copy-start.10
  229.6 7.4 %copy-start.7 = (f32[2,1536,128]{2,1,0:T(8,128)S(1)}, f32[2,1536,128]{2,1,0:T(8,128)}, u32[]{:S(2)}) copy-start(f32[2,1536,128]{2,1,0:T(8,128)} %param.21) | copy-start | bytes 4718596
  229.6 23.1 %collective-permute-start.3 = (bf16[1,118,1536]{2,1,0:T(8,128)(2,1)S(1)}, bf16[1,118,1536]{2,1,0:T(8,128)(2,1)S(1)}, u32[]{:S(2)}, u32[]{:S(2)}) collective-permute-start(bf16[1,118,1536]{2,1,0:T(8,128)(2,1)S(1)} %get-tuple-element.80), channel_id=1, source_target_pairs={{0,5},{1,0},{4,1},{5,4},{2,7},{3,2},{6,3},{7,6},{8,13},{9,8},{12,9... | collective-permute-start | bytes 1087496 | tf_op jit(solution)/shard_map/ppermute | solution.py:63
  232.5 20.2 %collective-permute-start.2 = (bf16[1,118,1536]{2,1,0:T(8,128)(2,1)S(1)}, bf16[1,118,1536]{2,1,0:T(8,128)(2,1)S(1)}, u32[]{:S(2)}, u32[]{:S(2)}) collective-permute-start(bf16[1,118,1536]{2,1,0:T(8,128)(2,1)S(1)} %get-tuple-element.81), channel_id=1, source_target_pairs={{0,1},{1,4},{4,5},{5,0},{2,3},{3,6},{6,7},{7,2},{8,9},{9,12},{12,1... | collective-permute-start | bytes 1087496 | tf_op jit(solution)/shard_map/ppermute | solution.py:62
  232.5 4.5 %copy-start.5 = (f32[2,1536,128]{2,1,0:T(8,128)S(1)}, f32[2,1536,128]{2,1,0:T(8,128)}, u32[]{:S(2)}) copy-start(f32[2,1536,128]{2,1,0:T(8,128)} %param.15) | copy-start | bytes 4718596
  232.5 4.5 %copy-start.6 = (f32[2,1536,128]{2,1,0:T(8,128)S(1)}, f32[2,1536,128]{2,1,0:T(8,128)}, u32[]{:S(2)}) copy-start(f32[2,1536,128]{2,1,0:T(8,128)} %param.18) | copy-start | bytes 4718596
  234.7 2.2 copy-start
  237.0 6.4 %copy-start.2 = (f32[512,1536]{1,0:T(8,128)S(1)}, f32[512,1536]{1,0:T(8,128)}, u32[]{:S(2)}) copy-start(f32[512,1536]{1,0:T(8,128)} %param.17) | copy-start | bytes 9437188
  237.0 6.4 %copy-start.3 = (f32[512,1536]{1,0:T(8,128)S(1)}, f32[512,1536]{1,0:T(8,128)}, u32[]{:S(2)}) copy-start(f32[512,1536]{1,0:T(8,128)} %param.20) | copy-start | bytes 9437188
  237.0 6.4 %copy-start.4 = (f32[512,1536]{1,0:T(8,128)S(1)}, f32[512,1536]{1,0:T(8,128)}, u32[]{:S(2)}) copy-start(f32[512,1536]{1,0:T(8,128)} %param.23) | copy-start | bytes 9437188
  240.1 15.7 %collective-permute-start.1 = (bf16[1,1536,128]{2,1,0:T(8,128)(2,1)S(1)}, bf16[1,1536,128]{2,1,0:T(8,128)(2,1)S(1)}, u32[]{:S(2)}, u32[]{:S(2)}) collective-permute-start(bf16[1,1536,128]{2,1,0:T(8,128)(2,1)S(1)} %get-tuple-element.78), channel_id=1, source_target_pairs={{0,5},{1,0},{4,1},{5,4},{2,7},{3,2},{6,3},{7,6},{8,13},{9,8},{12,9... | collective-permute-start | bytes 1179656 | tf_op jit(solution)/shard_map/ppermute | solution.py:63
  243.4 12.4 %collective-permute-start = (bf16[1,1536,128]{2,1,0:T(8,128)(2,1)S(1)}, bf16[1,1536,128]{2,1,0:T(8,128)(2,1)S(1)}, u32[]{:S(2)}, u32[]{:S(2)}) collective-permute-start(bf16[1,1536,128]{2,1,0:T(8,128)(2,1)S(1)} %get-tuple-element.79), channel_id=1, source_target_pairs={{0,1},{1,4},{4,5},{5,0},{2,3},{3,6},{6,7},{7,2},{8,9},{9,12},{12,1... | collective-permute-start | bytes 1179656 | tf_op jit(solution)/shard_map/ppermute | solution.py:62
  249.4 22.9 %collective-permute-start.5 = (bf16[256,1536]{1,0:T(8,128)(2,1)S(1)}, bf16[256,1536]{1,0:T(8,128)(2,1)S(1)}, u32[]{:S(2)}, u32[]{:S(2)}) collective-permute-start(bf16[256,1536]{1,0:T(8,128)(2,1)S(1)} %get-tuple-element.72), channel_id=1, source_target_pairs={{0,5},{1,0},{4,1},{5,4},{2,7},{3,2},{6,3},{7,6},{8,13},{9,8},{12,9... | collective-permute-start | bytes 2359304 | tf_op jit(solution)/shard_map/ppermute | solution.py:63
  252.7 19.6 %collective-permute-start.4 = (bf16[256,1536]{1,0:T(8,128)(2,1)S(1)}, bf16[256,1536]{1,0:T(8,128)(2,1)S(1)}, u32[]{:S(2)}, u32[]{:S(2)}) collective-permute-start(bf16[256,1536]{1,0:T(8,128)(2,1)S(1)} %get-tuple-element.73), channel_id=1, source_target_pairs={{0,1},{1,4},{4,5},{5,0},{2,3},{3,6},{6,7},{7,2},{8,9},{9,12},{12,1... | collective-permute-start | bytes 2359304 | tf_op jit(solution)/shard_map/ppermute | solution.py:62
Sparse Core Ops, SparseCore 0:
  41.9 19.5 reduce-scatter.3
  64.0 39.6 reduce-scatter.5
  106.8 25.4 reduce-scatter.7
  169.3 29.3 all-gather.5
  200.3 14.1 all-gather.7

commit v9 on v8

--- a/solution.py
+++ b/solution.py
@@ -25,7 +25,12 @@
 
 
 def reduce_flat(buf):
-    part = lax.psum_scatter(buf.astype(jnp.bfloat16), "core", scatter_dimension=0, tiled=False)
+    me = lax.axis_index("core")
+    flip = [(0, 1), (1, 0)]
+    mine = lax.dynamic_index_in_dim(buf, me, 0, keepdims=False)
+    theirs = lax.dynamic_index_in_dim(buf, 1 - me, 0, keepdims=False)
+    got = lax.ppermute(theirs.astype(jnp.bfloat16), "core", perm=flip)
+    part = (mine + got.astype(jnp.float32)).astype(jnp.bfloat16)
     part = lax.psum_scatter(part, XRING, scatter_dimension=0, tiled=False)
     part = lax.psum_scatter(part.astype(jnp.float32), "y", scatter_dimension=0, tiled=False)
     part = lax.psum(part, "z").astype(jnp.bfloat16)
@@ -36,7 +41,9 @@
     part = lax.all_gather(part, "y", axis=0)
     part = lax.all_gather(part, "xh", axis=0)
     part, squares = lax.optimization_barrier((part, squares))
-    part = lax.all_gather(part, "core", axis=0)
+    other = lax.ppermute(part, "core", perm=flip)
+    first = me == 0
+    part = jnp.stack([jnp.where(first, part, other), jnp.where(first, other, part)])
     return part, squares
 
 

time: 283 us -> 286 us (1.011)
  waiting for transfers between devices: 123 us -> 90.9 us
  local copies, waits for them, and re-layouts: 33.3 us -> 64.4 us
  other arithmetic: 39.6 us -> 46.4 us
    reduce_scatter x1 -> x0, waiting for transfers between devices: 19.7 us -> none  [reduce_flat(): lax.psum_scatter(buf.astype(jnp.bfloat16), 'core', scatter_dimension=0, t...]
    all_gather x1 -> x0, waiting for transfers between devices: 15 us -> none  [reduce_flat(): part = lax.all_gather(part, 'core', axis=0)]
    transpose x0 -> x1, local copies, waits for them, and re-layouts: none -> 10.4 us  [on_device(): jnp.transpose(buf, (1, 2, 0, 3, 4, 5, 6))]
    transpose x2, local copies, waits for them, and re-layouts: 3.4 us -> 12.2 us  [to_tiles(): return jnp.swapaxes(a, n + 1, n + 2)]
    ppermute x0 -> x2, waiting for transfers between devices: none -> 8.66 us  [the longest x1 5.78 us: reduce_flat(): got = lax.ppermute(theirs.astype(jnp.bfloat16), 'core', perm=flip)]
    reshape x2, local copies, waits for them, and re-layouts: 4.89 us -> 12.1 us  [to_tiles(): a = a.reshape(*lead, r // TR, TR, c // 128, 128)]
    convert_element_type x0 -> x1, other arithmetic: none -> 6.15 us  [reduce_flat(): part = (mine + got.astype(jnp.float32)).astype(jnp.bfloat16)]
    ppermute x3, waiting for transfers between devices: 15 us -> 9.01 us  [swap_halves(): lax.ppermute(first, XRING, perm=[(p, (p + 1) % n) for p in range(n)])]
  transfers between devices with their start and end apart: 11 -> 11, of which waited for: 6 -> 8; matrix products, arithmetic and copies ran while one was open for 7% -> 9% of each run, Pallas kernels for 0% -> 0%
where the time goes in v9:
time: 286 us
  waiting for transfers between devices  90.9 us (32%)
  local copies, waits for them, and re-layouts  64.4 us (23%)
  blocking collectives  61.1 us (21%)
  other arithmetic  46.4 us (16%)
  between operations  15.9 us (6%)
  starting transfers between devices  6.82 us (2%)
    reduce_scatter x1, waiting for transfers between devices, reduce_flat(): part = lax.psum_scatter(part, XRING, scatter_dimension=0, tiled=False)  40.8 us
    reduce_scatter x1, waiting for transfers between devices, reduce_flat(): lax.psum_scatter(part.astype(jnp.float32), 'y', scatter_dimension=0, tile...  26 us
    psum x3, blocking collectives, reduce_flat(): squares = lax.psum(squares, axis)  24.2 us
    psum x1, blocking collectives, reduce_flat(): part = lax.psum(part, 'z').astype(jnp.bfloat16)  21.8 us
    all_gather x1, blocking collectives, reduce_flat(): part = lax.all_gather(part, 'y', axis=0)  15 us
    unnamed x27, local copies, waits for them, and re-layouts  14.7 us
    transpose x2, local copies, waits for them, and re-layouts, to_tiles(): return jnp.swapaxes(a, n + 1, n + 2)  12.2 us
    reshape x2, local copies, waits for them, and re-layouts, to_tiles(): a = a.reshape(*lead, r // TR, TR, c // 128, 128)  12.1 us
  transfers between devices with their start and end apart: 11, of which 8 were waited for; matrix products, arithmetic and copies ran while one was open for 9% of the time, Pallas kernels for 0%

profile of v9, /device:TPU:0, one launch (start us, length us, event | category | flops | bytes accessed | tf_op | source)
XLA Modules:
  0.0 285.6 jit_solution(18009807084112186419)
XLA Ops:
  7.2 7.2 %convert_reduce_fusion = f32[1024,1536]{1,0:T(8,128)} fusion(bf16[2,1024,1536]{2,1,0:T(8,128)(2,1)} %param.14), kind=kLoop, calls=%fused_computation.1 | loop fusion | flops 4718592 | bytes 12582912 | tf_op jit(solution)/shard_map/reduce_sum | solution.py:118
  14.5 8.4 %reshape.80 = f32[64,16,12,128]{3,2,1,0:T(8,128)} reshape(f32[1024,1536]{1,0:T(8,128)} %convert_reduce_fusion) | data formatting | bytes 12582912 | tf_op jit(solution)/shard_map/reshape | solution.py:55
  22.9 9.2 %copy.56 = f32[64,12,16,128]{3,2,1,0:T(8,128)} copy(f32[64,12,16,128]{3,1,2,0:T(8,128)} %bitcast.61) | data formatting | bytes 12582912 | tf_op jit(solution)/shard_map/transpose | solution.py:57
  32.0 5.1 %convert_reduce_fusion.2 = f32[2,118,3072]{2,0,1:T(2,128)} fusion(bf16[2,2,118,3072]{3,1,2,0:T(2,128)(2,1)S(1)} %copy-done.4), kind=kLoop, calls=%fused_computation.7 | loop fusion | flops 2174976 | bytes 5799936 | tf_op jit(solution)/shard_map/reduce_sum | solution.py:112
  37.2 2.9 %pad.4 = f32[2,128,3072]{2,0,1:T(2,128)S(1)} pad(f32[2,118,3072]{2,0,1:T(2,128)} %convert_reduce_fusion.2, f32[]{:T(128)} %constant.20.clone.1), padding=0_0x0_10x0_0 | pad | bytes 6045700 | tf_op jit(solution)/shard_map/jit(_pad)/pad | solution.py:113
  40.0 3.7 %reshape.90 = f32[2,8,16,24,128]{4,3,0,2,1:T(8,128)} reshape(f32[2,128,3072]{2,0,1:T(2,128)S(1)} %pad.4) | data formatting | bytes 6291456 | tf_op jit(solution)/shard_map/reshape | solution.py:55
  43.7 3.1 %copy.53 = f32[2,8,24,16,128]{4,3,2,1,0:T(8,128)S(1)} copy(f32[2,8,24,16,128]{4,2,0,3,1:T(8,128)} %bitcast.70) | data formatting | bytes 6291456 | tf_op jit(solution)/shard_map/transpose | solution.py:57
  46.8 0.3 copy.54
  47.2 0.5 convert_reduce_fusion.1
  47.7 0.2 copy.55
  47.9 1.1 slice-done
  49.0 0.8 slice-done.1
  49.7 4.8 %pad_maximum_fusion = f32[2,768,16,128]{3,2,1,0:T(8,128)} fusion(f32[2,384,16,128]{3,2,1,0:T(8,128)S(1)} %bitcast.65, f32[2,192,16,128]{3,2,1,0:T(8,128)S(1)} %bitcast.68, f32[2,192,16,128]{3,2,1,0:T(8,128)S(1)} %bitcast.67), kind=kLoop, calls=%fused_computation | loop fusion | flops 6291456 | bytes 25165824 | tf_op jit(solution)/shard_map/concatenate | solution.py:127
  54.5 10.4 %copy.57 = f32[2,2,2,4,48,16,128]{6,5,4,3,2,1,0:T(8,128)} copy(f32[2,2,2,4,48,16,128]{6,5,4,3,1,0,2:T(8,128)} %bitcast.58) | data formatting | bytes 25165824 | tf_op jit(solution)/shard_map/transpose | solution.py:129
  64.9 3.3 %fusion.2 = bf16[4,4,48,16,128]{4,3,2,1,0:T(8,128)(2,1)S(1)} fusion(f32[2,4,4,48,16,128]{5,4,3,2,1,0:T(8,128)} %bitcast.59, s32[]{:T(128)S(6)} %select_n.56), kind=kLoop, calls=%fused_computation.10 | loop fusion | bytes 6291460 | tf_op jit(solution)/shard_map/convert_element_type | solution.py:32
  68.2 0.1 collective-permute-start
  68.3 5.8 %collective-permute-done = bf16[4,4,48,16,128]{4,3,2,1,0:T(8,128)(2,1)} collective-permute-done((bf16[4,4,48,16,128]{4,3,2,1,0:T(8,128)(2,1)S(1)}, bf16[4,4,48,16,128]{4,3,2,1,0:T(8,128)(2,1)}, u32[]{:S(2)}, u32[]{:S(2)}) %collective-permute-start) | collective-permute-done | bytes 3145760 | tf_op jit(solution)/shard_map/ppermute | solution.py:32
  74.1 6.2 %fusion = bf16[4,4,48,16,128]{4,3,2,1,0:T(8,128)(2,1)} fusion(bf16[4,4,48,16,128]{4,3,2,1,0:T(8,128)(2,1)} %collective-permute-done, f32[2,4,4,48,16,128]{5,4,3,2,1,0:T(8,128)} %bitcast.60, s32[]{:T(128)S(6)} %select_n.55), kind=kLoop, calls=%fused_computation.3 | loop fusion | flops 4718592 | bytes 12582916 | tf_op jit(solution)/shard_map/convert_element_type | solution.py:33
  80.3 40.8 %reduce-scatter.3.cloned.1.call-done = bf16[1,4,48,16,128]{4,3,2,1,0:T(8,128)(2,1)} async-done(((bf16[4,4,48,16,128]{4,3,2,1,0:T(8,128)(2,1)}), bf16[1,4,48,16,128]{4,3,2,1,0:T(8,128)(2,1)}) %reduce-scatter.3.cloned.1.call-update) | async-done | bytes 786448 | tf_op jit(solution)/shard_map/reduce_scatter | solution.py:34
  121.1 2.4 bitcast_convert_fusion
  123.6 26.0 %reduce-scatter.5.cloned.1.call-done = f32[1,48,16,128]{3,2,1,0:T(8,128)} async-done(((f32[4,48,16,128]{3,2,1,0:T(8,128)}), f32[1,48,16,128]{3,2,1,0:T(8,128)}) %reduce-scatter.5.cloned.1.call-update) | async-done | bytes 393232 | tf_op jit(solution)/shard_map/reduce_scatter | solution.py:35
  149.6 21.8 %all-reduce.2 = bf16[48,16,128]{2,1,0:T(8,128)(2,1)S(1)} all-reduce(f32[48,16,128]{2,1,0:T(8,128)} %bitcast.78), channel_id=1, replica_groups=mesh['z'=4,'y'=4,'xh'=2,'core'=2,'shard'=2] {'z'}, use_global_device_ids=true, to_apply=%region_5.6 | all-reduce | flops 98304 | bytes 589824 | tf_op jit(solution)/shard_map/psum | solution.py:36
  171.4 15.0 %all-gather = bf16[192,16,128]{2,1,0:T(8,128)(2,1)} all-gather(bf16[48,16,128]{2,1,0:T(8,128)(2,1)S(1)} %all-reduce.2), channel_id=2, replica_groups=mesh['z'=4,'y'=4,'xh'=2,'core'=2,'shard'=2] {'y'}, dimensions={0}, use_global_device_ids=true | all-gather | bytes 983040 | tf_op jit(solution)/shard_map/all_gather | solution.py:41
  186.5 0.7 multiply_reduce_fusion
  187.2 3.1 %psum.29 = f32[]{:T(128)} all-reduce(f32[]{:T(128)} %multiply_reduce_fusion), channel_id=1, replica_groups=mesh['z'=4,'y'=4,'xh'=2,'core'=2,'shard'=2] {'core'}, use_global_device_ids=true, to_apply=%region_7.8 | all-reduce | flops 1 | bytes 8 | tf_op jit(solution)/shard_map/psum | solution.py:40
  190.2 11.4 %psum.30 = f32[]{:T(128)} all-reduce(f32[]{:T(128)} %psum.29), channel_id=1, replica_groups=mesh['z'=4,'y'=4,'xh'=2,'core'=2,'shard'=2] {'xh','shard'}, use_global_device_ids=true, to_apply=%region_8.9 | all-reduce | flops 1 | bytes 8 | tf_op jit(solution)/shard_map/psum | solution.py:40
  201.7 9.7 %psum.31 = f32[]{:T(128)} all-reduce(f32[]{:T(128)} %psum.30), channel_id=1, replica_groups=mesh['z'=4,'y'=4,'xh'=2,'core'=2,'shard'=2] {'y'}, use_global_device_ids=true, to_apply=%region_9.10 | all-reduce | flops 1 | bytes 8 | tf_op jit(solution)/shard_map/psum | solution.py:40
  211.4 4.6 %all-gather.4.cloned.1.call-done = bf16[8,48,16,128]{3,2,1,0:T(8,128)(2,1)} async-done(((bf16[4,48,16,128]{3,2,1,0:T(8,128)(2,1)}), bf16[8,48,16,128]{3,2,1,0:T(8,128)(2,1)}) %all-gather.4.cloned.1.call-update) | async-done | bytes 1572880 | tf_op jit(solution)/shard_map/all_gather | solution.py:42
  216.7 2.9 %collective-permute-done.1 = bf16[2,4,48,16,128]{4,3,2,1,0:T(8,128)(2,1)S(1)} collective-permute-done((bf16[2,4,48,16,128]{4,3,2,1,0:T(8,128)(2,1)}, bf16[2,4,48,16,128]{4,3,2,1,0:T(8,128)(2,1)S(1)}, u32[]{:S(2)}, u32[]{:S(2)}) %collective-permute-start.1) | collective-permute-done | bytes 1572896 | tf_op jit(solution)/shard_map/ppermute | solution.py:44
  219.6 1.6 select_bitcast_fusion.1
  221.2 0.6 convert_multiply_fusion
  221.9 0.2 slice_multiply_fusion
  222.1 1.3 copy.63
  223.4 0.3 copy-done.2
  223.8 1.0 copy-done
  224.8 0.9 copy-done.1
  225.7 5.6 %fusion.8 = (bf16[512,1536]{1,0:T(8,128)(2,1)S(1)}, f32[512,1536]{1,0:T(8,128)}, f32[512,1536]{1,0:T(8,128)}, f32[512,1536]{1,0:T(8,128)}) fusion(f32[512,1536]{1,0:T(8,128)S(1)} %copy-done, f32[64,8,12,128]{3,2,1,0:T(8,128)S(1)} %bitcast.66, f32[512,1536]{1,0:T(8,128)S(1)} %copy-done.1, f32[512,1536]{1,0:T(8,128)S(1)} %copy-done.2), kind=kLoop, calls=%fused_computation.47 | loop fusion | flops 12582912 | bytes 23592960 | tf_op jit(solution)/shard_map/convert_element_type | solution.py:150
  231.3 1.3 fusion.18
  232.5 0.5 collective-permute-start.6
  233.0 2.8 collective-permute-start.7
  235.8 0.2 fusion.17
  236.0 1.8 copy.59
  237.8 2.6 reshape.85
  240.4 4.3 %fusion.11 = (bf16[2,118,1536]{2,1,0:T(8,128)(2,1)S(1)}, f32[2,118,1536]{2,1,0:T(8,128)S(1)}, f32[2,118,1536]{2,1,0:T(8,128)S(1)}, f32[2,118,1536]{2,1,0:T(8,128)S(1)}) fusion(f32[2,118,1536]{2,0,1:T(2,128)} %param.16, f32[2,128,1536]{2,1,0:T(8,128)} %reshape.85, f32[]{:T(128)S(6)} %min.3, f32[2,118,1536]{2,0,1:T(2,128)} %param.19, f32[2,118,1536]{2,0,1:T(2,128)} %param.22), kind=kLoop, calls=%fused_computation.48 | loop fusion | flops 6162432 | bytes 10874884 | tf_op jit(solution)/shard_map/convert_element_type | solution.py:149
  244.8 0.1 collective-permute-start.4
  244.8 3.2 %collective-permute-start.5 = (bf16[1,118,1536]{2,1,0:T(8,128)(2,1)S(1)}, bf16[1,118,1536]{2,1,0:T(8,128)(2,1)S(1)}, u32[]{:S(2)}, u32[]{:S(2)}) collective-permute-start(bf16[1,118,1536]{2,1,0:T(8,128)(2,1)S(1)} %get-tuple-element.82), channel_id=1, source_target_pairs={{0,5},{1,0},{4,1},{5,4},{2,7},{3,2},{6,3},{7,6},{8,13},{9,8},{12,9... | collective-permute-start | bytes 1087496 | tf_op jit(solution)/shard_map/ppermute | solution.py:70
  248.1 3.0 %fusion.14 = (bf16[2,1536,128]{2,1,0:T(8,128)(2,1)S(1)}, f32[2,1536,128]{2,1,0:T(8,128)}, f32[2,1536,128]{2,1,0:T(8,128)}, f32[2,1536,128]{2,1,0:T(8,128)}) fusion(f32[2,1536,128]{2,1,0:T(8,128)S(1)} %copy-done.5, f32[2,1536,128]{2,1,0:T(8,128)S(1)} %copy-done.6, f32[2,1536,128]{2,1,0:T(8,128)S(1)} %copy-done.7, f32[2,1536,128]{2,1,0:T(8,128)S(1)} %bitcast.74), kind=kLoop, calls=%fused_computation.49 | loop fusion | flops 6291456 | bytes 11796480 | tf_op jit(solution)/shard_map/convert_element_type | solution.py:148
  251.1 0.1 fusion.19
  251.1 0.1 collective-permute-start.2
  251.2 2.2 copy.64
  253.4 2.2 copy.65
  255.7 2.2 copy.66
  257.9 4.4 %collective-permute-done.4 = bf16[1,118,1536]{2,1,0:T(8,128)(2,1)S(1)} collective-permute-done((bf16[1,118,1536]{2,1,0:T(8,128)(2,1)S(1)}, bf16[1,118,1536]{2,1,0:T(8,128)(2,1)S(1)}, u32[]{:S(2)}, u32[]{:S(2)}) %collective-permute-start.4) | collective-permute-done | bytes 362528 | tf_op jit(solution)/shard_map/ppermute | solution.py:69
  262.3 0.1 broadcast_select_fusion.5
  262.4 0.2 pad_maximum_fusion.3
  262.6 2.6 copy.67
  265.2 4.7 %collective-permute-done.2 = bf16[1,1536,128]{2,1,0:T(8,128)(2,1)S(1)} collective-permute-done((bf16[1,1536,128]{2,1,0:T(8,128)(2,1)S(1)}, bf16[1,1536,128]{2,1,0:T(8,128)(2,1)S(1)}, u32[]{:S(2)}, u32[]{:S(2)}) %collective-permute-start.2) | collective-permute-done | bytes 393248 | tf_op jit(solution)/shard_map/ppermute | solution.py:69
  269.9 1.9 collective-permute-done.3
  271.8 0.2 broadcast_select_fusion.3
  272.0 1.2 pad_maximum_fusion.2
  273.3 1.2 constant_dynamic-update-slice_fusion.5
  274.5 1.2 constant_dynamic-update-slice_fusion.4
  275.7 0.4 broadcast_select_fusion.1
  276.1 1.9 pad_maximum_fusion.1
  (32 shorter events, 0.4 us)
Async XLA Ops:
  7.2 114.0 %reduce-scatter.3.cloned.1.call-start = ((), (), s32[]{:S(2)}) async-start(), calls=%async_computation.2 | async-start | bytes 3932160 | tf_op jit(solution)/shard_map/reduce_scatter | solution.py:34
  22.9 9.2 %copy-start.4 = (bf16[2,2,118,3072]{3,1,2,0:T(2,128)(2,1)S(1)}, bf16[2,2,118,3072]{3,1,2,0:T(2,128)(2,1)}, u32[]{:S(2)}) copy-start(bf16[2,2,118,3072]{3,1,2,0:T(2,128)(2,1)} %param.13) | copy-start | bytes 8699908
  43.7 3.4 %copy-start.3 = (bf16[2,2,3072,128]{3,2,1,0:T(8,128)(2,1)S(1)}, bf16[2,2,3072,128]{3,2,1,0:T(8,128)(2,1)}, u32[]{:S(2)}) copy-start(bf16[2,2,3072,128]{3,2,1,0:T(8,128)(2,1)} %param.12) | copy-start | bytes 9437188
  46.8 2.2 slice-start
  47.1 2.6 slice-start.1
  68.2 5.9 %collective-permute-start = (bf16[4,4,48,16,128]{4,3,2,1,0:T(8,128)(2,1)S(1)}, bf16[4,4,48,16,128]{4,3,2,1,0:T(8,128)(2,1)}, u32[]{:S(2)}, u32[]{:S(2)}) collective-permute-start(bf16[4,4,48,16,128]{4,3,2,1,0:T(8,128)(2,1)S(1)} %fusion.2), channel_id=1, source_target_pairs={{0,2},{2,0},{1,3},{3,1},{4,6},{6,4},{5,7},{7,5},{8,10},{10,8},{9,1... | collective-permute-start | bytes 9437192 | tf_op jit(solution)/shard_map/ppermute | solution.py:32
  80.3 69.3 %reduce-scatter.5.cloned.1.call-start = ((), (), s32[]{:S(2)}) async-start(), calls=%async_computation.3 | async-start | bytes 1966080 | tf_op jit(solution)/shard_map/reduce_scatter | solution.py:35
  123.6 92.4 %all-gather.4.cloned.1.call-start = ((), (), s32[]{:S(2)}) async-start(), calls=%async_computation.4 | async-start | bytes 2359296 | tf_op jit(solution)/shard_map/all_gather | solution.py:42
  216.0 3.6 %collective-permute-start.1 = (bf16[2,4,48,16,128]{4,3,2,1,0:T(8,128)(2,1)}, bf16[2,4,48,16,128]{4,3,2,1,0:T(8,128)(2,1)S(1)}, u32[]{:S(2)}, u32[]{:S(2)}) collective-permute-start(bf16[2,4,48,16,128]{4,3,2,1,0:T(8,128)(2,1)} %bitcast.76), channel_id=1, source_target_pairs={{0,2},{2,0},{1,3},{3,1},{4,6},{6,4},{5,7},{7,5},{8,10},{10,8},{9,1... | collective-permute-start | bytes 4718600 | tf_op jit(solution)/shard_map/ppermute | solution.py:44
  221.9 1.9 copy-start.2
  222.1 2.7 copy-start
  222.1 3.6 %copy-start.1 = (f32[512,1536]{1,0:T(8,128)S(1)}, f32[512,1536]{1,0:T(8,128)}, u32[]{:S(2)}) copy-start(f32[512,1536]{1,0:T(8,128)} %param.20) | copy-start | bytes 9437188
  232.5 40.7 %collective-permute-start.6 = (bf16[256,1536]{1,0:T(8,128)(2,1)}, bf16[256,1536]{1,0:T(8,128)(2,1)}, u32[]{:S(2)}, u32[]{:S(2)}) collective-permute-start(bf16[256,1536]{1,0:T(8,128)(2,1)} %get-tuple-element.75), channel_id=1, source_target_pairs={{0,1},{1,4},{4,5},{5,0},{2,3},{3,6},{6,7},{7,2},{8,9},{9,12},{12,1... | collective-permute-start | bytes 2359304 | tf_op jit(solution)/shard_map/ppermute | solution.py:69
  233.0 41.4 %collective-permute-start.7 = (bf16[256,1536]{1,0:T(8,128)(2,1)}, bf16[256,1536]{1,0:T(8,128)(2,1)}, u32[]{:S(2)}, u32[]{:S(2)}) collective-permute-start(bf16[256,1536]{1,0:T(8,128)(2,1)} %get-tuple-element.74), channel_id=1, source_target_pairs={{0,5},{1,0},{4,1},{5,4},{2,7},{3,2},{6,3},{7,6},{8,13},{9,8},{12,9... | collective-permute-start | bytes 2359304 | tf_op jit(solution)/shard_map/ppermute | solution.py:70
  240.4 7.7 %copy-start.5 = (f32[2,1536,128]{2,1,0:T(8,128)S(1)}, f32[2,1536,128]{2,1,0:T(8,128)}, u32[]{:S(2)}) copy-start(f32[2,1536,128]{2,1,0:T(8,128)} %param.15) | copy-start | bytes 4718596
  240.4 7.7 %copy-start.6 = (f32[2,1536,128]{2,1,0:T(8,128)S(1)}, f32[2,1536,128]{2,1,0:T(8,128)}, u32[]{:S(2)}) copy-start(f32[2,1536,128]{2,1,0:T(8,128)} %param.18) | copy-start | bytes 4718596
  240.4 7.7 %copy-start.7 = (f32[2,1536,128]{2,1,0:T(8,128)S(1)}, f32[2,1536,128]{2,1,0:T(8,128)}, u32[]{:S(2)}) copy-start(f32[2,1536,128]{2,1,0:T(8,128)} %param.21) | copy-start | bytes 4718596
  244.8 17.5 %collective-permute-start.4 = (bf16[1,118,1536]{2,1,0:T(8,128)(2,1)S(1)}, bf16[1,118,1536]{2,1,0:T(8,128)(2,1)S(1)}, u32[]{:S(2)}, u32[]{:S(2)}) collective-permute-start(bf16[1,118,1536]{2,1,0:T(8,128)(2,1)S(1)} %get-tuple-element.83), channel_id=1, source_target_pairs={{0,1},{1,4},{4,5},{5,0},{2,3},{3,6},{6,7},{7,2},{8,9},{9,12},{12,1... | collective-permute-start | bytes 1087496 | tf_op jit(solution)/shard_map/ppermute | solution.py:69
  244.8 17.4 %collective-permute-start.5 = (bf16[1,118,1536]{2,1,0:T(8,128)(2,1)S(1)}, bf16[1,118,1536]{2,1,0:T(8,128)(2,1)S(1)}, u32[]{:S(2)}, u32[]{:S(2)}) collective-permute-start(bf16[1,118,1536]{2,1,0:T(8,128)(2,1)S(1)} %get-tuple-element.82), channel_id=1, source_target_pairs={{0,5},{1,0},{4,1},{5,4},{2,7},{3,2},{6,3},{7,6},{8,13},{9,8},{12,9... | collective-permute-start | bytes 1087496 | tf_op jit(solution)/shard_map/ppermute | solution.py:70
  251.1 18.7 %collective-permute-start.2 = (bf16[1,1536,128]{2,1,0:T(8,128)(2,1)S(1)}, bf16[1,1536,128]{2,1,0:T(8,128)(2,1)S(1)}, u32[]{:S(2)}, u32[]{:S(2)}) collective-permute-start(bf16[1,1536,128]{2,1,0:T(8,128)(2,1)S(1)} %get-tuple-element.81), channel_id=1, source_target_pairs={{0,1},{1,4},{4,5},{5,0},{2,3},{3,6},{6,7},{7,2},{8,9},{9,12},{12,1... | collective-permute-start | bytes 1179656 | tf_op jit(solution)/shard_map/ppermute | solution.py:69
  262.2 9.5 %collective-permute-start.3 = (bf16[1,1536,128]{2,1,0:T(8,128)(2,1)S(1)}, bf16[1,1536,128]{2,1,0:T(8,128)(2,1)S(1)}, u32[]{:S(2)}, u32[]{:S(2)}) collective-permute-start(bf16[1,1536,128]{2,1,0:T(8,128)(2,1)S(1)} %get-tuple-element.80), channel_id=1, source_target_pairs={{0,5},{1,0},{4,1},{5,4},{2,7},{3,2},{6,3},{7,6},{8,13},{9,8},{12,9... | collective-permute-start | bytes 1179656 | tf_op jit(solution)/shard_map/ppermute | solution.py:70
Sparse Core Ops, SparseCore 0:
  80.4 40.6 reduce-scatter.2
  124.1 25.4 reduce-scatter.4
  186.6 29.3 all-gather.3

commit v10 on v9

--- a/solution.py
+++ b/solution.py
@@ -27,10 +27,11 @@
 def reduce_flat(buf):
     me = lax.axis_index("core")
     flip = [(0, 1), (1, 0)]
-    mine = lax.dynamic_index_in_dim(buf, me, 0, keepdims=False)
-    theirs = lax.dynamic_index_in_dim(buf, 1 - me, 0, keepdims=False)
-    got = lax.ppermute(theirs.astype(jnp.bfloat16), "core", perm=flip)
-    part = (mine + got.astype(jnp.float32)).astype(jnp.bfloat16)
+    low = buf.astype(jnp.bfloat16)
+    mine = lax.dynamic_index_in_dim(low, me, 0, keepdims=False)
+    theirs = lax.dynamic_index_in_dim(low, 1 - me, 0, keepdims=False)
+    got = lax.ppermute(theirs, "core", perm=flip)
+    part = (mine.astype(jnp.float32) + got.astype(jnp.float32)).astype(jnp.bfloat16)
     part = lax.psum_scatter(part, XRING, scatter_dimension=0, tiled=False)
     part = lax.psum_scatter(part.astype(jnp.float32), "y", scatter_dimension=0, tiled=False)
     part = lax.psum(part, "z").astype(jnp.bfloat16)

time: 286 us -> 272 us (0.951)
  local copies, waits for them, and re-layouts: 64.4 us -> 48.9 us
    transpose x1 -> x0, local copies, waits for them, and re-layouts: 10.4 us -> none  [on_device(): jnp.transpose(buf, (1, 2, 0, 3, 4, 5, 6))]
    transpose x2, local copies, waits for them, and re-layouts: 12.2 us -> 4.81 us  [to_tiles(): return jnp.swapaxes(a, n + 1, n + 2)]
    reshape x2, local copies, waits for them, and re-layouts: 12.1 us -> 8.5 us  [to_tiles(): a = a.reshape(*lead, r // TR, TR, c // 128, 128)]
    reduce_sum x1, other arithmetic: 0.49 us -> 3.99 us  [on_device(): sx = to_tiles(jnp.sum(grad_xproj, axis=0, dtype=jnp.float32))]
    unnamed x27 -> x19, local copies, waits for them, and re-layouts: 14.7 us -> 12.8 us
where the time goes in v10:
time: 272 us
  waiting for transfers between devices  90.9 us (33%)
  blocking collectives  61.1 us (22%)
  local copies, waits for them, and re-layouts  48.9 us (18%)
  other arithmetic  48.1 us (18%)
  between operations  15.8 us (6%)
  starting transfers between devices  6.82 us (3%)
    reduce_scatter x1, waiting for transfers between devices, reduce_flat(): part = lax.psum_scatter(part, XRING, scatter_dimension=0, tiled=False)  40.8 us
    reduce_scatter x1, waiting for transfers between devices, reduce_flat(): lax.psum_scatter(part.astype(jnp.float32), 'y', scatter_dimension=0, tile...  26 us
    psum x3, blocking collectives, reduce_flat(): squares = lax.psum(squares, axis)  24.2 us
    psum x1, blocking collectives, reduce_flat(): part = lax.psum(part, 'z').astype(jnp.bfloat16)  21.8 us
    all_gather x1, blocking collectives, reduce_flat(): part = lax.all_gather(part, 'y', axis=0)  15 us
    unnamed x19, local copies, waits for them, and re-layouts  12.8 us
    ppermute x3, waiting for transfers between devices, swap_halves(): lax.ppermute(first, XRING, perm=[(p, (p + 1) % n) for p in range(n)])  9.01 us
    reshape x2, local copies, waits for them, and re-layouts, to_tiles(): a = a.reshape(*lead, r // TR, TR, c // 128, 128)  8.5 us
  transfers between devices with their start and end apart: 11, of which 8 were waited for; matrix products, arithmetic and copies ran while one was open for 9% of the time, Pallas kernels for 0%

profile of v10, /device:TPU:0, one launch (start us, length us, event | category | flops | bytes accessed | tf_op | source)
XLA Modules:
  0.0 271.7 jit_solution(11457368867459160750)
XLA Ops:
  7.2 6.1 %reduce.2 = bf16[1024,1536]{1,0:T(8,128)(2,1)S(1)} reduce(bf16[2,1024,1536]{2,1,0:T(8,128)(2,1)} %param.14, bf16[]{:T(256)} %constant.22.clone.1), dimensions={0}, to_apply=%region_2.3.clone | reduce | flops 1572864 | bytes 9437186 | tf_op jit(solution)/shard_map/reduce_sum | solution.py:119
  13.3 3.6 %reshape.85 = bf16[64,16,12,128]{3,2,1,0:T(8,128)(2,1)} reshape(bf16[1024,1536]{1,0:T(8,128)(2,1)S(1)} %reduce.2) | data formatting | bytes 6291456 | tf_op jit(solution)/shard_map/reshape | solution.py:56
  16.9 3.0 %copy.56 = bf16[64,12,16,128]{3,2,1,0:T(8,128)(2,1)S(1)} copy(bf16[64,12,16,128]{3,1,2,0:T(8,128)(2,1)} %bitcast.61) | data formatting | bytes 6291456 | tf_op jit(solution)/shard_map/transpose | solution.py:58
  19.9 7.6 %reduce = bf16[2,118,3072]{2,0,1:T(2,128)(2,1)} reduce(bf16[2,2,118,3072]{3,1,2,0:T(2,128)(2,1)} %param.13, bf16[]{:T(256)} %constant.22.clone.1), dimensions={0}, to_apply=%region_0.0.clone | reduce | flops 724992 | bytes 4349954 | tf_op jit(solution)/shard_map/reduce_sum | solution.py:113
  27.5 3.7 %pad.5 = bf16[2,128,3072]{2,0,1:T(2,128)(2,1)} pad(bf16[2,118,3072]{2,0,1:T(2,128)(2,1)} %reduce, bf16[]{:T(256)} %constant.22.clone.1), padding=0_0x0_10x0_0 | pad | bytes 3022850 | tf_op jit(solution)/shard_map/jit(_pad)/pad | solution.py:114
  31.2 4.8 %reshape.94 = bf16[2,8,16,24,128]{4,3,0,2,1:T(8,128)(2,1)} reshape(bf16[2,128,3072]{2,0,1:T(2,128)(2,1)} %pad.5) | data formatting | bytes 3145728 | tf_op jit(solution)/shard_map/reshape | solution.py:56
  36.1 1.8 copy.53
  37.9 1.4 copy.54
  39.3 4.0 %reduce.1 = bf16[2,3072,128]{2,1,0:T(8,128)(2,1)} reduce(bf16[2,2,3072,128]{3,2,1,0:T(8,128)(2,1)} %param.12, bf16[]{:T(256)} %constant.22.clone.1), dimensions={0}, to_apply=%region_1.0.clone | reduce | flops 786432 | bytes 4718594 | tf_op jit(solution)/shard_map/reduce_sum | solution.py:108
  43.3 2.8 %copy.55 = bf16[2,2,96,16,128]{4,3,2,1,0:T(8,128)(2,1)} copy(bf16[2,2,96,16,128]{4,3,2,0,1:T(8,128)(2,1)} %bitcast.70) | data formatting | bytes 3145728 | tf_op jit(solution)/shard_map/transpose | solution.py:110
  46.1 2.5 pad_maximum_fusion
  48.6 4.1 %copy.57 = bf16[2,2,2,4,48,16,128]{6,5,4,3,2,1,0:T(8,128)(2,1)} copy(bf16[2,2,2,4,48,16,128]{6,5,4,3,1,0,2:T(8,128)(2,1)S(1)} %bitcast.60) | data formatting | bytes 12582912 | tf_op jit(solution)/shard_map/convert_element_type | solution.py:30
  52.7 2.4 dynamic-slice_bitcast_fusion
  55.2 0.1 collective-permute-start
  55.3 5.8 %collective-permute-done = bf16[4,4,48,16,128]{4,3,2,1,0:T(8,128)(2,1)} collective-permute-done((bf16[4,4,48,16,128]{4,3,2,1,0:T(8,128)(2,1)S(1)}, bf16[4,4,48,16,128]{4,3,2,1,0:T(8,128)(2,1)}, u32[]{:S(2)}, u32[]{:S(2)}) %collective-permute-start) | collective-permute-done | bytes 3145760 | tf_op jit(solution)/shard_map/ppermute | solution.py:33
  61.0 5.3 %fusion = bf16[4,4,48,16,128]{4,3,2,1,0:T(8,128)(2,1)} fusion(bf16[4,4,48,16,128]{4,3,2,1,0:T(8,128)(2,1)} %collective-permute-done, bf16[2,4,4,48,16,128]{5,4,3,2,1,0:T(8,128)(2,1)} %bitcast.59, s32[]{:T(128)S(6)} %select_n.55), kind=kLoop, calls=%fused_computation.2 | loop fusion | flops 6291456 | bytes 9437188 | tf_op jit(solution)/shard_map/convert_element_type | solution.py:34
  66.5 40.8 %reduce-scatter.3.cloned.1.call-done = bf16[1,4,48,16,128]{4,3,2,1,0:T(8,128)(2,1)} async-done(((bf16[4,4,48,16,128]{4,3,2,1,0:T(8,128)(2,1)}), bf16[1,4,48,16,128]{4,3,2,1,0:T(8,128)(2,1)}) %reduce-scatter.3.cloned.1.call-update) | async-done | bytes 786448 | tf_op jit(solution)/shard_map/reduce_scatter | solution.py:35
  107.2 2.4 bitcast_convert_fusion
  109.7 0.0 all-gather.4.cloned.1.call-start
  109.7 26.0 %reduce-scatter.5.cloned.1.call-done = f32[1,48,16,128]{3,2,1,0:T(8,128)} async-done(((f32[4,48,16,128]{3,2,1,0:T(8,128)}), f32[1,48,16,128]{3,2,1,0:T(8,128)}) %reduce-scatter.5.cloned.1.call-update) | async-done | bytes 393232 | tf_op jit(solution)/shard_map/reduce_scatter | solution.py:36
  135.7 21.8 %all-reduce.2 = bf16[48,16,128]{2,1,0:T(8,128)(2,1)S(1)} all-reduce(f32[48,16,128]{2,1,0:T(8,128)} %bitcast.75), channel_id=1, replica_groups=mesh['z'=4,'y'=4,'xh'=2,'core'=2,'shard'=2] {'z'}, use_global_device_ids=true, to_apply=%region_5.6 | all-reduce | flops 98304 | bytes 589824 | tf_op jit(solution)/shard_map/psum | solution.py:37
  157.5 15.0 %all-gather = bf16[192,16,128]{2,1,0:T(8,128)(2,1)} all-gather(bf16[48,16,128]{2,1,0:T(8,128)(2,1)S(1)} %all-reduce.2), channel_id=2, replica_groups=mesh['z'=4,'y'=4,'xh'=2,'core'=2,'shard'=2] {'y'}, dimensions={0}, use_global_device_ids=true | all-gather | bytes 983040 | tf_op jit(solution)/shard_map/all_gather | solution.py:42
  172.6 0.7 multiply_reduce_fusion
  173.3 3.1 %psum.29 = f32[]{:T(128)} all-reduce(f32[]{:T(128)} %multiply_reduce_fusion), channel_id=1, replica_groups=mesh['z'=4,'y'=4,'xh'=2,'core'=2,'shard'=2] {'core'}, use_global_device_ids=true, to_apply=%region_7.8 | all-reduce | flops 1 | bytes 8 | tf_op jit(solution)/shard_map/psum | solution.py:41
  176.3 11.4 %psum.30 = f32[]{:T(128)} all-reduce(f32[]{:T(128)} %psum.29), channel_id=1, replica_groups=mesh['z'=4,'y'=4,'xh'=2,'core'=2,'shard'=2] {'xh','shard'}, use_global_device_ids=true, to_apply=%region_8.9 | all-reduce | flops 1 | bytes 8 | tf_op jit(solution)/shard_map/psum | solution.py:41
  187.8 9.7 %psum.31 = f32[]{:T(128)} all-reduce(f32[]{:T(128)} %psum.30), channel_id=1, replica_groups=mesh['z'=4,'y'=4,'xh'=2,'core'=2,'shard'=2] {'y'}, use_global_device_ids=true, to_apply=%region_9.10 | all-reduce | flops 1 | bytes 8 | tf_op jit(solution)/shard_map/psum | solution.py:41
  197.5 4.6 %all-gather.4.cloned.1.call-done = bf16[8,48,16,128]{3,2,1,0:T(8,128)(2,1)} async-done(((bf16[4,48,16,128]{3,2,1,0:T(8,128)(2,1)}), bf16[8,48,16,128]{3,2,1,0:T(8,128)(2,1)}) %all-gather.4.cloned.1.call-update) | async-done | bytes 1572880 | tf_op jit(solution)/shard_map/all_gather | solution.py:43
  202.9 2.9 %collective-permute-done.1 = bf16[2,4,48,16,128]{4,3,2,1,0:T(8,128)(2,1)S(1)} collective-permute-done((bf16[2,4,48,16,128]{4,3,2,1,0:T(8,128)(2,1)}, bf16[2,4,48,16,128]{4,3,2,1,0:T(8,128)(2,1)S(1)}, u32[]{:S(2)}, u32[]{:S(2)}) %collective-permute-start.1) | collective-permute-done | bytes 1572896 | tf_op jit(solution)/shard_map/ppermute | solution.py:45
  205.7 1.6 select_bitcast_fusion.1
  207.4 0.6 convert_multiply_fusion
  208.0 0.2 slice_multiply_fusion
  208.2 1.3 copy.63
  209.5 0.3 copy-done.2
  209.9 1.0 copy-done
  210.9 0.9 copy-done.1
  211.8 5.6 %fusion.7 = (bf16[512,1536]{1,0:T(8,128)(2,1)S(1)}, f32[512,1536]{1,0:T(8,128)}, f32[512,1536]{1,0:T(8,128)}, f32[512,1536]{1,0:T(8,128)}) fusion(f32[512,1536]{1,0:T(8,128)S(1)} %copy-done, f32[64,8,12,128]{3,2,1,0:T(8,128)S(1)} %bitcast.62, f32[512,1536]{1,0:T(8,128)S(1)} %copy-done.1, f32[512,1536]{1,0:T(8,128)S(1)} %copy-done.2), kind=kLoop, calls=%fused_computation.43 | loop fusion | flops 12582912 | bytes 23592960 | tf_op jit(solution)/shard_map/convert_element_type | solution.py:151
  217.4 1.3 fusion.17
  218.6 0.5 collective-permute-start.6
  219.1 2.8 %collective-permute-start.7 = (bf16[256,1536]{1,0:T(8,128)(2,1)}, bf16[256,1536]{1,0:T(8,128)(2,1)}, u32[]{:S(2)}, u32[]{:S(2)}) collective-permute-start(bf16[256,1536]{1,0:T(8,128)(2,1)} %get-tuple-element.74), channel_id=1, source_target_pairs={{0,5},{1,0},{4,1},{5,4},{2,7},{3,2},{6,3},{7,6},{8,13},{9,8},{12,9... | collective-permute-start | bytes 2359304 | tf_op jit(solution)/shard_map/ppermute | solution.py:71
  221.9 0.2 fusion.16
  222.1 1.8 copy.59
  223.9 2.6 reshape.88
  226.5 4.3 %fusion.10 = (bf16[2,118,1536]{2,1,0:T(8,128)(2,1)S(1)}, f32[2,118,1536]{2,1,0:T(8,128)S(1)}, f32[2,118,1536]{2,1,0:T(8,128)S(1)}, f32[2,118,1536]{2,1,0:T(8,128)S(1)}) fusion(f32[2,118,1536]{2,0,1:T(2,128)} %param.16, f32[2,128,1536]{2,1,0:T(8,128)} %reshape.88, f32[]{:T(128)S(6)} %min.3, f32[2,118,1536]{2,0,1:T(2,128)} %param.19, f32[2,118,1536]{2,0,1:T(2,128)} %param.22), kind=kLoop, calls=%fused_computation.44 | loop fusion | flops 6162432 | bytes 10874884 | tf_op jit(solution)/shard_map/convert_element_type | solution.py:150
  230.9 0.1 collective-permute-start.4
  231.0 3.2 %collective-permute-start.5 = (bf16[1,118,1536]{2,1,0:T(8,128)(2,1)S(1)}, bf16[1,118,1536]{2,1,0:T(8,128)(2,1)S(1)}, u32[]{:S(2)}, u32[]{:S(2)}) collective-permute-start(bf16[1,118,1536]{2,1,0:T(8,128)(2,1)S(1)} %get-tuple-element.82), channel_id=1, source_target_pairs={{0,5},{1,0},{4,1},{5,4},{2,7},{3,2},{6,3},{7,6},{8,13},{9,8},{12,9... | collective-permute-start | bytes 1087496 | tf_op jit(solution)/shard_map/ppermute | solution.py:71
  234.2 3.0 %fusion.13 = (bf16[2,1536,128]{2,1,0:T(8,128)(2,1)S(1)}, f32[2,1536,128]{2,1,0:T(8,128)}, f32[2,1536,128]{2,1,0:T(8,128)}, f32[2,1536,128]{2,1,0:T(8,128)}) fusion(f32[2,1536,128]{2,1,0:T(8,128)S(1)} %copy-done.3, f32[2,1536,128]{2,1,0:T(8,128)S(1)} %copy-done.4, f32[2,1536,128]{2,1,0:T(8,128)S(1)} %copy-done.5, f32[2,1536,128]{2,1,0:T(8,128)S(1)} %bitcast.71), kind=kLoop, calls=%fused_computation.45 | loop fusion | flops 6291456 | bytes 11796480 | tf_op jit(solution)/shard_map/convert_element_type | solution.py:149
  237.2 0.1 fusion.18
  237.3 0.1 collective-permute-start.2
  237.3 2.2 copy.64
  239.6 2.2 copy.65
  241.8 2.2 copy.66
  244.0 4.4 %collective-permute-done.4 = bf16[1,118,1536]{2,1,0:T(8,128)(2,1)S(1)} collective-permute-done((bf16[1,118,1536]{2,1,0:T(8,128)(2,1)S(1)}, bf16[1,118,1536]{2,1,0:T(8,128)(2,1)S(1)}, u32[]{:S(2)}, u32[]{:S(2)}) %collective-permute-start.4) | collective-permute-done | bytes 362528 | tf_op jit(solution)/shard_map/ppermute | solution.py:70
  248.4 0.1 broadcast_select_fusion.5
  248.5 0.2 pad_maximum_fusion.3
  248.7 2.6 copy.67
  251.3 4.7 %collective-permute-done.2 = bf16[1,1536,128]{2,1,0:T(8,128)(2,1)S(1)} collective-permute-done((bf16[1,1536,128]{2,1,0:T(8,128)(2,1)S(1)}, bf16[1,1536,128]{2,1,0:T(8,128)(2,1)S(1)}, u32[]{:S(2)}, u32[]{:S(2)}) %collective-permute-start.2) | collective-permute-done | bytes 393248 | tf_op jit(solution)/shard_map/ppermute | solution.py:70
  256.0 1.9 collective-permute-done.3
  257.9 0.1 constant_dynamic-update-slice_fusion
  257.9 0.2 broadcast_select_fusion.3
  258.1 1.2 pad_maximum_fusion.2
  259.4 1.2 constant_dynamic-update-slice_fusion.5
  260.6 1.2 constant_dynamic-update-slice_fusion.4
  261.8 0.4 broadcast_select_fusion.1
  262.2 1.9 pad_maximum_fusion.1
  (23 shorter events, 0.3 us)
Async XLA Ops:
  7.2 100.1 %reduce-scatter.3.cloned.1.call-start = ((), (), s32[]{:S(2)}) async-start(), calls=%async_computation.2 | async-start | bytes 3932160 | tf_op jit(solution)/shard_map/reduce_scatter | solution.py:35
  55.2 5.9 %collective-permute-start = (bf16[4,4,48,16,128]{4,3,2,1,0:T(8,128)(2,1)S(1)}, bf16[4,4,48,16,128]{4,3,2,1,0:T(8,128)(2,1)}, u32[]{:S(2)}, u32[]{:S(2)}) collective-permute-start(bf16[4,4,48,16,128]{4,3,2,1,0:T(8,128)(2,1)S(1)} %dynamic-slice_bitcast_fusion), channel_id=1, source_target_pairs={{0,2},{2,0},{1,3},{3,1},{4,6},{6,4},{5,7},{7,5},{8,10},{10,8},{9,1... | collective-permute-start | bytes 9437192 | tf_op jit(solution)/shard_map/ppermute | solution.py:33
  66.4 69.3 %reduce-scatter.5.cloned.1.call-start = ((), (), s32[]{:S(2)}) async-start(), calls=%async_computation.3 | async-start | bytes 1966080 | tf_op jit(solution)/shard_map/reduce_scatter | solution.py:36
  109.7 92.4 %all-gather.4.cloned.1.call-start = ((), (), s32[]{:S(2)}) async-start(), calls=%async_computation.4 | async-start | bytes 2359296 | tf_op jit(solution)/shard_map/all_gather | solution.py:43
  202.1 3.6 %collective-permute-start.1 = (bf16[2,4,48,16,128]{4,3,2,1,0:T(8,128)(2,1)}, bf16[2,4,48,16,128]{4,3,2,1,0:T(8,128)(2,1)S(1)}, u32[]{:S(2)}, u32[]{:S(2)}) collective-permute-start(bf16[2,4,48,16,128]{4,3,2,1,0:T(8,128)(2,1)} %bitcast.73), channel_id=1, source_target_pairs={{0,2},{2,0},{1,3},{3,1},{4,6},{6,4},{5,7},{7,5},{8,10},{10,8},{9,1... | collective-permute-start | bytes 4718600 | tf_op jit(solution)/shard_map/ppermute | solution.py:45
  208.0 1.9 copy-start.2
  208.2 2.7 copy-start
  208.2 3.6 %copy-start.1 = (f32[512,1536]{1,0:T(8,128)S(1)}, f32[512,1536]{1,0:T(8,128)}, u32[]{:S(2)}) copy-start(f32[512,1536]{1,0:T(8,128)} %param.20) | copy-start | bytes 9437188
  218.6 40.7 %collective-permute-start.6 = (bf16[256,1536]{1,0:T(8,128)(2,1)}, bf16[256,1536]{1,0:T(8,128)(2,1)}, u32[]{:S(2)}, u32[]{:S(2)}) collective-permute-start(bf16[256,1536]{1,0:T(8,128)(2,1)} %get-tuple-element.75), channel_id=1, source_target_pairs={{0,1},{1,4},{4,5},{5,0},{2,3},{3,6},{6,7},{7,2},{8,9},{9,12},{12,1... | collective-permute-start | bytes 2359304 | tf_op jit(solution)/shard_map/ppermute | solution.py:70
  219.1 41.5 %collective-permute-start.7 = (bf16[256,1536]{1,0:T(8,128)(2,1)}, bf16[256,1536]{1,0:T(8,128)(2,1)}, u32[]{:S(2)}, u32[]{:S(2)}) collective-permute-start(bf16[256,1536]{1,0:T(8,128)(2,1)} %get-tuple-element.74), channel_id=1, source_target_pairs={{0,5},{1,0},{4,1},{5,4},{2,7},{3,2},{6,3},{7,6},{8,13},{9,8},{12,9... | collective-permute-start | bytes 2359304 | tf_op jit(solution)/shard_map/ppermute | solution.py:71
  226.5 7.7 %copy-start.3 = (f32[2,1536,128]{2,1,0:T(8,128)S(1)}, f32[2,1536,128]{2,1,0:T(8,128)}, u32[]{:S(2)}) copy-start(f32[2,1536,128]{2,1,0:T(8,128)} %param.15) | copy-start | bytes 4718596
  226.5 7.7 %copy-start.4 = (f32[2,1536,128]{2,1,0:T(8,128)S(1)}, f32[2,1536,128]{2,1,0:T(8,128)}, u32[]{:S(2)}) copy-start(f32[2,1536,128]{2,1,0:T(8,128)} %param.18) | copy-start | bytes 4718596
  226.5 7.7 %copy-start.5 = (f32[2,1536,128]{2,1,0:T(8,128)S(1)}, f32[2,1536,128]{2,1,0:T(8,128)}, u32[]{:S(2)}) copy-start(f32[2,1536,128]{2,1,0:T(8,128)} %param.21) | copy-start | bytes 4718596
  230.9 17.5 %collective-permute-start.4 = (bf16[1,118,1536]{2,1,0:T(8,128)(2,1)S(1)}, bf16[1,118,1536]{2,1,0:T(8,128)(2,1)S(1)}, u32[]{:S(2)}, u32[]{:S(2)}) collective-permute-start(bf16[1,118,1536]{2,1,0:T(8,128)(2,1)S(1)} %get-tuple-element.83), channel_id=1, source_target_pairs={{0,1},{1,4},{4,5},{5,0},{2,3},{3,6},{6,7},{7,2},{8,9},{9,12},{12,1... | collective-permute-start | bytes 1087496 | tf_op jit(solution)/shard_map/ppermute | solution.py:70
  231.0 17.4 %collective-permute-start.5 = (bf16[1,118,1536]{2,1,0:T(8,128)(2,1)S(1)}, bf16[1,118,1536]{2,1,0:T(8,128)(2,1)S(1)}, u32[]{:S(2)}, u32[]{:S(2)}) collective-permute-start(bf16[1,118,1536]{2,1,0:T(8,128)(2,1)S(1)} %get-tuple-element.82), channel_id=1, source_target_pairs={{0,5},{1,0},{4,1},{5,4},{2,7},{3,2},{6,3},{7,6},{8,13},{9,8},{12,9... | collective-permute-start | bytes 1087496 | tf_op jit(solution)/shard_map/ppermute | solution.py:71
  237.3 18.7 %collective-permute-start.2 = (bf16[1,1536,128]{2,1,0:T(8,128)(2,1)S(1)}, bf16[1,1536,128]{2,1,0:T(8,128)(2,1)S(1)}, u32[]{:S(2)}, u32[]{:S(2)}) collective-permute-start(bf16[1,1536,128]{2,1,0:T(8,128)(2,1)S(1)} %get-tuple-element.81), channel_id=1, source_target_pairs={{0,1},{1,4},{4,5},{5,0},{2,3},{3,6},{6,7},{7,2},{8,9},{9,12},{12,1... | collective-permute-start | bytes 1179656 | tf_op jit(solution)/shard_map/ppermute | solution.py:70
  248.4 9.5 %collective-permute-start.3 = (bf16[1,1536,128]{2,1,0:T(8,128)(2,1)S(1)}, bf16[1,1536,128]{2,1,0:T(8,128)(2,1)S(1)}, u32[]{:S(2)}, u32[]{:S(2)}) collective-permute-start(bf16[1,1536,128]{2,1,0:T(8,128)(2,1)S(1)} %get-tuple-element.80), channel_id=1, source_target_pairs={{0,5},{1,0},{4,1},{5,4},{2,7},{3,2},{6,3},{7,6},{8,13},{9,8},{12,9... | collective-permute-start | bytes 1179656 | tf_op jit(solution)/shard_map/ppermute | solution.py:71
Sparse Core Ops, SparseCore 0:
  66.5 40.6 reduce-scatter.2
  110.2 25.4 reduce-scatter.4
  172.7 29.3 all-gather.3

commit v11 on v10

--- a/solution.py
+++ b/solution.py
@@ -39,8 +39,7 @@
     squares = jnp.sum(wide * wide)
     for axis in ("core", XRING, "y"):
         squares = lax.psum(squares, axis)
-    part = lax.all_gather(part, "y", axis=0)
-    part = lax.all_gather(part, "xh", axis=0)
+    part = lax.all_gather(part, ("xh", "y"), axis=0)
     part, squares = lax.optimization_barrier((part, squares))
     other = lax.ppermute(part, "core", perm=flip)
     first = me == 0

time: 272 us -> 276 us (1.015)
  waiting for transfers between devices: 90.9 us -> 108 us
  blocking collectives: 61.1 us -> 46.5 us
    all_gather x1, waiting for transfers between devices: 4.59 us -> 21.8 us  [reduce_flat(): part = lax.all_gather(part, ('xh', 'y'), axis=0)]
    all_gather x1 -> x0, blocking collectives: 15 us -> none  [reduce_flat(): part = lax.all_gather(part, 'y', axis=0)]
where the time goes in v11:
time: 276 us; the launch traced here: 275 us
  waiting for transfers between devices  108 us (39%)
  other arithmetic  49.1 us (18%)
  local copies, waits for them, and re-layouts  48.9 us (18%)
  blocking collectives  46.5 us (17%)
  between operations  15.8 us (6%)
  starting transfers between devices  6.82 us (2%)
    reduce_scatter x1, waiting for transfers between devices, reduce_flat(): part = lax.psum_scatter(part, XRING, scatter_dimension=0, tiled=False)  40.8 us
    reduce_scatter x1, waiting for transfers between devices, reduce_flat(): lax.psum_scatter(part.astype(jnp.float32), 'y', scatter_dimension=0, tile...  26 us
    psum x3, blocking collectives, reduce_flat(): squares = lax.psum(squares, axis)  24.2 us
    psum x1, blocking collectives, reduce_flat(): part = lax.psum(part, 'z').astype(jnp.bfloat16)  22.3 us
    all_gather x1, waiting for transfers between devices, reduce_flat(): part = lax.all_gather(part, ('xh', 'y'), axis=0)  21.8 us
    unnamed x19, local copies, waits for them, and re-layouts  12.8 us
    ppermute x3, waiting for transfers between devices, swap_halves(): lax.ppermute(first, XRING, perm=[(p, (p + 1) % n) for p in range(n)])  9.01 us
    reshape x2, local copies, waits for them, and re-layouts, to_tiles(): a = a.reshape(*lead, r // TR, TR, c // 128, 128)  8.5 us
  transfers between devices with their start and end apart: 11, of which 8 were waited for; matrix products, arithmetic and copies ran while one was open for 9% of the time, Pallas kernels for 0%

profile of v11, /device:TPU:0, one launch (start us, length us, event | category | flops | bytes accessed | tf_op | source)
XLA Modules:
  0.0 275.3 jit_solution(4395603345059351244)
XLA Ops:
  7.2 6.1 %reduce.2 = bf16[1024,1536]{1,0:T(8,128)(2,1)S(1)} reduce(bf16[2,1024,1536]{2,1,0:T(8,128)(2,1)} %param.14, bf16[]{:T(256)} %constant.22.clone.1), dimensions={0}, to_apply=%region_2.3.clone | reduce | flops 1572864 | bytes 9437186 | tf_op jit(solution)/shard_map/reduce_sum | solution.py:118
  13.3 3.6 %reshape.85 = bf16[64,16,12,128]{3,2,1,0:T(8,128)(2,1)} reshape(bf16[1024,1536]{1,0:T(8,128)(2,1)S(1)} %reduce.2) | data formatting | bytes 6291456 | tf_op jit(solution)/shard_map/reshape | solution.py:55
  16.9 3.0 %copy.56 = bf16[64,12,16,128]{3,2,1,0:T(8,128)(2,1)S(1)} copy(bf16[64,12,16,128]{3,1,2,0:T(8,128)(2,1)} %bitcast.60) | data formatting | bytes 6291456 | tf_op jit(solution)/shard_map/transpose | solution.py:57
  19.9 7.6 %reduce = bf16[2,118,3072]{2,0,1:T(2,128)(2,1)} reduce(bf16[2,2,118,3072]{3,1,2,0:T(2,128)(2,1)} %param.13, bf16[]{:T(256)} %constant.22.clone.1), dimensions={0}, to_apply=%region_0.0.clone | reduce | flops 724992 | bytes 4349954 | tf_op jit(solution)/shard_map/reduce_sum | solution.py:112
  27.5 3.7 %pad.5 = bf16[2,128,3072]{2,0,1:T(2,128)(2,1)} pad(bf16[2,118,3072]{2,0,1:T(2,128)(2,1)} %reduce, bf16[]{:T(256)} %constant.22.clone.1), padding=0_0x0_10x0_0 | pad | bytes 3022850 | tf_op jit(solution)/shard_map/jit(_pad)/pad | solution.py:113
  31.2 4.8 %reshape.93 = bf16[2,8,16,24,128]{4,3,0,2,1:T(8,128)(2,1)} reshape(bf16[2,128,3072]{2,0,1:T(2,128)(2,1)} %pad.5) | data formatting | bytes 3145728 | tf_op jit(solution)/shard_map/reshape | solution.py:55
  36.1 1.8 copy.53
  37.9 1.4 copy.54
  39.3 4.0 %reduce.1 = bf16[2,3072,128]{2,1,0:T(8,128)(2,1)} reduce(bf16[2,2,3072,128]{3,2,1,0:T(8,128)(2,1)} %param.12, bf16[]{:T(256)} %constant.22.clone.1), dimensions={0}, to_apply=%region_1.0.clone | reduce | flops 786432 | bytes 4718594 | tf_op jit(solution)/shard_map/reduce_sum | solution.py:107
  43.3 2.8 %copy.55 = bf16[2,2,96,16,128]{4,3,2,1,0:T(8,128)(2,1)} copy(bf16[2,2,96,16,128]{4,3,2,0,1:T(8,128)(2,1)} %bitcast.69) | data formatting | bytes 3145728 | tf_op jit(solution)/shard_map/transpose | solution.py:109
  46.1 2.5 pad_maximum_fusion
  48.6 4.1 %copy.57 = bf16[2,2,2,4,48,16,128]{6,5,4,3,2,1,0:T(8,128)(2,1)} copy(bf16[2,2,2,4,48,16,128]{6,5,4,3,1,0,2:T(8,128)(2,1)S(1)} %bitcast.59) | data formatting | bytes 12582912 | tf_op jit(solution)/shard_map/convert_element_type | solution.py:30
  52.7 2.4 dynamic-slice_bitcast_fusion
  55.2 0.1 collective-permute-start
  55.3 5.8 %collective-permute-done = bf16[4,4,48,16,128]{4,3,2,1,0:T(8,128)(2,1)} collective-permute-done((bf16[4,4,48,16,128]{4,3,2,1,0:T(8,128)(2,1)S(1)}, bf16[4,4,48,16,128]{4,3,2,1,0:T(8,128)(2,1)}, u32[]{:S(2)}, u32[]{:S(2)}) %collective-permute-start) | collective-permute-done | bytes 3145760 | tf_op jit(solution)/shard_map/ppermute | solution.py:33
  61.0 5.3 %fusion = bf16[4,4,48,16,128]{4,3,2,1,0:T(8,128)(2,1)} fusion(bf16[4,4,48,16,128]{4,3,2,1,0:T(8,128)(2,1)} %collective-permute-done, bf16[2,4,4,48,16,128]{5,4,3,2,1,0:T(8,128)(2,1)} %bitcast.58, s32[]{:T(128)S(6)} %select_n.55), kind=kLoop, calls=%fused_computation.2 | loop fusion | flops 6291456 | bytes 9437188 | tf_op jit(solution)/shard_map/convert_element_type | solution.py:34
  66.4 0.0 reduce-scatter.5.cloned.1.call-start
  66.5 40.8 %reduce-scatter.3.cloned.1.call-done = bf16[1,4,48,16,128]{4,3,2,1,0:T(8,128)(2,1)} async-done(((bf16[4,4,48,16,128]{4,3,2,1,0:T(8,128)(2,1)}), bf16[1,4,48,16,128]{4,3,2,1,0:T(8,128)(2,1)}) %reduce-scatter.3.cloned.1.call-update) | async-done | bytes 786448 | tf_op jit(solution)/shard_map/reduce_scatter | solution.py:35
  107.2 2.4 bitcast_convert_fusion
  109.7 0.0 all-gather.3.cloned.1.call-start
  109.7 26.0 %reduce-scatter.5.cloned.1.call-done = f32[1,48,16,128]{3,2,1,0:T(8,128)} async-done(((f32[4,48,16,128]{3,2,1,0:T(8,128)}), f32[1,48,16,128]{3,2,1,0:T(8,128)}) %reduce-scatter.5.cloned.1.call-update) | async-done | bytes 393232 | tf_op jit(solution)/shard_map/reduce_scatter | solution.py:36
  135.7 22.3 %all-reduce.2 = bf16[48,16,128]{2,1,0:T(8,128)(2,1)} all-reduce(f32[48,16,128]{2,1,0:T(8,128)} %bitcast.73), channel_id=1, replica_groups=mesh['z'=4,'y'=4,'xh'=2,'core'=2,'shard'=2] {'z'}, use_global_device_ids=true, to_apply=%region_5.6 | all-reduce | flops 98304 | bytes 589824 | tf_op jit(solution)/shard_map/psum | solution.py:37
  158.0 1.6 multiply_reduce_fusion
  159.7 3.1 %psum.29 = f32[]{:T(128)} all-reduce(f32[]{:T(128)} %multiply_reduce_fusion), channel_id=1, replica_groups=mesh['z'=4,'y'=4,'xh'=2,'core'=2,'shard'=2] {'core'}, use_global_device_ids=true, to_apply=%region_7.8 | all-reduce | flops 1 | bytes 8 | tf_op jit(solution)/shard_map/psum | solution.py:41
  162.8 11.4 %psum.30 = f32[]{:T(128)} all-reduce(f32[]{:T(128)} %psum.29), channel_id=1, replica_groups=mesh['z'=4,'y'=4,'xh'=2,'core'=2,'shard'=2] {'xh','shard'}, use_global_device_ids=true, to_apply=%region_8.9 | all-reduce | flops 1 | bytes 8 | tf_op jit(solution)/shard_map/psum | solution.py:41
  174.2 9.7 %psum.31 = f32[]{:T(128)} all-reduce(f32[]{:T(128)} %psum.30), channel_id=1, replica_groups=mesh['z'=4,'y'=4,'xh'=2,'core'=2,'shard'=2] {'y'}, use_global_device_ids=true, to_apply=%region_9.10 | all-reduce | flops 1 | bytes 8 | tf_op jit(solution)/shard_map/psum | solution.py:41
  183.9 21.8 %all-gather.3.cloned.1.call-done = bf16[384,16,128]{2,1,0:T(8,128)(2,1)} async-done(((bf16[48,16,128]{2,1,0:T(8,128)(2,1)}), bf16[384,16,128]{2,1,0:T(8,128)(2,1)}) %all-gather.3.cloned.1.call-update) | async-done | bytes 1572880 | tf_op jit(solution)/shard_map/all_gather | solution.py:42
  206.4 2.9 %collective-permute-done.1 = bf16[8,48,16,128]{3,2,1,0:T(8,128)(2,1)S(1)} collective-permute-done((bf16[8,48,16,128]{3,2,1,0:T(8,128)(2,1)}, bf16[8,48,16,128]{3,2,1,0:T(8,128)(2,1)S(1)}, u32[]{:S(2)}, u32[]{:S(2)}) %collective-permute-start.1) | collective-permute-done | bytes 1572896 | tf_op jit(solution)/shard_map/ppermute | solution.py:44
  209.3 1.6 select_bitcast_fusion.1
  210.9 0.6 convert_multiply_fusion
  211.5 0.2 slice_multiply_fusion
  211.8 1.3 copy.63
  213.1 0.3 copy-done.2
  213.4 1.0 copy-done
  214.4 0.9 copy-done.1
  215.3 5.6 %fusion.7 = (bf16[512,1536]{1,0:T(8,128)(2,1)S(1)}, f32[512,1536]{1,0:T(8,128)}, f32[512,1536]{1,0:T(8,128)}, f32[512,1536]{1,0:T(8,128)}) fusion(f32[512,1536]{1,0:T(8,128)S(1)} %copy-done, f32[64,8,12,128]{3,2,1,0:T(8,128)S(1)} %bitcast.61, f32[512,1536]{1,0:T(8,128)S(1)} %copy-done.1, f32[512,1536]{1,0:T(8,128)S(1)} %copy-done.2), kind=kLoop, calls=%fused_computation.43 | loop fusion | flops 12582912 | bytes 23592960 | tf_op jit(solution)/shard_map/convert_element_type | solution.py:150
  220.9 1.3 fusion.17
  222.2 0.6 collective-permute-start.6
  222.8 2.7 collective-permute-start.7
  225.4 0.2 fusion.16
  225.6 1.8 copy.59
  227.5 2.6 reshape.88
  230.1 4.3 %fusion.10 = (bf16[2,118,1536]{2,1,0:T(8,128)(2,1)S(1)}, f32[2,118,1536]{2,1,0:T(8,128)S(1)}, f32[2,118,1536]{2,1,0:T(8,128)S(1)}, f32[2,118,1536]{2,1,0:T(8,128)S(1)}) fusion(f32[2,118,1536]{2,0,1:T(2,128)} %param.16, f32[2,128,1536]{2,1,0:T(8,128)} %reshape.88, f32[]{:T(128)S(6)} %min.3, f32[2,118,1536]{2,0,1:T(2,128)} %param.19, f32[2,118,1536]{2,0,1:T(2,128)} %param.22), kind=kLoop, calls=%fused_computation.44 | loop fusion | flops 6162432 | bytes 10874884 | tf_op jit(solution)/shard_map/convert_element_type | solution.py:149
  234.4 0.1 collective-permute-start.4
  234.5 3.2 %collective-permute-start.5 = (bf16[1,118,1536]{2,1,0:T(8,128)(2,1)S(1)}, bf16[1,118,1536]{2,1,0:T(8,128)(2,1)S(1)}, u32[]{:S(2)}, u32[]{:S(2)}) collective-permute-start(bf16[1,118,1536]{2,1,0:T(8,128)(2,1)S(1)} %get-tuple-element.82), channel_id=1, source_target_pairs={{0,5},{1,0},{4,1},{5,4},{2,7},{3,2},{6,3},{7,6},{8,13},{9,8},{12,9... | collective-permute-start | bytes 1087496 | tf_op jit(solution)/shard_map/ppermute | solution.py:70
  237.7 3.0 %fusion.13 = (bf16[2,1536,128]{2,1,0:T(8,128)(2,1)S(1)}, f32[2,1536,128]{2,1,0:T(8,128)}, f32[2,1536,128]{2,1,0:T(8,128)}, f32[2,1536,128]{2,1,0:T(8,128)}) fusion(f32[2,1536,128]{2,1,0:T(8,128)S(1)} %copy-done.3, f32[2,1536,128]{2,1,0:T(8,128)S(1)} %copy-done.4, f32[2,1536,128]{2,1,0:T(8,128)S(1)} %copy-done.5, f32[2,1536,128]{2,1,0:T(8,128)S(1)} %bitcast.70), kind=kLoop, calls=%fused_computation.45 | loop fusion | flops 6291456 | bytes 11796480 | tf_op jit(solution)/shard_map/convert_element_type | solution.py:148
  240.7 0.1 fusion.18
  240.8 0.1 collective-permute-start.2
  240.9 2.2 copy.64
  243.1 2.2 copy.65
  245.3 2.2 copy.66
  247.5 4.4 %collective-permute-done.4 = bf16[1,118,1536]{2,1,0:T(8,128)(2,1)S(1)} collective-permute-done((bf16[1,118,1536]{2,1,0:T(8,128)(2,1)S(1)}, bf16[1,118,1536]{2,1,0:T(8,128)(2,1)S(1)}, u32[]{:S(2)}, u32[]{:S(2)}) %collective-permute-start.4) | collective-permute-done | bytes 362528 | tf_op jit(solution)/shard_map/ppermute | solution.py:69
  252.0 0.1 broadcast_select_fusion.5
  252.1 0.2 pad_maximum_fusion.3
  252.3 2.6 copy.67
  254.9 4.7 %collective-permute-done.2 = bf16[1,1536,128]{2,1,0:T(8,128)(2,1)S(1)} collective-permute-done((bf16[1,1536,128]{2,1,0:T(8,128)(2,1)S(1)}, bf16[1,1536,128]{2,1,0:T(8,128)(2,1)S(1)}, u32[]{:S(2)}, u32[]{:S(2)}) %collective-permute-start.2) | collective-permute-done | bytes 393248 | tf_op jit(solution)/shard_map/ppermute | solution.py:69
  259.6 1.9 collective-permute-done.3
  261.4 0.1 constant_dynamic-update-slice_fusion
  261.5 0.2 broadcast_select_fusion.3
  261.7 1.2 pad_maximum_fusion.2
  262.9 1.2 constant_dynamic-update-slice_fusion.5
  264.1 1.2 constant_dynamic-update-slice_fusion.4
  265.3 0.4 broadcast_select_fusion.1
  265.7 1.9 pad_maximum_fusion.1
  (22 shorter events, 0.2 us)
Async XLA Ops:
  7.2 100.1 %reduce-scatter.3.cloned.1.call-start = ((), (), s32[]{:S(2)}) async-start(), calls=%async_computation.2 | async-start | bytes 3932160 | tf_op jit(solution)/shard_map/reduce_scatter | solution.py:35
  55.2 5.9 %collective-permute-start = (bf16[4,4,48,16,128]{4,3,2,1,0:T(8,128)(2,1)S(1)}, bf16[4,4,48,16,128]{4,3,2,1,0:T(8,128)(2,1)}, u32[]{:S(2)}, u32[]{:S(2)}) collective-permute-start(bf16[4,4,48,16,128]{4,3,2,1,0:T(8,128)(2,1)S(1)} %dynamic-slice_bitcast_fusion), channel_id=1, source_target_pairs={{0,2},{2,0},{1,3},{3,1},{4,6},{6,4},{5,7},{7,5},{8,10},{10,8},{9,1... | collective-permute-start | bytes 9437192 | tf_op jit(solution)/shard_map/ppermute | solution.py:33
  66.4 69.3 %reduce-scatter.5.cloned.1.call-start = ((), (), s32[]{:S(2)}) async-start(), calls=%async_computation.3 | async-start | bytes 1966080 | tf_op jit(solution)/shard_map/reduce_scatter | solution.py:36
  109.7 96.0 %all-gather.3.cloned.1.call-start = ((), (), s32[]{:S(2)}) async-start(), calls=%async_computation.4 | async-start | bytes 1769472 | tf_op jit(solution)/shard_map/all_gather | solution.py:42
  205.7 3.6 %collective-permute-start.1 = (bf16[8,48,16,128]{3,2,1,0:T(8,128)(2,1)}, bf16[8,48,16,128]{3,2,1,0:T(8,128)(2,1)S(1)}, u32[]{:S(2)}, u32[]{:S(2)}) collective-permute-start(bf16[8,48,16,128]{3,2,1,0:T(8,128)(2,1)} %bitcast.71), channel_id=1, source_target_pairs={{0,2},{2,0},{1,3},{3,1},{4,6},{6,4},{5,7},{7,5},{8,10},{10,8},{9,1... | collective-permute-start | bytes 4718600 | tf_op jit(solution)/shard_map/ppermute | solution.py:44
  211.5 1.9 copy-start.2
  211.8 2.7 copy-start
  211.8 3.6 %copy-start.1 = (f32[512,1536]{1,0:T(8,128)S(1)}, f32[512,1536]{1,0:T(8,128)}, u32[]{:S(2)}) copy-start(f32[512,1536]{1,0:T(8,128)} %param.20) | copy-start | bytes 9437188
  222.2 40.7 %collective-permute-start.6 = (bf16[256,1536]{1,0:T(8,128)(2,1)}, bf16[256,1536]{1,0:T(8,128)(2,1)}, u32[]{:S(2)}, u32[]{:S(2)}) collective-permute-start(bf16[256,1536]{1,0:T(8,128)(2,1)} %get-tuple-element.75), channel_id=1, source_target_pairs={{0,1},{1,4},{4,5},{5,0},{2,3},{3,6},{6,7},{7,2},{8,9},{9,12},{12,1... | collective-permute-start | bytes 2359304 | tf_op jit(solution)/shard_map/ppermute | solution.py:69
  222.8 41.4 %collective-permute-start.7 = (bf16[256,1536]{1,0:T(8,128)(2,1)}, bf16[256,1536]{1,0:T(8,128)(2,1)}, u32[]{:S(2)}, u32[]{:S(2)}) collective-permute-start(bf16[256,1536]{1,0:T(8,128)(2,1)} %get-tuple-element.74), channel_id=1, source_target_pairs={{0,5},{1,0},{4,1},{5,4},{2,7},{3,2},{6,3},{7,6},{8,13},{9,8},{12,9... | collective-permute-start | bytes 2359304 | tf_op jit(solution)/shard_map/ppermute | solution.py:70
  230.1 7.7 %copy-start.3 = (f32[2,1536,128]{2,1,0:T(8,128)S(1)}, f32[2,1536,128]{2,1,0:T(8,128)}, u32[]{:S(2)}) copy-start(f32[2,1536,128]{2,1,0:T(8,128)} %param.15) | copy-start | bytes 4718596
  230.1 7.7 %copy-start.4 = (f32[2,1536,128]{2,1,0:T(8,128)S(1)}, f32[2,1536,128]{2,1,0:T(8,128)}, u32[]{:S(2)}) copy-start(f32[2,1536,128]{2,1,0:T(8,128)} %param.18) | copy-start | bytes 4718596
  230.1 7.7 %copy-start.5 = (f32[2,1536,128]{2,1,0:T(8,128)S(1)}, f32[2,1536,128]{2,1,0:T(8,128)}, u32[]{:S(2)}) copy-start(f32[2,1536,128]{2,1,0:T(8,128)} %param.21) | copy-start | bytes 4718596
  234.4 17.5 %collective-permute-start.4 = (bf16[1,118,1536]{2,1,0:T(8,128)(2,1)S(1)}, bf16[1,118,1536]{2,1,0:T(8,128)(2,1)S(1)}, u32[]{:S(2)}, u32[]{:S(2)}) collective-permute-start(bf16[1,118,1536]{2,1,0:T(8,128)(2,1)S(1)} %get-tuple-element.83), channel_id=1, source_target_pairs={{0,1},{1,4},{4,5},{5,0},{2,3},{3,6},{6,7},{7,2},{8,9},{9,12},{12,1... | collective-permute-start | bytes 1087496 | tf_op jit(solution)/shard_map/ppermute | solution.py:69
  234.5 17.4 %collective-permute-start.5 = (bf16[1,118,1536]{2,1,0:T(8,128)(2,1)S(1)}, bf16[1,118,1536]{2,1,0:T(8,128)(2,1)S(1)}, u32[]{:S(2)}, u32[]{:S(2)}) collective-permute-start(bf16[1,118,1536]{2,1,0:T(8,128)(2,1)S(1)} %get-tuple-element.82), channel_id=1, source_target_pairs={{0,5},{1,0},{4,1},{5,4},{2,7},{3,2},{6,3},{7,6},{8,13},{9,8},{12,9... | collective-permute-start | bytes 1087496 | tf_op jit(solution)/shard_map/ppermute | solution.py:70
  240.8 18.7 %collective-permute-start.2 = (bf16[1,1536,128]{2,1,0:T(8,128)(2,1)S(1)}, bf16[1,1536,128]{2,1,0:T(8,128)(2,1)S(1)}, u32[]{:S(2)}, u32[]{:S(2)}) collective-permute-start(bf16[1,1536,128]{2,1,0:T(8,128)(2,1)S(1)} %get-tuple-element.81), channel_id=1, source_target_pairs={{0,1},{1,4},{4,5},{5,0},{2,3},{3,6},{6,7},{7,2},{8,9},{9,12},{12,1... | collective-permute-start | bytes 1179656 | tf_op jit(solution)/shard_map/ppermute | solution.py:69
  251.9 9.5 %collective-permute-start.3 = (bf16[1,1536,128]{2,1,0:T(8,128)(2,1)S(1)}, bf16[1,1536,128]{2,1,0:T(8,128)(2,1)S(1)}, u32[]{:S(2)}, u32[]{:S(2)}) collective-permute-start(bf16[1,1536,128]{2,1,0:T(8,128)(2,1)S(1)} %get-tuple-element.80), channel_id=1, source_target_pairs={{0,5},{1,0},{4,1},{5,4},{2,7},{3,2},{6,3},{7,6},{8,13},{9,8},{12,9... | collective-permute-start | bytes 1179656 | tf_op jit(solution)/shard_map/ppermute | solution.py:70
Sparse Core Ops, SparseCore 0:
  66.5 40.6 reduce-scatter.2
  110.2 25.4 reduce-scatter.4
  158.2 47.4 all-gather.2

commit v12 on v10

--- a/solution.py
+++ b/solution.py
@@ -33,8 +33,8 @@
     got = lax.ppermute(theirs, "core", perm=flip)
     part = (mine.astype(jnp.float32) + got.astype(jnp.float32)).astype(jnp.bfloat16)
     part = lax.psum_scatter(part, XRING, scatter_dimension=0, tiled=False)
-    part = lax.psum_scatter(part.astype(jnp.float32), "y", scatter_dimension=0, tiled=False)
-    part = lax.psum(part, "z").astype(jnp.bfloat16)
+    part = lax.psum_scatter(part, "y", scatter_dimension=0, tiled=False)
+    part = lax.psum(part.astype(jnp.float32), "z").astype(jnp.bfloat16)
     wide = part.astype(jnp.float32)
     squares = jnp.sum(wide * wide)
     for axis in ("core", XRING, "y"):

time: 272 us -> 269 us (0.989)
  no operation moved by 1% of the time
where the time goes in v12:
time: 269 us; the launch traced here: 268 us
  waiting for transfers between devices  90.9 us (34%)
  blocking collectives  59.1 us (22%)
  local copies, waits for them, and re-layouts  48.9 us (18%)
  other arithmetic  46.7 us (17%)
  between operations  15.8 us (6%)
  starting transfers between devices  6.82 us (3%)
    reduce_scatter x1, waiting for transfers between devices, reduce_flat(): part = lax.psum_scatter(part, XRING, scatter_dimension=0, tiled=False)  40.8 us
    reduce_scatter x1, waiting for transfers between devices, reduce_flat(): part = lax.psum_scatter(part, 'y', scatter_dimension=0, tiled=False)  24.6 us
    psum x3, blocking collectives, reduce_flat(): squares = lax.psum(squares, axis)  22.9 us
    psum x1, blocking collectives, reduce_flat(): part = lax.psum(part.astype(jnp.float32), 'z').astype(jnp.bfloat16)  21 us
    all_gather x1, blocking collectives, reduce_flat(): part = lax.all_gather(part, 'y', axis=0)  15.1 us
    unnamed x19, local copies, waits for them, and re-layouts  12.8 us
    ppermute x3, waiting for transfers between devices, swap_halves(): lax.ppermute(first, XRING, perm=[(p, (p + 1) % n) for p in range(n)])  9.01 us
    reshape x2, local copies, waits for them, and re-layouts, to_tiles(): a = a.reshape(*lead, r // TR, TR, c // 128, 128)  8.5 us
  transfers between devices with their start and end apart: 11, of which 8 were waited for; matrix products, arithmetic and copies ran while one was open for 9% of the time, Pallas kernels for 0%

profile of v12, /device:TPU:0, one launch (start us, length us, event | category | flops | bytes accessed | tf_op | source)
XLA Modules:
  0.0 268.1 jit_solution(13045764781399073192)
XLA Ops:
  7.2 6.1 %reduce.2 = bf16[1024,1536]{1,0:T(8,128)(2,1)S(1)} reduce(bf16[2,1024,1536]{2,1,0:T(8,128)(2,1)} %param.14, bf16[]{:T(256)} %constant.22.clone.1), dimensions={0}, to_apply=%region_2.3.clone | reduce | flops 1572864 | bytes 9437186 | tf_op jit(solution)/shard_map/reduce_sum | solution.py:119
  13.3 3.6 %reshape.85 = bf16[64,16,12,128]{3,2,1,0:T(8,128)(2,1)} reshape(bf16[1024,1536]{1,0:T(8,128)(2,1)S(1)} %reduce.2) | data formatting | bytes 6291456 | tf_op jit(solution)/shard_map/reshape | solution.py:56
  16.9 3.0 %copy.56 = bf16[64,12,16,128]{3,2,1,0:T(8,128)(2,1)S(1)} copy(bf16[64,12,16,128]{3,1,2,0:T(8,128)(2,1)} %bitcast.61) | data formatting | bytes 6291456 | tf_op jit(solution)/shard_map/transpose | solution.py:58
  19.9 7.6 %reduce = bf16[2,118,3072]{2,0,1:T(2,128)(2,1)} reduce(bf16[2,2,118,3072]{3,1,2,0:T(2,128)(2,1)} %param.13, bf16[]{:T(256)} %constant.22.clone.1), dimensions={0}, to_apply=%region_0.0.clone | reduce | flops 724992 | bytes 4349954 | tf_op jit(solution)/shard_map/reduce_sum | solution.py:113
  27.5 3.7 %pad.5 = bf16[2,128,3072]{2,0,1:T(2,128)(2,1)} pad(bf16[2,118,3072]{2,0,1:T(2,128)(2,1)} %reduce, bf16[]{:T(256)} %constant.22.clone.1), padding=0_0x0_10x0_0 | pad | bytes 3022850 | tf_op jit(solution)/shard_map/jit(_pad)/pad | solution.py:114
  31.2 4.8 %reshape.94 = bf16[2,8,16,24,128]{4,3,0,2,1:T(8,128)(2,1)} reshape(bf16[2,128,3072]{2,0,1:T(2,128)(2,1)} %pad.5) | data formatting | bytes 3145728 | tf_op jit(solution)/shard_map/reshape | solution.py:56
  36.1 1.8 copy.53
  37.9 1.4 copy.54
  39.3 4.0 %reduce.1 = bf16[2,3072,128]{2,1,0:T(8,128)(2,1)} reduce(bf16[2,2,3072,128]{3,2,1,0:T(8,128)(2,1)} %param.12, bf16[]{:T(256)} %constant.22.clone.1), dimensions={0}, to_apply=%region_1.0.clone | reduce | flops 786432 | bytes 4718594 | tf_op jit(solution)/shard_map/reduce_sum | solution.py:108
  43.3 2.8 %copy.55 = bf16[2,2,96,16,128]{4,3,2,1,0:T(8,128)(2,1)} copy(bf16[2,2,96,16,128]{4,3,2,0,1:T(8,128)(2,1)} %bitcast.70) | data formatting | bytes 3145728 | tf_op jit(solution)/shard_map/transpose | solution.py:110
  46.1 2.5 pad_maximum_fusion
  48.6 4.1 %copy.57 = bf16[2,2,2,4,48,16,128]{6,5,4,3,2,1,0:T(8,128)(2,1)} copy(bf16[2,2,2,4,48,16,128]{6,5,4,3,1,0,2:T(8,128)(2,1)S(1)} %bitcast.60) | data formatting | bytes 12582912 | tf_op jit(solution)/shard_map/convert_element_type | solution.py:30
  52.7 2.4 dynamic-slice_bitcast_fusion
  55.2 0.1 collective-permute-start
  55.3 5.8 %collective-permute-done = bf16[4,4,48,16,128]{4,3,2,1,0:T(8,128)(2,1)} collective-permute-done((bf16[4,4,48,16,128]{4,3,2,1,0:T(8,128)(2,1)S(1)}, bf16[4,4,48,16,128]{4,3,2,1,0:T(8,128)(2,1)}, u32[]{:S(2)}, u32[]{:S(2)}) %collective-permute-start) | collective-permute-done | bytes 3145760 | tf_op jit(solution)/shard_map/ppermute | solution.py:33
  61.0 5.3 %fusion = bf16[4,4,48,16,128]{4,3,2,1,0:T(8,128)(2,1)} fusion(bf16[4,4,48,16,128]{4,3,2,1,0:T(8,128)(2,1)} %collective-permute-done, bf16[2,4,4,48,16,128]{5,4,3,2,1,0:T(8,128)(2,1)} %bitcast.59, s32[]{:T(128)S(6)} %select_n.55), kind=kLoop, calls=%fused_computation.2 | loop fusion | flops 6291456 | bytes 9437188 | tf_op jit(solution)/shard_map/convert_element_type | solution.py:34
  66.4 0.0 reduce-scatter.5.cloned.1.call-start
  66.5 40.8 %reduce-scatter.3.cloned.1.call-done = bf16[1,4,48,16,128]{4,3,2,1,0:T(8,128)(2,1)} async-done(((bf16[4,4,48,16,128]{4,3,2,1,0:T(8,128)(2,1)}), bf16[1,4,48,16,128]{4,3,2,1,0:T(8,128)(2,1)}) %reduce-scatter.3.cloned.1.call-update) | async-done | bytes 786448 | tf_op jit(solution)/shard_map/reduce_scatter | solution.py:35
  107.3 24.6 %reduce-scatter.5.cloned.1.call-done = bf16[1,48,16,128]{3,2,1,0:T(8,128)(2,1)} async-done(((bf16[4,48,16,128]{3,2,1,0:T(8,128)(2,1)}), bf16[1,48,16,128]{3,2,1,0:T(8,128)(2,1)}) %reduce-scatter.5.cloned.1.call-update) | async-done | bytes 196624 | tf_op jit(solution)/shard_map/reduce_scatter | solution.py:36
  131.9 1.0 bitcast_convert_fusion
  132.9 21.0 %all-reduce.2 = bf16[48,16,128]{2,1,0:T(8,128)(2,1)S(1)} all-reduce(f32[48,16,128]{2,1,0:T(8,128)S(1)} %bitcast_convert_fusion), channel_id=1, replica_groups=mesh['z'=4,'y'=4,'xh'=2,'core'=2,'shard'=2] {'z'}, use_global_device_ids=true, to_apply=%region_5.6 | all-reduce | flops 98304 | bytes 589824 | tf_op jit(solution)/shard_map/psum | solution.py:37
  153.9 15.1 %all-gather = bf16[192,16,128]{2,1,0:T(8,128)(2,1)} all-gather(bf16[48,16,128]{2,1,0:T(8,128)(2,1)S(1)} %all-reduce.2), channel_id=2, replica_groups=mesh['z'=4,'y'=4,'xh'=2,'core'=2,'shard'=2] {'y'}, dimensions={0}, use_global_device_ids=true | all-gather | bytes 983040 | tf_op jit(solution)/shard_map/all_gather | solution.py:42
  169.1 0.7 multiply_reduce_fusion
  169.8 3.1 %psum.29 = f32[]{:T(128)} all-reduce(f32[]{:T(128)} %multiply_reduce_fusion), channel_id=1, replica_groups=mesh['z'=4,'y'=4,'xh'=2,'core'=2,'shard'=2] {'core'}, use_global_device_ids=true, to_apply=%region_7.8 | all-reduce | flops 1 | bytes 8 | tf_op jit(solution)/shard_map/psum | solution.py:41
  172.8 11.4 %psum.30 = f32[]{:T(128)} all-reduce(f32[]{:T(128)} %psum.29), channel_id=1, replica_groups=mesh['z'=4,'y'=4,'xh'=2,'core'=2,'shard'=2] {'xh','shard'}, use_global_device_ids=true, to_apply=%region_8.9 | all-reduce | flops 1 | bytes 8 | tf_op jit(solution)/shard_map/psum | solution.py:41
  184.2 8.5 %psum.31 = f32[]{:T(128)} all-reduce(f32[]{:T(128)} %psum.30), channel_id=1, replica_groups=mesh['z'=4,'y'=4,'xh'=2,'core'=2,'shard'=2] {'y'}, use_global_device_ids=true, to_apply=%region_9.10 | all-reduce | flops 1 | bytes 8 | tf_op jit(solution)/shard_map/psum | solution.py:41
  192.7 5.9 %all-gather.4.cloned.1.call-done = bf16[8,48,16,128]{3,2,1,0:T(8,128)(2,1)} async-done(((bf16[4,48,16,128]{3,2,1,0:T(8,128)(2,1)}), bf16[8,48,16,128]{3,2,1,0:T(8,128)(2,1)}) %all-gather.4.cloned.1.call-update) | async-done | bytes 1572880 | tf_op jit(solution)/shard_map/all_gather | solution.py:43
  199.3 2.9 %collective-permute-done.1 = bf16[2,4,48,16,128]{4,3,2,1,0:T(8,128)(2,1)S(1)} collective-permute-done((bf16[2,4,48,16,128]{4,3,2,1,0:T(8,128)(2,1)}, bf16[2,4,48,16,128]{4,3,2,1,0:T(8,128)(2,1)S(1)}, u32[]{:S(2)}, u32[]{:S(2)}) %collective-permute-start.1) | collective-permute-done | bytes 1572896 | tf_op jit(solution)/shard_map/ppermute | solution.py:45
  202.2 1.6 select_bitcast_fusion.1
  203.8 0.6 convert_multiply_fusion
  204.4 0.2 slice_multiply_fusion
  204.7 1.3 copy.63
  206.0 0.3 copy-done.2
  206.3 1.0 copy-done
  207.3 0.9 copy-done.1
  208.2 5.6 %fusion.7 = (bf16[512,1536]{1,0:T(8,128)(2,1)S(1)}, f32[512,1536]{1,0:T(8,128)}, f32[512,1536]{1,0:T(8,128)}, f32[512,1536]{1,0:T(8,128)}) fusion(f32[512,1536]{1,0:T(8,128)S(1)} %copy-done, f32[64,8,12,128]{3,2,1,0:T(8,128)S(1)} %bitcast.62, f32[512,1536]{1,0:T(8,128)S(1)} %copy-done.1, f32[512,1536]{1,0:T(8,128)S(1)} %copy-done.2), kind=kLoop, calls=%fused_computation.43 | loop fusion | flops 12582912 | bytes 23592960 | tf_op jit(solution)/shard_map/convert_element_type | solution.py:151
  213.8 1.3 fusion.17
  215.1 0.5 collective-permute-start.6
  215.6 2.8 %collective-permute-start.7 = (bf16[256,1536]{1,0:T(8,128)(2,1)}, bf16[256,1536]{1,0:T(8,128)(2,1)}, u32[]{:S(2)}, u32[]{:S(2)}) collective-permute-start(bf16[256,1536]{1,0:T(8,128)(2,1)} %get-tuple-element.74), channel_id=1, source_target_pairs={{0,5},{1,0},{4,1},{5,4},{2,7},{3,2},{6,3},{7,6},{8,13},{9,8},{12,9... | collective-permute-start | bytes 2359304 | tf_op jit(solution)/shard_map/ppermute | solution.py:71
  218.3 0.2 fusion.16
  218.5 1.8 copy.59
  220.4 2.6 reshape.88
  223.0 4.3 %fusion.10 = (bf16[2,118,1536]{2,1,0:T(8,128)(2,1)S(1)}, f32[2,118,1536]{2,1,0:T(8,128)S(1)}, f32[2,118,1536]{2,1,0:T(8,128)S(1)}, f32[2,118,1536]{2,1,0:T(8,128)S(1)}) fusion(f32[2,118,1536]{2,0,1:T(2,128)} %param.16, f32[2,128,1536]{2,1,0:T(8,128)} %reshape.88, f32[]{:T(128)S(6)} %min.3, f32[2,118,1536]{2,0,1:T(2,128)} %param.19, f32[2,118,1536]{2,0,1:T(2,128)} %param.22), kind=kLoop, calls=%fused_computation.44 | loop fusion | flops 6162432 | bytes 10874884 | tf_op jit(solution)/shard_map/convert_element_type | solution.py:150
  227.3 0.1 collective-permute-start.4
  227.4 3.2 %collective-permute-start.5 = (bf16[1,118,1536]{2,1,0:T(8,128)(2,1)S(1)}, bf16[1,118,1536]{2,1,0:T(8,128)(2,1)S(1)}, u32[]{:S(2)}, u32[]{:S(2)}) collective-permute-start(bf16[1,118,1536]{2,1,0:T(8,128)(2,1)S(1)} %get-tuple-element.82), channel_id=1, source_target_pairs={{0,5},{1,0},{4,1},{5,4},{2,7},{3,2},{6,3},{7,6},{8,13},{9,8},{12,9... | collective-permute-start | bytes 1087496 | tf_op jit(solution)/shard_map/ppermute | solution.py:71
  230.6 3.0 %fusion.13 = (bf16[2,1536,128]{2,1,0:T(8,128)(2,1)S(1)}, f32[2,1536,128]{2,1,0:T(8,128)}, f32[2,1536,128]{2,1,0:T(8,128)}, f32[2,1536,128]{2,1,0:T(8,128)}) fusion(f32[2,1536,128]{2,1,0:T(8,128)S(1)} %copy-done.3, f32[2,1536,128]{2,1,0:T(8,128)S(1)} %copy-done.4, f32[2,1536,128]{2,1,0:T(8,128)S(1)} %copy-done.5, f32[2,1536,128]{2,1,0:T(8,128)S(1)} %bitcast.71), kind=kLoop, calls=%fused_computation.45 | loop fusion | flops 6291456 | bytes 11796480 | tf_op jit(solution)/shard_map/convert_element_type | solution.py:149
  233.6 0.1 fusion.18
  233.7 0.1 collective-permute-start.2
  233.8 2.2 copy.64
  236.0 2.2 copy.65
  238.2 2.2 copy.66
  240.4 4.4 %collective-permute-done.4 = bf16[1,118,1536]{2,1,0:T(8,128)(2,1)S(1)} collective-permute-done((bf16[1,118,1536]{2,1,0:T(8,128)(2,1)S(1)}, bf16[1,118,1536]{2,1,0:T(8,128)(2,1)S(1)}, u32[]{:S(2)}, u32[]{:S(2)}) %collective-permute-start.4) | collective-permute-done | bytes 362528 | tf_op jit(solution)/shard_map/ppermute | solution.py:70
  244.9 0.1 broadcast_select_fusion.5
  245.0 0.2 pad_maximum_fusion.3
  245.2 2.6 copy.67
  247.8 4.7 %collective-permute-done.2 = bf16[1,1536,128]{2,1,0:T(8,128)(2,1)S(1)} collective-permute-done((bf16[1,1536,128]{2,1,0:T(8,128)(2,1)S(1)}, bf16[1,1536,128]{2,1,0:T(8,128)(2,1)S(1)}, u32[]{:S(2)}, u32[]{:S(2)}) %collective-permute-start.2) | collective-permute-done | bytes 393248 | tf_op jit(solution)/shard_map/ppermute | solution.py:70
  252.4 1.9 collective-permute-done.3
  254.3 0.1 constant_dynamic-update-slice_fusion
  254.4 0.2 broadcast_select_fusion.3
  254.6 1.2 pad_maximum_fusion.2
  255.8 1.2 constant_dynamic-update-slice_fusion.5
  257.0 1.2 constant_dynamic-update-slice_fusion.4
  258.2 0.4 broadcast_select_fusion.1
  258.6 1.9 pad_maximum_fusion.1
  (23 shorter events, 0.3 us)
Async XLA Ops:
  7.2 100.1 %reduce-scatter.3.cloned.1.call-start = ((), (), s32[]{:S(2)}) async-start(), calls=%async_computation.2 | async-start | bytes 3932160 | tf_op jit(solution)/shard_map/reduce_scatter | solution.py:35
  55.2 5.9 %collective-permute-start = (bf16[4,4,48,16,128]{4,3,2,1,0:T(8,128)(2,1)S(1)}, bf16[4,4,48,16,128]{4,3,2,1,0:T(8,128)(2,1)}, u32[]{:S(2)}, u32[]{:S(2)}) collective-permute-start(bf16[4,4,48,16,128]{4,3,2,1,0:T(8,128)(2,1)S(1)} %dynamic-slice_bitcast_fusion), channel_id=1, source_target_pairs={{0,2},{2,0},{1,3},{3,1},{4,6},{6,4},{5,7},{7,5},{8,10},{10,8},{9,1... | collective-permute-start | bytes 9437192 | tf_op jit(solution)/shard_map/ppermute | solution.py:33
  66.4 65.5 %reduce-scatter.5.cloned.1.call-start = ((), (), s32[]{:S(2)}) async-start(), calls=%async_computation.3 | async-start | bytes 983040 | tf_op jit(solution)/shard_map/reduce_scatter | solution.py:36
  107.3 91.3 %all-gather.4.cloned.1.call-start = ((), (), s32[]{:S(2)}) async-start(), calls=%async_computation.4 | async-start | bytes 2359296 | tf_op jit(solution)/shard_map/all_gather | solution.py:43
  198.6 3.6 %collective-permute-start.1 = (bf16[2,4,48,16,128]{4,3,2,1,0:T(8,128)(2,1)}, bf16[2,4,48,16,128]{4,3,2,1,0:T(8,128)(2,1)S(1)}, u32[]{:S(2)}, u32[]{:S(2)}) collective-permute-start(bf16[2,4,48,16,128]{4,3,2,1,0:T(8,128)(2,1)} %bitcast.73), channel_id=1, source_target_pairs={{0,2},{2,0},{1,3},{3,1},{4,6},{6,4},{5,7},{7,5},{8,10},{10,8},{9,1... | collective-permute-start | bytes 4718600 | tf_op jit(solution)/shard_map/ppermute | solution.py:45
  204.4 1.9 copy-start.2
  204.7 2.7 copy-start
  204.7 3.6 %copy-start.1 = (f32[512,1536]{1,0:T(8,128)S(1)}, f32[512,1536]{1,0:T(8,128)}, u32[]{:S(2)}) copy-start(f32[512,1536]{1,0:T(8,128)} %param.20) | copy-start | bytes 9437188
  215.1 40.7 %collective-permute-start.6 = (bf16[256,1536]{1,0:T(8,128)(2,1)}, bf16[256,1536]{1,0:T(8,128)(2,1)}, u32[]{:S(2)}, u32[]{:S(2)}) collective-permute-start(bf16[256,1536]{1,0:T(8,128)(2,1)} %get-tuple-element.75), channel_id=1, source_target_pairs={{0,1},{1,4},{4,5},{5,0},{2,3},{3,6},{6,7},{7,2},{8,9},{9,12},{12,1... | collective-permute-start | bytes 2359304 | tf_op jit(solution)/shard_map/ppermute | solution.py:70
  215.6 41.5 %collective-permute-start.7 = (bf16[256,1536]{1,0:T(8,128)(2,1)}, bf16[256,1536]{1,0:T(8,128)(2,1)}, u32[]{:S(2)}, u32[]{:S(2)}) collective-permute-start(bf16[256,1536]{1,0:T(8,128)(2,1)} %get-tuple-element.74), channel_id=1, source_target_pairs={{0,5},{1,0},{4,1},{5,4},{2,7},{3,2},{6,3},{7,6},{8,13},{9,8},{12,9... | collective-permute-start | bytes 2359304 | tf_op jit(solution)/shard_map/ppermute | solution.py:71
  222.9 7.7 %copy-start.3 = (f32[2,1536,128]{2,1,0:T(8,128)S(1)}, f32[2,1536,128]{2,1,0:T(8,128)}, u32[]{:S(2)}) copy-start(f32[2,1536,128]{2,1,0:T(8,128)} %param.15) | copy-start | bytes 4718596
  223.0 7.7 %copy-start.4 = (f32[2,1536,128]{2,1,0:T(8,128)S(1)}, f32[2,1536,128]{2,1,0:T(8,128)}, u32[]{:S(2)}) copy-start(f32[2,1536,128]{2,1,0:T(8,128)} %param.18) | copy-start | bytes 4718596
  223.0 7.7 %copy-start.5 = (f32[2,1536,128]{2,1,0:T(8,128)S(1)}, f32[2,1536,128]{2,1,0:T(8,128)}, u32[]{:S(2)}) copy-start(f32[2,1536,128]{2,1,0:T(8,128)} %param.21) | copy-start | bytes 4718596
  227.3 17.5 %collective-permute-start.4 = (bf16[1,118,1536]{2,1,0:T(8,128)(2,1)S(1)}, bf16[1,118,1536]{2,1,0:T(8,128)(2,1)S(1)}, u32[]{:S(2)}, u32[]{:S(2)}) collective-permute-start(bf16[1,118,1536]{2,1,0:T(8,128)(2,1)S(1)} %get-tuple-element.83), channel_id=1, source_target_pairs={{0,1},{1,4},{4,5},{5,0},{2,3},{3,6},{6,7},{7,2},{8,9},{9,12},{12,1... | collective-permute-start | bytes 1087496 | tf_op jit(solution)/shard_map/ppermute | solution.py:70
  227.4 17.4 %collective-permute-start.5 = (bf16[1,118,1536]{2,1,0:T(8,128)(2,1)S(1)}, bf16[1,118,1536]{2,1,0:T(8,128)(2,1)S(1)}, u32[]{:S(2)}, u32[]{:S(2)}) collective-permute-start(bf16[1,118,1536]{2,1,0:T(8,128)(2,1)S(1)} %get-tuple-element.82), channel_id=1, source_target_pairs={{0,5},{1,0},{4,1},{5,4},{2,7},{3,2},{6,3},{7,6},{8,13},{9,8},{12,9... | collective-permute-start | bytes 1087496 | tf_op jit(solution)/shard_map/ppermute | solution.py:71
  233.7 18.7 %collective-permute-start.2 = (bf16[1,1536,128]{2,1,0:T(8,128)(2,1)S(1)}, bf16[1,1536,128]{2,1,0:T(8,128)(2,1)S(1)}, u32[]{:S(2)}, u32[]{:S(2)}) collective-permute-start(bf16[1,1536,128]{2,1,0:T(8,128)(2,1)S(1)} %get-tuple-element.81), channel_id=1, source_target_pairs={{0,1},{1,4},{4,5},{5,0},{2,3},{3,6},{6,7},{7,2},{8,9},{9,12},{12,1... | collective-permute-start | bytes 1179656 | tf_op jit(solution)/shard_map/ppermute | solution.py:70
  244.8 9.5 %collective-permute-start.3 = (bf16[1,1536,128]{2,1,0:T(8,128)(2,1)S(1)}, bf16[1,1536,128]{2,1,0:T(8,128)(2,1)S(1)}, u32[]{:S(2)}, u32[]{:S(2)}) collective-permute-start(bf16[1,1536,128]{2,1,0:T(8,128)(2,1)S(1)} %get-tuple-element.80), channel_id=1, source_target_pairs={{0,5},{1,0},{4,1},{5,4},{2,7},{3,2},{6,3},{7,6},{8,13},{9,8},{12,9... | collective-permute-start | bytes 1179656 | tf_op jit(solution)/shard_map/ppermute | solution.py:71
Sparse Core Ops, SparseCore 0:
  66.5 40.6 reduce-scatter.2
  109.7 22.2 reduce-scatter.4
  169.2 29.3 all-gather.3
